TPU v7x, 128 devices: a whole 4x4x4 slice. The times are simulated.
128 devices in a mesh: ty: 8 (over z, core), tx: 16 (over x, y).
Axes of the slice: x: 4, y: 4, z: 4, core: 2. Of those that a mesh axis runs over, the one named last changes fastest.
Arguments:
- specimen: float32 [2, 8192, 8192], P(None, 'ty', 'tx'), may hold values from -6 to 6
- probe_modes: float32 [2, 3, 512, 512], replicated, may hold values from -6 to 6
- amplitude: float32 [256, 512, 512], P(('ty', 'tx')), may hold values from 0.5 to 3
- offsets: int32 [256, 2], P(('ty', 'tx')), may hold values from 0 to 1023, as said below
- live_slots: int32 [256], P(('ty', 'tx')), may hold values from 0 to 1, as said below
Outputs:
- specimen_grad: float32 [2, 8192, 8192], P(None, 'ty', 'tx')
- probe_grad: float32 [2, 3, 512, 512], replicated
Inputs may be any that keep to these rules, and one draw needn't show every extreme that they name: `offsets`: offsets are a row below 1024 and a column below 512 within the tile of the slot's device, chosen so that the 512 x 512 patch lies inside the object. `live_slots`: on each device the live slots come first; the two devices with tx indices 2m and 2m+1 and the same ty index hold exactly 2 live slots together.
All inputs are finite; a program needn't handle non-finite values.
Results may differ from a plain program's by a relative error of at most 0.0038.
The roundings to bfloat16 on the way count: a program that leaves them out, or rounds other values in their place, can miss the bound.
Values sent between devices are 32-bit elements; how exact they have to be, the bound alone decides.
No kernel may reach another device: no remote copies, remote signals or barrier semaphores. Data moves between devices by JAX's collectives and lax.ppermute only.
A program may use at most 128 MiB of HBM per device.

v0:
```python
import math

import jax
import jax.numpy as jnp
from jax import lax
from jax.sharding import Mesh
from jax.sharding import PartitionSpec as P

TY = ("ty_0", "ty_1")
TX = ("tx_0", "tx_1")
TY_TX = ("ty_0", "ty_1", "tx_0", "tx_1")


def passed_along(value, axis, steps):
    count = lax.axis_size(axis)
    initial, last = (max(0, -steps), min(count, count - steps))
    return lax.ppermute(value, axis, [(source, source + steps) for source in range(initial, last)])


def partner(value, axis, apart):
    mask = 2**apart
    pairs = [(source, source ^ mask) for source in range(lax.axis_size(axis))]
    return lax.ppermute(value, axis, pairs)


def filled_up(lines, devices):
    spare = -len(lines) % devices
    return jnp.pad(lines, [(0, spare)] + [(0, 0)] * (lines.ndim - 1))


def sum_in_order(parts, axes, sequence):
    dims = [lax.axis_size(a) for a in axes]
    parts = parts.reshape(*dims, *parts.shape[1:])
    parts = parts.transpose(*sequence, *range(len(axes), parts.ndim))
    parts = parts.reshape(-1, *parts.shape[len(axes) :])
    for k in sequence:
        parts = lax.psum_scatter(parts, axes[k], scatter_dimension=0, tiled=True)
    return parts[0]


def gather_in_order(shard, axes, sequence):
    parts = shard
    for k in sequence:
        parts = lax.all_gather(parts, axes[k])
    done = sequence[::-1]
    back = [done.index(k) for k in range(len(axes))]
    parts = parts.transpose(*back, *range(len(axes), parts.ndim))
    return parts.reshape(-1, *shard.shape)


def sum_in_two_steps(shard, axes, sequence):
    devices, lines = (lax.axis_size(axes), shard.reshape(-1, *shard.shape[1:][-1:]))
    parts = filled_up(lines, devices).reshape(devices, -1, *lines.shape[1:])
    own = sum_in_order(parts, axes, sequence)
    whole = gather_in_order(own, axes, sequence[::-1]).reshape(-1, *lines.shape[1:])
    return whole[: len(lines)].reshape(shard.shape)


def tables(length):
    index = jnp.arange(length, dtype=jnp.int32)
    phase = index[:, None] * index[None, :] % length
    angle = phase.astype(jnp.float32) * (2.0 * math.pi / length)
    scale = 1.0 / math.sqrt(length)
    return (
        (jnp.cos(angle) * scale).astype(jnp.bfloat16),
        (jnp.sin(angle) * scale).astype(jnp.bfloat16),
    )


def transform(real_part, imag_part, cos_table, sin_table, orient):
    length = real_part.shape[-1]
    stacked = jnp.concatenate([real_part, imag_part], axis=2)
    cos_part = jnp.einsum("ij,mjk->mik", cos_table, stacked, preferred_element_type=jnp.float32)
    sin_part = jnp.einsum("ij,mjk->mik", sin_table, stacked, preferred_element_type=jnp.float32)
    middle_re = (cos_part[:, :, :length] + orient * sin_part[:, :, length:]).astype(jnp.bfloat16)
    middle_im = (cos_part[:, :, length:] - orient * sin_part[:, :, :length]).astype(jnp.bfloat16)
    stacked = jnp.concatenate([middle_re, middle_im], axis=1)
    cos_part = jnp.einsum("mij,jk->mik", stacked, cos_table, preferred_element_type=jnp.float32)
    sin_part = jnp.einsum("mij,jk->mik", stacked, sin_table, preferred_element_type=jnp.float32)
    result_re = cos_part[:, :length] + orient * sin_part[:, length:]
    result_im = cos_part[:, length:] - orient * sin_part[:, :length]
    return (result_re, result_im)


def slot_terms(window, probe_modes, measured, alive_mask, cos_table, sin_table):
    window_re, window_im = (window[0], window[1])
    probe_re, probe_im = (probe_modes[0], probe_modes[1])
    wave_re = (probe_re * window_re - probe_im * window_im).astype(jnp.bfloat16)
    wave_im = (probe_re * window_im + probe_im * window_re).astype(jnp.bfloat16)
    far_re, far_im = transform(wave_re, wave_im, cos_table, sin_table, 1.0)
    intensity = jnp.sum(far_re * far_re + far_im * far_im, axis=0)
    factor = measured * lax.rsqrt(jnp.maximum(intensity, 1.0)) - 1.0
    delta_re = (far_re * factor).astype(jnp.bfloat16)
    delta_im = (far_im * factor).astype(jnp.bfloat16)
    back_re, back_im = transform(delta_re, delta_im, cos_table, sin_table, -1.0)
    back_re = back_re * alive_mask
    back_im = back_im * alive_mask
    grad_re = jnp.sum(probe_re * back_re + probe_im * back_im, axis=0)
    grad_im = jnp.sum(probe_re * back_im - probe_im * back_re, axis=0)
    mode_re = window_re * back_re + window_im * back_im
    mode_im = window_re * back_im - window_im * back_re
    return (jnp.stack([grad_re, grad_im]), jnp.stack([mode_re, mode_im]))


def local(specimen, probe_modes, amplitude, offsets, live_slots):
    tile_h = specimen.shape[1]
    tile_w = specimen.shape[2]
    width = probe_modes.shape[2]
    slots = live_slots.shape[0]
    devices_all = lax.axis_size(TY) * lax.axis_size(TX)
    anchor = jnp.zeros((), jnp.int32)
    right_part = passed_along(specimen, TX, -1)
    upper_rows = jnp.concatenate([specimen, right_part], axis=2)
    lower_rows = passed_along(upper_rows[:, :width, :], TY, -1)
    extended = jnp.concatenate([upper_rows, lower_rows], axis=1)
    cos_table, sin_table = tables(width)

    def crop(row_at, col_at):
        return lax.dynamic_slice(extended, (anchor, row_at, col_at), (2, width, width))

    windows = jax.vmap(crop)(offsets[:, 0], offsets[:, 1])
    alive_own = live_slots.astype(jnp.float32)

    def process(slot_items):
        window, measured, alive_mask = slot_items
        return slot_terms(window, probe_modes, measured, alive_mask, cos_table, sin_table)

    half_slots = slots // 2
    live_count = jnp.sum(alive_own)
    got_windows, got_measured, got_count = partner(
        (windows[half_slots:], amplitude[half_slots:], live_count), TX, 0
    )
    position = jnp.arange(half_slots, dtype=jnp.int32)
    taken = jnp.minimum(live_count, float(half_slots)).astype(jnp.int32)
    got_alive = ((position + half_slots).astype(jnp.float32) < got_count).astype(jnp.float32)
    pool_windows = jnp.concatenate([windows[:half_slots], got_windows], axis=0)
    pool_measured = jnp.concatenate([amplitude[:half_slots], got_measured], axis=0)
    pool_alive = jnp.concatenate([alive_own[:half_slots], got_alive], axis=0)
    order_index = jnp.where(position < taken, position, half_slots + position - taken)
    work_windows = jnp.take(pool_windows, order_index, axis=0)
    work_measured = jnp.take(pool_measured, order_index, axis=0)
    work_alive = jnp.take(pool_alive, order_index, axis=0)
    grad_terms, probe_terms = lax.map(process, (work_windows, work_measured, work_alive))
    padded_terms = jnp.concatenate([grad_terms, jnp.zeros_like(grad_terms)], axis=0)
    returned = jnp.take(padded_terms, taken + position, axis=0)
    got_back = partner(returned, TX, 0)
    kept = jnp.where((position < taken)[:, None, None, None], grad_terms, 0.0)
    own_terms = jnp.concatenate([kept, got_back], axis=0)
    probe_total = sum_in_two_steps(jnp.sum(probe_terms, axis=0), TY_TX, (1, 0, 2, 3))
    probe_grad = probe_total * (1.0 / math.sqrt(slots * devices_all))

    def place(slot_index, grad_ext):
        row_at = offsets[slot_index, 0]
        col_at = offsets[slot_index, 1]
        current = lax.dynamic_slice(grad_ext, (anchor, row_at, col_at), (2, width, width))
        return lax.dynamic_update_slice(
            grad_ext, current + own_terms[slot_index], (anchor, row_at, col_at)
        )

    grad_ext = lax.fori_loop(0, slots, place, jnp.zeros(extended.shape, jnp.float32))
    from_above = passed_along(grad_ext[:, tile_h:, :], TY, 1)
    upper_grad = grad_ext[:, :tile_h, :].at[:, :width, :].add(from_above)
    from_left = passed_along(upper_grad[:, :, tile_w:], TX, 1)
    core_grad = upper_grad[:, :, :tile_w].at[:, :, :width].add(from_left)
    return (core_grad, probe_grad)


def solution(mesh):
    finer = Mesh(mesh.devices.reshape(4, 2, 4, 4), ("ty_0", "ty_1", "tx_0", "tx_1"))
    placed = (P(None, TY, TX), P(), P(TY_TX, None, None), P(TY_TX, None), P(TY_TX))
    return jax.shard_map(
        local, mesh=finer, in_specs=placed, out_specs=(P(None, TY, TX), P()), check_vma=False
    )
```

profile of v0, /device:TPU:48, one launch (start us, length us, event | category | flops | bytes accessed | tf_op | source)
XLA Modules:
  0.0 679.7 jit_solution(4102758416133087349)
XLA Ops:
  12.4 89.2 %collective-permute-done = f32[2,1024,512]{2,1,0:T(8,128)S(1)} collective-permute-done((f32[2,1024,512]{2,1,0:T(8,128)}, f32[2,1024,512]{2,1,0:T(8,128)S(1)}, u32[]{:S(2)}, u32[]{:S(2)}) %collective-permute-start) | collective-permute-done | bytes 4194336 | tf_op jit(solution)/shard_map/ppermute | solution.py:17
  108.9 46.1 %collective-permute-done.1 = f32[2,512,1024]{2,1,0:T(8,128)} collective-permute-done((f32[2,512,1024]{2,1,0:T(8,128)}, f32[2,512,1024]{2,1,0:T(8,128)}, u32[]{:S(2)}, u32[]{:S(2)}) %collective-permute-start.1) | collective-permute-done | bytes 4194336 | tf_op jit(solution)/shard_map/ppermute | solution.py:17
  155.0 9.5 %pad_maximum_fusion = f32[2,1536,1024]{2,1,0:T(8,128)} fusion(f32[2,512,1024]{2,1,0:T(8,128)} %collective-permute-done.1, f32[2,1024,1024]{2,1,0:T(8,128)} %copy-done), kind=kLoop, calls=%fused_computation.5 | loop fusion | flops 3145728 | bytes 25165824 | tf_op jit(solution)/shard_map/concatenate | solution.py:115
  164.5 11.0 %while.26 = (s32[]{:T(128)}, f32[2,1536,1024]{2,1,0:T(8,128)}, s32[2,3]{1,0:T(2,128)S(1)}, f32[2,2,512,512]{3,2,1,0:T(8,128)}, s32[]{:T(128)}) while((s32[]{:T(128)}, f32[2,1536,1024]{2,1,0:T(8,128)}, s32[2,3]{1,0:T(2,128)S(1)}, f32[2,2,512,512]{3,2,1,0:T(8,128)}, s32[]{:T(128)}) %tuple.90), condition=%wide.while_cond.3, body=%wide.while_body.3.sunk | while | flops 2 | bytes 4195445 | solution.py:119
  191.7 37.5 %collective-permute-done.4 = f32[]{:T(128)} collective-permute-done((f32[]{:T(128)}, f32[]{:T(128)}, u32[]{:S(2)}, u32[]{:S(2)}) %collective-permute-start.4) | collective-permute-done | bytes 36 | tf_op jit(solution)/shard_map/ppermute | solution.py:23
  240.6 8.7 %convolution_bitcast_fusion = f32[3,512,1024]{2,1,0:T(8,128)} fusion(bf16[3,512,512]{2,1,0:T(8,128)(2,1)S(1)} %get-tuple-element.215, bf16[3,512,512]{2,1,0:T(8,128)(2,1)S(1)} %get-tuple-element.214), kind=kOutput, calls=%fused_computation.57 | convolution fusion | flops 1621098496 | bytes 9437184 | tf_op jit(solution)/shard_map/while/body/eval_jaxpr/ij,mjk->mik/dot_general | solution.py:74
  253.4 5.5 fusion.23
  258.9 5.6 fusion.24
  267.7 5.8 multiply_convert_fusion.1
  273.5 7.0 %convolution_bitcast_fusion.2 = f32[3,512,1024]{2,1,0:T(8,128)S(1)} fusion(bf16[3,512,512]{1,2,0:T(8,128)(2,1)} %get-tuple-element.209, bf16[3,512,512]{1,2,0:T(8,128)(2,1)S(1)} %get-tuple-element.208), kind=kOutput, calls=%fused_computation.59 | convolution fusion | flops 1621098496 | bytes 9437184 | tf_op jit(solution)/shard_map/while/body/eval_jaxpr/ij,mjk->mik/dot_general | solution.py:74
  280.5 8.3 %convolution_bitcast_fusion.3 = f32[3,512,1024]{2,1,0:T(8,128)} fusion(bf16[3,512,512]{1,2,0:T(8,128)(2,1)S(1)} %copy-done.4, bf16[3,512,512]{1,2,0:T(8,128)(2,1)S(1)} %get-tuple-element.208), kind=kOutput, calls=%fused_computation.60 | convolution fusion | flops 1621098496 | bytes 9437184 | tf_op jit(solution)/shard_map/while/body/eval_jaxpr/ij,mjk->mik/dot_general | solution.py:73
  298.4 8.2 %fusion.22 = f32[3,1024,512]{2,1,0:T(8,128)} fusion(bf16[3,512,512]{2,1,0:T(8,128)(2,1)S(1)} %get-tuple-element.211, bf16[3,512,512]{2,1,0:T(8,128)(2,1)S(1)} %get-tuple-element.210), kind=kOutput, calls=%fused_computation.69 | convolution fusion | flops 1621098496 | bytes 9437184 | tf_op jit(solution)/shard_map/while/body/eval_jaxpr/mij,jk->mik/dot_general | solution.py:78
  318.2 22.1 %reduce-scatter.5.cloned.1.call-done = f32[64,24,512]{2,1,0:T(8,128)} async-done(((f32[128,24,512]{2,1,0:T(8,128)}), f32[64,24,512]{2,1,0:T(8,128)}) %reduce-scatter.5.cloned.1.call-update) | async-done | bytes 3145744 | tf_op jit(solution)/shard_map/reduce_scatter | solution.py:37
  340.4 40.7 %reduce-scatter.7.cloned.1.call-done = f32[16,24,512]{2,1,0:T(8,128)} async-done(((f32[64,24,512]{2,1,0:T(8,128)}), f32[16,24,512]{2,1,0:T(8,128)}) %reduce-scatter.7.cloned.1.call-update) | async-done | bytes 786448 | tf_op jit(solution)/shard_map/reduce_scatter | solution.py:37
  384.2 23.0 %reduce-scatter.9.cloned.1.call-done = f32[4,24,512]{2,1,0:T(8,128)} async-done(((f32[16,24,512]{2,1,0:T(8,128)}), f32[4,24,512]{2,1,0:T(8,128)}) %reduce-scatter.9.cloned.1.call-update) | async-done | bytes 196624 | tf_op jit(solution)/shard_map/reduce_scatter | solution.py:37
  407.2 21.3 %reduce-scatter.11.cloned.1.call-done = f32[1,24,512]{2,1,0:T(8,128)} async-done(((f32[4,24,512]{2,1,0:T(8,128)}), f32[1,24,512]{2,1,0:T(8,128)}) %reduce-scatter.11.cloned.1.call-update) | async-done | bytes 49168 | tf_op jit(solution)/shard_map/reduce_scatter | solution.py:37
  428.5 12.2 %all_gather.21 = f32[4,24,512]{2,1,0:T(8,128)S(1)} all-gather(f32[1,24,512]{2,1,0:T(8,128)} %reduce-scatter.11.cloned.1.call-done), channel_id=1, replica_groups=mesh['ty_0'=4,'ty_1'=2,'tx_0'=4,'tx_1'=4] {'tx_1'}, dimensions={0}, use_global_device_ids=true | all-gather | bytes 245760 | tf_op jit(solution)/shard_map/all_gather | solution.py:44
  440.7 15.1 %all-gather = f32[16,24,512]{2,1,0:T(8,128)} all-gather(f32[4,24,512]{2,1,0:T(8,128)S(1)} %all_gather.21), channel_id=2, replica_groups=mesh['ty_0'=4,'ty_1'=2,'tx_0'=4,'tx_1'=4] {'tx_0'}, dimensions={0}, use_global_device_ids=true | all-gather | bytes 983040 | tf_op jit(solution)/shard_map/all_gather | solution.py:44
  460.5 6.3 broadcast_in_dim.55
  466.8 42.8 %while.25 = (s32[]{:T(128)}, f32[2,1536,1024]{2,1,0:T(8,128)}, s32[2,2]{1,0:T(2,128)S(1)}, f32[2,2,512,512]{3,2,1,0:T(8,128)}, s32[]{:T(128)}, /*index=5*/s32[]{:T(128)}, s32[]{:T(128)}, s32[]{:T(128)}) while((s32[]{:T(128)}, f32[2,1536,1024]{2,1,0:T(8,128)}, s32[2,2]{1,0:T(2,128)S(1)}, f32[2,2,512,512]{3,2,1,0:T(8,128)}, s32[]{:T(128)}, ...), condition=%wide.region_5.7_spmd, body=%wide.region_4.6_spmd.sunk | while | flops 524296 | bytes 10485957 | solution.py:160
  474.2 13.6 %dynamic_update_slice.14 = f32[2,1536,1024]{2,1,0:T(8,128)} dynamic-update-slice(f32[2,1536,1024]{2,1,0:T(8,128)} %get-tuple-element.307, f32[2,512,512]{2,1,0:T(8,128)S(1)} %bitcast_add_fusion.2, s32[]{:T(128)} %constant.177.clone.1..sunk, s32[]{:T(128)S(6)} %select_n.152, s32[]{:T(128)S(6)} %select_n.153) | dynamic-update-slice | bytes 4194308 | tf_op jit(solution)/shard_map/while/body/eval_jaxpr/dynamic_update_slice | solution.py:156
  495.3 14.3 %dynamic_update_slice.14 = f32[2,1536,1024]{2,1,0:T(8,128)} dynamic-update-slice(f32[2,1536,1024]{2,1,0:T(8,128)} %get-tuple-element.307, f32[2,512,512]{2,1,0:T(8,128)S(1)} %bitcast_add_fusion.2, s32[]{:T(128)} %constant.177.clone.1..sunk, s32[]{:T(128)S(6)} %select_n.152, s32[]{:T(128)S(6)} %select_n.153) | dynamic-update-slice | bytes 4194308 | tf_op jit(solution)/shard_map/while/body/eval_jaxpr/dynamic_update_slice | solution.py:156
  520.7 43.7 %collective-permute-done.6 = f32[2,512,1024]{2,1,0:T(8,128)} collective-permute-done((f32[2,512,1024]{2,1,0:T(8,128)}, f32[2,512,1024]{2,1,0:T(8,128)}, u32[]{:S(2)}, u32[]{:S(2)}) %collective-permute-start.6) | collective-permute-done | bytes 4194336 | tf_op jit(solution)/shard_map/ppermute | solution.py:17
  571.4 91.2 %collective-permute-done.7 = f32[2,1024,512]{2,1,0:T(8,128)S(1)} collective-permute-done((f32[2,1024,512]{2,1,0:T(8,128)S(1)}, f32[2,1024,512]{2,1,0:T(8,128)S(1)}, u32[]{:S(2)}, u32[]{:S(2)}) %collective-permute-start.7) | collective-permute-done | bytes 4194336 | tf_op jit(solution)/shard_map/ppermute | solution.py:17
  (93 shorter events, 120.4 us)
Async XLA Ops:
  7.2 333.2 %reduce-scatter.5.cloned.1.call-start = ((), (), s32[]{:S(2)}) async-start(), calls=%async_computation.4 | async-start | bytes 9437184 | tf_op jit(solution)/shard_map/reduce_scatter | solution.py:37
  7.2 94.4 %collective-permute-start = (f32[2,1024,512]{2,1,0:T(8,128)}, f32[2,1024,512]{2,1,0:T(8,128)S(1)}, u32[]{:S(2)}, u32[]{:S(2)}) collective-permute-start(f32[2,1024,512]{2,1,0:T(8,128)} %param.15), channel_id=1, source_target_pairs={{1,0},{2,1},{3,2},{4,3},{5,4},{6,5},{7,6},{8,7},{9,8},{10,9},{11,1... | collective-permute-start | bytes 12582920 | tf_op jit(solution)/shard_map/ppermute | solution.py:17
  102.3 4.5 copy-start
  102.3 6.4 copy-start.5
  106.8 48.2 %collective-permute-start.1 = (f32[2,512,1024]{2,1,0:T(8,128)}, f32[2,512,1024]{2,1,0:T(8,128)}, u32[]{:S(2)}, u32[]{:S(2)}) collective-permute-start(f32[2,512,1024]{2,1,0:T(8,128)} %slice.235), channel_id=1, source_target_pairs={{16,0},{32,16},{48,32},{64,48},{80,64},{96,80},{112,96},{17,1},{33... | collective-permute-start | bytes 12582920 | tf_op jit(solution)/shard_map/ppermute | solution.py:17
  175.6 8.2 %copy-start.6 = (s32[2]{0:T(128)S(1)}, s32[2]{0:T(128)}, u32[]{:S(2)}) copy-start(s32[2]{0:T(128)} %param.19) | copy-start | bytes 28
  175.6 8.9 %copy-start.3 = (f32[2,512,512]{2,1,0:T(8,128)S(1)}, f32[2,512,512]{2,1,0:T(8,128)}, u32[]{:S(2)}) copy-start(f32[2,512,512]{2,1,0:T(8,128)} %param.17) | copy-start | bytes 6291460
  180.4 50.7 %collective-permute-start.2 = (f32[1,2,512,512]{3,2,1,0:T(8,128)}, f32[1,2,512,512]{3,2,1,0:T(8,128)}, u32[]{:S(2)}, u32[]{:S(2)}) collective-permute-start(f32[1,2,512,512]{3,2,1,0:T(8,128)} %get-tuple-element.217), channel_id=1, source_target_pairs={{0,1},{1,0},{2,3},{3,2},{4,5},{5,4},{6,7},{7,6},{8,9},{9,8},{10,11... | collective-permute-start | bytes 6291464 | tf_op jit(solution)/shard_map/ppermute | solution.py:23
  184.5 44.7 %collective-permute-start.4 = (f32[]{:T(128)}, f32[]{:T(128)}, u32[]{:S(2)}, u32[]{:S(2)}) collective-permute-start(f32[]{:T(128)} %convert_reduce_fusion), channel_id=1, source_target_pairs={{0,1},{1,0},{2,3},{3,2},{4,5},{5,4},{6,7},{7,6},{8,9},{9,8},{10,11... | collective-permute-start | bytes 20 | tf_op jit(solution)/shard_map/ppermute | solution.py:23
  187.0 80.3 %collective-permute-start.3 = (f32[1,512,512]{1,2,0:T(8,128)}, f32[1,512,512]{1,2,0:T(8,128)}, u32[]{:S(2)}, u32[]{:S(2)}) collective-permute-start(f32[1,512,512]{1,2,0:T(8,128)} %copy.40), channel_id=1, source_target_pairs={{0,1},{1,0},{2,3},{3,2},{4,5},{5,4},{6,7},{7,6},{8,9},{9,8},{10,11... | collective-permute-start | bytes 3145736 | tf_op jit(solution)/shard_map/ppermute | solution.py:23
  190.0 43.6 %slice-start = ((s8[6291456]{0:T(1024)(128)(4,1)}), s8[2097152]{0:T(1024)(128)(4,1)S(1)}, s32[]{:S(2)}) async-start(s8[6291456]{0:T(1024)(128)(4,1)} %bitcast.117), calls=%async_computation.10 | async-start | bytes 4194304
  231.1 2.8 slice-start.1
  264.6 2.7 copy-start.1
  273.5 7.0 %copy-start.4 = (bf16[3,512,512]{1,2,0:T(8,128)(2,1)S(1)}, bf16[3,512,512]{1,2,0:T(8,128)(2,1)}, u32[]{:S(2)}) copy-start(bf16[3,512,512]{1,2,0:T(8,128)(2,1)} %get-tuple-element.209) | copy-start | bytes 4718596
  318.1 63.1 %copy-start.2 = (f32[512,512]{1,0:T(8,128)S(1)}, f32[512,512]{1,0:T(8,128)}, u32[]{:S(2)}) copy-start(f32[512,512]{1,0:T(8,128)} %get-tuple-element.184) | copy-start | bytes 3145732
  318.1 63.0 %reduce-scatter.7.cloned.1.call-start = ((), (), s32[]{:S(2)}) async-start(), calls=%async_computation.5 | async-start | bytes 3932160 | tf_op jit(solution)/shard_map/reduce_scatter | solution.py:37
  340.3 66.8 %reduce-scatter.9.cloned.1.call-start = ((), (), s32[]{:S(2)}) async-start(), calls=%async_computation.6 | async-start | bytes 983040 | tf_op jit(solution)/shard_map/reduce_scatter | solution.py:37
  381.2 47.4 %reduce-scatter.11.cloned.1.call-start = ((), (), s32[]{:S(2)}) async-start(), calls=%async_computation.7 | async-start | bytes 245760 | tf_op jit(solution)/shard_map/reduce_scatter | solution.py:37
  383.0 73.2 %collective-permute-start.5 = (f32[1,2,512,512]{3,2,1,0:T(8,128)}, f32[1,2,512,512]{3,2,1,0:T(8,128)}, u32[]{:S(2)}, u32[]{:S(2)}) collective-permute-start(f32[1,2,512,512]{3,2,1,0:T(8,128)} %fusion.18), channel_id=1, source_target_pairs={{0,1},{1,0},{2,3},{3,2},{4,5},{5,4},{6,7},{7,6},{8,9},{9,8},{10,11... | collective-permute-start | bytes 6291464 | tf_op jit(solution)/shard_map/ppermute | solution.py:23
  407.2 109.3 %all-gather.6.cloned.1.call-start = ((), (), s32[]{:S(2)}) async-start(), calls=%async_computation.8 | async-start | bytes 3932160 | tf_op jit(solution)/shard_map/all_gather | solution.py:44
  455.9 209.8 %all-gather.8.cloned.1.call-start = ((), (), s32[]{:S(2)}) async-start(), calls=%async_computation.9 | async-start | bytes 9437184 | tf_op jit(solution)/shard_map/all_gather | solution.py:44
  514.4 50.1 %collective-permute-start.6 = (f32[2,512,1024]{2,1,0:T(8,128)}, f32[2,512,1024]{2,1,0:T(8,128)}, u32[]{:S(2)}, u32[]{:S(2)}) collective-permute-start(f32[2,512,1024]{2,1,0:T(8,128)} %slice.192), channel_id=1, source_target_pairs={{0,16},{16,32},{32,48},{48,64},{64,80},{80,96},{96,112},{1,17},{17... | collective-permute-start | bytes 12582920 | tf_op jit(solution)/shard_map/ppermute | solution.py:17
  569.4 93.3 %collective-permute-start.7 = (f32[2,1024,512]{2,1,0:T(8,128)S(1)}, f32[2,1024,512]{2,1,0:T(8,128)S(1)}, u32[]{:S(2)}, u32[]{:S(2)}) collective-permute-start(f32[2,1024,512]{2,1,0:T(8,128)S(1)} %slice.255), channel_id=1, source_target_pairs={{0,1},{1,2},{2,3},{3,4},{4,5},{5,6},{6,7},{7,8},{8,9},{9,10},{10,1... | collective-permute-start | bytes 12582920 | tf_op jit(solution)/shard_map/ppermute | solution.py:17
Sparse Core Ops, SparseCore 0:
  318.2 22.0 reduce-scatter.4
  342.7 38.3 reduce-scatter.6
  383.5 23.5 reduce-scatter.8
  409.3 19.1 reduce-scatter.10
  456.0 39.0 all-gather.5
  516.6 20.6 all-gather.7
where the time goes:
time: 689 us; the launch traced here: 680 us
  waiting for transfers between devices  415 us (60%)
  local copies, waits for them, and re-layouts  81.9 us (12%)
  other arithmetic  62 us (9%)
  matrix products  53.8 us (8%)
  blocking collectives  27.3 us (4%)
  between operations  16.5 us (2%)
  starting transfers between devices  15.5 us (2%)
  loops' own time  7.55 us (1%)
    ppermute x4, waiting for transfers between devices, passed_along(): lax.ppermute(value, axis, [(source, source + steps) for source in range(i...  270 us
    reduce_scatter x4, waiting for transfers between devices, sum_in_order(): parts = lax.psum_scatter(parts, axes[k], scatter_dimension=0, tiled=True)  107 us
    ppermute x4, waiting for transfers between devices, partner(): return lax.ppermute(value, axis, pairs)  37.5 us
    dynamic_update_slice x2, local copies, waits for them, and re-layouts, place(): lax.dynamic_update_slice(grad_ext, current + own_terms[slot_index], (anch...  27.9 us
    all_gather x2, blocking collectives, gather_in_order(): parts = lax.all_gather(parts, axes[k])  27.3 us
    dot_general x2, matrix products, transform(): jnp.einsum('ij,mjk->mik', sin_table, stacked, preferred_element_type=jnp....  15.7 us
    dot_general x2, matrix products, transform(): jnp.einsum('mij,jk->mik', stacked, cos_table, preferred_element_type=jnp....  13.8 us
  transfers between devices with their start and end apart: 14, of which 9 were waited for; matrix products, arithmetic and copies ran while one was open for 16% of the time, Pallas kernels for 0%

commit v1 on v0

--- a/solution.py
+++ b/solution.py
@@ -54,6 +54,40 @@
     own = sum_in_order(parts, axes, sequence)
     whole = gather_in_order(own, axes, sequence[::-1]).reshape(-1, *lines.shape[1:])
     return whole[: len(lines)].reshape(shard.shape)
+
+
+def scatter_axis(lines, axis):
+    count = lax.axis_size(axis)
+    me = lax.axis_index(axis)
+    chunks = lines.reshape(count, -1, lines.shape[-1])
+    total = lax.dynamic_index_in_dim(chunks, me, keepdims=False)
+    for step in range(1, count):
+        sent = lax.dynamic_index_in_dim(chunks, (me + step) % count, keepdims=False)
+        pairs = [(source, (source + step) % count) for source in range(count)]
+        total = total + lax.ppermute(sent, axis, pairs)
+    return total
+
+
+def gather_axis(piece, axis):
+    count = lax.axis_size(axis)
+    me = lax.axis_index(axis)
+    whole = jnp.zeros((count,) + piece.shape, piece.dtype)
+    whole = lax.dynamic_update_index_in_dim(whole, piece, me, 0)
+    for step in range(1, count):
+        pairs = [(source, (source + step) % count) for source in range(count)]
+        got = lax.ppermute(piece, axis, pairs)
+        whole = lax.dynamic_update_index_in_dim(whole, got, (me - step) % count, 0)
+    return whole.reshape(-1, piece.shape[-1])
+
+
+def all_sum(value, axes, scale):
+    lines = value.reshape(-1, value.shape[-1])
+    for axis in axes:
+        lines = scatter_axis(lines, axis)
+    lines = lines * scale
+    for axis in axes[::-1]:
+        lines = gather_axis(lines, axis)
+    return lines.reshape(value.shape)
 
 
 def tables(length):
@@ -109,16 +143,22 @@
     slots = live_slots.shape[0]
     devices_all = lax.axis_size(TY) * lax.axis_size(TX)
     anchor = jnp.zeros((), jnp.int32)
-    right_part = passed_along(specimen, TX, -1)
-    upper_rows = jnp.concatenate([specimen, right_part], axis=2)
-    lower_rows = passed_along(upper_rows[:, :width, :], TY, -1)
+    right_top = passed_along(specimen[:, :width, :], TX, -1)
+    later_rows, right_top = lax.optimization_barrier((specimen[:, width:, :], right_top))
+    right_bottom = passed_along(later_rows, TX, -1)
+    below_own = passed_along(specimen[:, :width, :], TY, -1)
+    below_right = passed_along(right_top, TY, -1)
+    upper_rows = jnp.concatenate(
+        [specimen, jnp.concatenate([right_top, right_bottom], axis=1)], axis=2
+    )
+    lower_rows = jnp.concatenate([below_own, below_right], axis=2)
     extended = jnp.concatenate([upper_rows, lower_rows], axis=1)
     cos_table, sin_table = tables(width)
 
     def crop(row_at, col_at):
         return lax.dynamic_slice(extended, (anchor, row_at, col_at), (2, width, width))
 
-    windows = jax.vmap(crop)(offsets[:, 0], offsets[:, 1])
+    windows = jnp.stack([crop(offsets[k, 0], offsets[k, 1]) for k in range(slots)])
     alive_own = live_slots.astype(jnp.float32)
 
     def process(slot_items):
@@ -146,8 +186,9 @@
     got_back = partner(returned, TX, 0)
     kept = jnp.where((position < taken)[:, None, None, None], grad_terms, 0.0)
     own_terms = jnp.concatenate([kept, got_back], axis=0)
-    probe_total = sum_in_two_steps(jnp.sum(probe_terms, axis=0), TY_TX, (1, 0, 2, 3))
-    probe_grad = probe_total * (1.0 / math.sqrt(slots * devices_all))
+    probe_grad = all_sum(
+        jnp.sum(probe_terms, axis=0), ("ty_1", "ty_0", "tx_0", "tx_1"), 1.0 / math.sqrt(slots * devices_all)
+    )
 
     def place(slot_index, grad_ext):
         row_at = offsets[slot_index, 0]
@@ -157,11 +198,17 @@
             grad_ext, current + own_terms[slot_index], (anchor, row_at, col_at)
         )
 
-    grad_ext = lax.fori_loop(0, slots, place, jnp.zeros(extended.shape, jnp.float32))
-    from_above = passed_along(grad_ext[:, tile_h:, :], TY, 1)
-    upper_grad = grad_ext[:, :tile_h, :].at[:, :width, :].add(from_above)
-    from_left = passed_along(upper_grad[:, :, tile_w:], TX, 1)
-    core_grad = upper_grad[:, :, :tile_w].at[:, :, :width].add(from_left)
+    grad_ext = jnp.zeros(extended.shape, jnp.float32)
+    for k in range(slots):
+        grad_ext = place(k, grad_ext)
+    corner_above = passed_along(grad_ext[:, tile_h:, tile_w:], TY, 1)
+    below_part, corner_above = lax.optimization_barrier((grad_ext[:, tile_h:, :tile_w], corner_above))
+    below_above = passed_along(below_part, TY, 1)
+    left_bottom = passed_along(grad_ext[:, width:tile_h, tile_w:], TX, 1)
+    left_top = passed_along(grad_ext[:, :width, tile_w:] + corner_above, TX, 1)
+    top = (grad_ext[:, :width, :tile_w] + below_above).at[:, :, :width].add(left_top)
+    bottom = grad_ext[:, width:tile_h, :tile_w].at[:, :, :width].add(left_bottom)
+    core_grad = jnp.concatenate([top, bottom], axis=1)
     return (core_grad, probe_grad)
 
 

time: 689 us -> 479 us (0.70)
  the two profiles are of different devices: /device:TPU:48 before, /device:TPU:4 now
where the time goes in v1:
time: 479 us; the launch traced here: 473 us
  waiting for transfers between devices  227 us (47%)
  local copies, waits for them, and re-layouts  68.3 us (14%)
  starting transfers between devices  67.3 us (14%)
  other arithmetic  54 us (11%)
  matrix products  45.8 us (10%)
  between operations  10.7 us (2%)
    ppermute x8, waiting for transfers between devices, passed_along(): lax.ppermute(value, axis, [(source, source + steps) for source in range(i...  144 us
    ppermute x4, waiting for transfers between devices, partner(): return lax.ppermute(value, axis, pairs)  42.3 us
    dynamic_update_slice x2, local copies, waits for them, and re-layouts, place(): lax.dynamic_update_slice(grad_ext, current + own_terms[slot_index], (anch...  27.5 us
    ppermute x10, starting transfers between devices, gather_axis(): got = lax.ppermute(piece, axis, pairs)  25.1 us
    ppermute x10, waiting for transfers between devices, gather_axis(): got = lax.ppermute(piece, axis, pairs)  22.3 us
    ppermute x8, starting transfers between devices, passed_along(): lax.ppermute(value, axis, [(source, source + steps) for source in range(i...  22.2 us
    ppermute x10, waiting for transfers between devices, scatter_axis(): total = total + lax.ppermute(sent, axis, pairs)  18 us
    ppermute x10, starting transfers between devices, scatter_axis(): total = total + lax.ppermute(sent, axis, pairs)  17.6 us
  transfers between devices with their start and end apart: 32, of which 15 were waited for; matrix products, arithmetic and copies ran while one was open for 22% of the time, Pallas kernels for 0%

profile of v1, /device:TPU:4, one launch (start us, length us, event | category | flops | bytes accessed | tf_op | source)
XLA Modules:
  0.0 473.0 jit_solution(4913805690016648676)
XLA Ops:
  5.3 4.9 %collective-permute-start = (f32[2,512,512]{2,1,0:T(8,128)}, f32[2,512,512]{2,1,0:T(8,128)S(1)}, u32[]{:S(2)}, u32[]{:S(2)}) collective-permute-start(f32[2,512,512]{2,1,0:T(8,128)} %get-tuple-element.133), channel_id=1, source_target_pairs={{1,0},{2,1},{3,2},{4,3},{5,4},{6,5},{7,6},{8,7},{9,8},{10,9},{11,1... | collective-permute-start | bytes 6291464 | tf_op jit(solution)/shard_map/ppermute | solution.py:17
  11.5 43.9 %collective-permute-done = f32[2,512,512]{2,1,0:T(8,128)S(1)} collective-permute-done((f32[2,512,512]{2,1,0:T(8,128)}, f32[2,512,512]{2,1,0:T(8,128)S(1)}, u32[]{:S(2)}, u32[]{:S(2)}) %collective-permute-start) | collective-permute-done | bytes 2097184 | tf_op jit(solution)/shard_map/ppermute | solution.py:17
  55.4 6.4 %collective-permute-start.1 = (f32[2,512,512]{2,1,0:T(8,128)}, f32[2,512,512]{2,1,0:T(8,128)}, u32[]{:S(2)}, u32[]{:S(2)}) collective-permute-start(f32[2,512,512]{2,1,0:T(8,128)} %get-tuple-element.75), channel_id=1, source_target_pairs={{1,0},{2,1},{3,2},{4,3},{5,4},{6,5},{7,6},{8,7},{9,8},{10,9},{11,1... | collective-permute-start | bytes 6291464 | tf_op jit(solution)/shard_map/ppermute | solution.py:17
  71.0 35.1 %collective-permute-done.1 = f32[2,512,512]{2,1,0:T(8,128)} collective-permute-done((f32[2,512,512]{2,1,0:T(8,128)}, f32[2,512,512]{2,1,0:T(8,128)}, u32[]{:S(2)}, u32[]{:S(2)}) %collective-permute-start.1) | collective-permute-done | bytes 2097184 | tf_op jit(solution)/shard_map/ppermute | solution.py:17
  106.1 8.9 %maximum_maximum_fusion = f32[2,1536,1024]{2,1,0:T(8,128)S(1)} fusion(f32[2,512,512]{2,1,0:T(8,128)} %collective-permute-done.3, f32[2,512,512]{2,1,0:T(8,128)} %collective-permute-done.2, f32[2,512,512]{2,1,0:T(8,128)} %collective-permute-done.1, f32[2,512,512]{2,1,0:T(8,128)S(1)} %collective-permute-done, f32[2,1024,512]{2,1,0:T(8,128)} %param.15), kind=kLoop, calls=%fused_computation | loop fusion | flops 12582912 | bytes 25165824 | tf_op jit(solution)/shard_map/concatenate | solution.py:155
  124.8 42.3 %collective-permute-done.6 = f32[]{:T(128)} collective-permute-done((f32[]{:T(128)}, f32[]{:T(128)}, u32[]{:S(2)}, u32[]{:S(2)}) %collective-permute-start.6) | collective-permute-done | bytes 36 | tf_op jit(solution)/shard_map/ppermute | solution.py:23
  173.1 5.4 %convolution_bitcast_fusion.1 = f32[3,512,1024]{2,1,0:T(8,128)S(1)} fusion(bf16[3,512,512]{2,1,0:T(8,128)(2,1)S(1)} %get-tuple-element.131, bf16[3,512,512]{2,1,0:T(8,128)(2,1)S(1)} %get-tuple-element.130), kind=kOutput, calls=%fused_computation.60 | convolution fusion | flops 1621098496 | bytes 9437184 | tf_op jit(solution)/shard_map/while/body/eval_jaxpr/ij,mjk->mik/dot_general | solution.py:107
  178.5 5.6 %convolution_bitcast_fusion = f32[3,512,1024]{2,1,0:T(8,128)S(1)} fusion(bf16[3,512,512]{2,1,0:T(8,128)(2,1)S(1)} %get-tuple-element.131, bf16[3,512,512]{2,1,0:T(8,128)(2,1)S(1)} %get-tuple-element.130), kind=kOutput, calls=%fused_computation.59 | convolution fusion | flops 1621098496 | bytes 9437184 | tf_op jit(solution)/shard_map/while/body/eval_jaxpr/ij,mjk->mik/dot_general | solution.py:108
  186.0 5.5 %fusion.29 = f32[3,1024,512]{1,2,0:T(8,128)S(1)} fusion(bf16[3,512,512]{2,1,0:T(8,128)(2,1)S(1)} %get-tuple-element.127, bf16[3,512,512]{2,1,0:T(8,128)(2,1)S(1)} %get-tuple-element.126), kind=kOutput, calls=%fused_computation.78 | convolution fusion | flops 1621098496 | bytes 9437184 | tf_op jit(solution)/shard_map/while/body/eval_jaxpr/mij,jk->mik/dot_general | solution.py:113
  191.6 5.7 %fusion.30 = f32[3,1024,512]{1,2,0:T(8,128)S(1)} fusion(bf16[3,512,512]{2,1,0:T(8,128)(2,1)S(1)} %get-tuple-element.127, bf16[3,512,512]{2,1,0:T(8,128)(2,1)S(1)} %get-tuple-element.126), kind=kOutput, calls=%fused_computation.79 | convolution fusion | flops 1621098496 | bytes 9437184 | tf_op jit(solution)/shard_map/while/body/eval_jaxpr/mij,jk->mik/dot_general | solution.py:112
  201.3 5.5 %convolution_bitcast_fusion.2 = f32[3,512,1024]{2,1,0:T(8,128)S(1)} fusion(bf16[3,512,512]{1,2,0:T(8,128)(2,1)S(1)} %get-tuple-element.119, bf16[3,512,512]{1,2,0:T(8,128)(2,1)S(1)} %get-tuple-element.118), kind=kOutput, calls=%fused_computation.61 | convolution fusion | flops 1621098496 | bytes 9437184 | tf_op jit(solution)/shard_map/while/body/eval_jaxpr/ij,mjk->mik/dot_general | solution.py:108
  206.7 5.9 %convolution_bitcast_fusion.3 = f32[3,512,1024]{2,1,0:T(8,128)S(1)} fusion(bf16[3,512,512]{1,2,0:T(8,128)(2,1)S(1)} %get-tuple-element.119, bf16[3,512,512]{1,2,0:T(8,128)(2,1)S(1)} %get-tuple-element.118), kind=kOutput, calls=%fused_computation.62 | convolution fusion | flops 1621098496 | bytes 9437184 | tf_op jit(solution)/shard_map/while/body/eval_jaxpr/ij,mjk->mik/dot_general | solution.py:107
  216.0 5.0 %fusion.27 = f32[3,1024,512]{2,1,0:T(8,128)S(1)} fusion(bf16[3,512,512]{2,1,0:T(8,128)(2,1)S(1)} %get-tuple-element.125, bf16[3,512,512]{2,1,0:T(8,128)(2,1)S(1)} %get-tuple-element.124), kind=kOutput, calls=%fused_computation.76 | convolution fusion | flops 1621098496 | bytes 9437184 | tf_op jit(solution)/shard_map/while/body/eval_jaxpr/mij,jk->mik/dot_general | solution.py:113
  221.1 7.1 %fusion.28 = f32[3,1024,512]{2,1,0:T(8,128)S(1)} fusion(bf16[3,512,512]{2,1,0:T(8,128)(2,1)} %copy-done.12, bf16[3,512,512]{2,1,0:T(8,128)(2,1)} %copy-done.11), kind=kOutput, calls=%fused_computation.77 | convolution fusion | flops 1621098496 | bytes 9437184 | tf_op jit(solution)/shard_map/while/body/eval_jaxpr/mij,jk->mik/dot_general | solution.py:112
  255.2 6.2 %broadcast_in_dim.111 = f32[2,1536,1024]{2,1,0:T(8,128)} broadcast(f32[]{:T(128)} %constant.337.clone.1), dimensions={} | broadcast | bytes 12582916 | tf_op jit(solution)/shard_map/broadcast_in_dim | solution.py:201
  261.4 13.6 %dynamic_update_slice.58 = f32[2,1536,1024]{2,1,0:T(8,128)} dynamic-update-slice(f32[2,1536,1024]{2,1,0:T(8,128)} %broadcast_in_dim.111, f32[2,512,512]{2,1,0:T(8,128)S(1)} %copy-done.5, s32[]{:T(128)} %constant.340.clone.1, s32[]{:T(128)S(6)} %select_n.254, s32[]{:T(128)S(6)} %select_n.255) | dynamic-update-slice | bytes 4194308 | tf_op jit(solution)/shard_map/dynamic_update_slice | solution.py:197
  275.0 13.2 %collective-permute-done.15 = f32[384,512]{1,0:T(8,128)} collective-permute-done((f32[384,512]{1,0:T(8,128)}, f32[384,512]{1,0:T(8,128)}, u32[]{:S(2)}, u32[]{:S(2)}) %collective-permute-start.15) | collective-permute-done | bytes 786464 | tf_op jit(solution)/shard_map/ppermute | solution.py:67
  300.1 13.9 %dynamic_update_slice.59 = f32[2,1536,1024]{2,1,0:T(8,128)} dynamic-update-slice(f32[2,1536,1024]{2,1,0:T(8,128)} %dynamic_update_slice.58, f32[2,512,512]{2,1,0:T(8,128)S(1)} %bitcast_add_fusion, s32[]{:T(128)} %constant.340.clone.1, s32[]{:T(128)S(6)} %select_n.256, s32[]{:T(128)S(6)} %select_n.257) | dynamic-update-slice | bytes 4194308 | tf_op jit(solution)/shard_map/dynamic_update_slice | solution.py:197
  323.0 4.7 fusion.112
  350.7 10.3 %collective-permute-start.30 = (f32[384,512]{1,0:T(8,128)}, f32[384,512]{1,0:T(8,128)S(1)}, u32[]{:S(2)}, u32[]{:S(2)}) collective-permute-start(f32[384,512]{1,0:T(8,128)} %bitcast.62), channel_id=1, source_target_pairs={{0,96},{32,0},{64,32},{96,64},{1,97},{33,1},{65,33},{97,65},{2,98}... | collective-permute-start | bytes 2359304 | tf_op jit(solution)/shard_map/ppermute | solution.py:78
  372.7 13.5 %collective-permute-done.29 = f32[384,512]{1,0:T(8,128)} collective-permute-done((f32[384,512]{1,0:T(8,128)}, f32[384,512]{1,0:T(8,128)}, u32[]{:S(2)}, u32[]{:S(2)}) %collective-permute-start.29) | collective-permute-done | bytes 786464 | tf_op jit(solution)/shard_map/ppermute | solution.py:78
  391.6 19.6 %collective-permute-done.10 = f32[2,512,512]{2,1,0:T(8,128)S(1)} collective-permute-done((f32[2,512,512]{2,1,0:T(8,128)S(1)}, f32[2,512,512]{2,1,0:T(8,128)S(1)}, u32[]{:S(2)}, u32[]{:S(2)}) %collective-permute-start.10) | collective-permute-done | bytes 2097184 | tf_op jit(solution)/shard_map/ppermute | solution.py:17
  411.2 5.3 %fusion.26 = (f32[2,512,512]{2,1,0:T(8,128)}, f32[2,512,512]{2,1,0:T(8,128)}) fusion(f32[2,512,512]{2,1,0:T(8,128)S(1)} %collective-permute-done.10, f32[2,512,512]{2,1,0:T(8,128)S(1)} %collective-permute-done.9, f32[2,1536,1024]{2,1,0:T(8,128)} %dynamic_update_slice.59), kind=kLoop, calls=%fused_computation.69 | loop fusion | flops 1048576 | bytes 12582912 | tf_op jit(solution)/shard_map/add | solution.py:209
  421.9 45.7 %collective-permute-done.11 = f32[2,512,512]{2,1,0:T(8,128)} collective-permute-done((f32[2,512,512]{2,1,0:T(8,128)}, f32[2,512,512]{2,1,0:T(8,128)}, u32[]{:S(2)}, u32[]{:S(2)}) %collective-permute-start.11) | collective-permute-done | bytes 2097184 | tf_op jit(solution)/shard_map/ppermute | solution.py:17
  (147 shorter events, 129.2 us)
Async XLA Ops:
  5.3 50.1 %collective-permute-start = (f32[2,512,512]{2,1,0:T(8,128)}, f32[2,512,512]{2,1,0:T(8,128)S(1)}, u32[]{:S(2)}, u32[]{:S(2)}) collective-permute-start(f32[2,512,512]{2,1,0:T(8,128)} %get-tuple-element.133), channel_id=1, source_target_pairs={{1,0},{2,1},{3,2},{4,3},{5,4},{6,5},{7,6},{8,7},{9,8},{10,9},{11,1... | collective-permute-start | bytes 6291464 | tf_op jit(solution)/shard_map/ppermute | solution.py:17
  10.2 60.8 %collective-permute-start.2 = (f32[2,512,512]{2,1,0:T(8,128)}, f32[2,512,512]{2,1,0:T(8,128)}, u32[]{:S(2)}, u32[]{:S(2)}) collective-permute-start(f32[2,512,512]{2,1,0:T(8,128)} %get-tuple-element.133), channel_id=1, source_target_pairs={{16,0},{32,16},{48,32},{64,48},{80,64},{96,80},{112,96},{17,1},{33... | collective-permute-start | bytes 6291464 | tf_op jit(solution)/shard_map/ppermute | solution.py:17
  55.4 50.7 %collective-permute-start.1 = (f32[2,512,512]{2,1,0:T(8,128)}, f32[2,512,512]{2,1,0:T(8,128)}, u32[]{:S(2)}, u32[]{:S(2)}) collective-permute-start(f32[2,512,512]{2,1,0:T(8,128)} %get-tuple-element.75), channel_id=1, source_target_pairs={{1,0},{2,1},{3,2},{4,3},{5,4},{6,5},{7,6},{8,7},{9,8},{10,9},{11,1... | collective-permute-start | bytes 6291464 | tf_op jit(solution)/shard_map/ppermute | solution.py:17
  61.8 44.3 %collective-permute-start.3 = (f32[2,512,512]{2,1,0:T(8,128)S(1)}, f32[2,512,512]{2,1,0:T(8,128)}, u32[]{:S(2)}, u32[]{:S(2)}) collective-permute-start(f32[2,512,512]{2,1,0:T(8,128)S(1)} %collective-permute-done), channel_id=1, source_target_pairs={{16,0},{32,16},{48,32},{64,48},{80,64},{96,80},{112,96},{17,1},{33... | collective-permute-start | bytes 6291464 | tf_op jit(solution)/shard_map/ppermute | solution.py:17
  118.2 50.9 %collective-permute-start.4 = (f32[1,2,512,512]{3,2,1,0:T(8,128)}, f32[1,2,512,512]{3,2,1,0:T(8,128)}, u32[]{:S(2)}, u32[]{:S(2)}) collective-permute-start(f32[1,2,512,512]{3,2,1,0:T(8,128)} %get-tuple-element.128), channel_id=1, source_target_pairs={{0,1},{1,0},{2,3},{3,2},{4,5},{5,4},{6,7},{7,6},{8,9},{9,8},{10,11... | collective-permute-start | bytes 6291464 | tf_op jit(solution)/shard_map/ppermute | solution.py:23
  118.8 48.3 %collective-permute-start.6 = (f32[]{:T(128)}, f32[]{:T(128)}, u32[]{:S(2)}, u32[]{:S(2)}) collective-permute-start(f32[]{:T(128)} %convert_reduce_fusion), channel_id=1, source_target_pairs={{0,1},{1,0},{2,3},{3,2},{4,5},{5,4},{6,7},{7,6},{8,9},{9,8},{10,11... | collective-permute-start | bytes 20 | tf_op jit(solution)/shard_map/ppermute | solution.py:23
  122.4 76.6 %collective-permute-start.5 = (f32[1,512,512]{1,2,0:T(8,128)}, f32[1,512,512]{1,2,0:T(8,128)}, u32[]{:S(2)}, u32[]{:S(2)}) collective-permute-start(f32[1,512,512]{1,2,0:T(8,128)} %copy.25), channel_id=1, source_target_pairs={{0,1},{1,0},{2,3},{3,2},{4,5},{5,4},{6,7},{7,6},{8,9},{9,8},{10,11... | collective-permute-start | bytes 3145736 | tf_op jit(solution)/shard_map/ppermute | solution.py:23
  240.4 56.6 %collective-permute-start.7 = (f32[1,2,512,512]{3,2,1,0:T(8,128)}, f32[1,2,512,512]{3,2,1,0:T(8,128)}, u32[]{:S(2)}, u32[]{:S(2)}) collective-permute-start(f32[1,2,512,512]{3,2,1,0:T(8,128)} %fusion.23), channel_id=1, source_target_pairs={{0,1},{1,0},{2,3},{3,2},{4,5},{5,4},{6,7},{7,6},{8,9},{9,8},{10,11... | collective-permute-start | bytes 6291464 | tf_op jit(solution)/shard_map/ppermute | solution.py:23
  249.3 25.7 %collective-permute-start.13 = (f32[384,512]{1,0:T(8,128)}, f32[384,512]{1,0:T(8,128)S(1)}, u32[]{:S(2)}, u32[]{:S(2)}) collective-permute-start(f32[384,512]{1,0:T(8,128)} %get-tuple-element.135), channel_id=1, source_target_pairs={{0,32},{32,64},{64,96},{96,0},{1,33},{33,65},{65,97},{97,1},{2,34}... | collective-permute-start | bytes 2359304 | tf_op jit(solution)/shard_map/ppermute | solution.py:67
  251.2 37.0 %collective-permute-start.15 = (f32[384,512]{1,0:T(8,128)}, f32[384,512]{1,0:T(8,128)}, u32[]{:S(2)}, u32[]{:S(2)}) collective-permute-start(f32[384,512]{1,0:T(8,128)} %get-tuple-element.136), channel_id=1, source_target_pairs={{0,96},{32,0},{64,32},{96,64},{1,97},{33,1},{65,33},{97,65},{2,98}... | collective-permute-start | bytes 2359304 | tf_op jit(solution)/shard_map/ppermute | solution.py:67
  253.3 36.9 %collective-permute-start.14 = (f32[384,512]{1,0:T(8,128)}, f32[384,512]{1,0:T(8,128)}, u32[]{:S(2)}, u32[]{:S(2)}) collective-permute-start(f32[384,512]{1,0:T(8,128)} %get-tuple-element.137), channel_id=1, source_target_pairs={{0,64},{32,96},{64,0},{96,32},{1,65},{33,97},{65,1},{97,33},{2,66}... | collective-permute-start | bytes 2359304 | tf_op jit(solution)/shard_map/ppermute | solution.py:67
  293.2 20.8 %collective-permute-start.16 = (f32[96,512]{1,0:T(8,128)}, f32[96,512]{1,0:T(8,128)S(1)}, u32[]{:S(2)}, u32[]{:S(2)}) collective-permute-start(f32[96,512]{1,0:T(8,128)} %get-tuple-element.144), channel_id=1, source_target_pairs={{0,4},{4,8},{8,12},{12,0},{1,5},{5,9},{9,13},{13,1},{2,6},{6,10},{... | collective-permute-start | bytes 589832 | tf_op jit(solution)/shard_map/ppermute | solution.py:67
  294.9 19.1 %collective-permute-start.18 = (f32[96,512]{1,0:T(8,128)S(1)}, f32[96,512]{1,0:T(8,128)}, u32[]{:S(2)}, u32[]{:S(2)}) collective-permute-start(f32[96,512]{1,0:T(8,128)S(1)} %get-tuple-element.145), channel_id=1, source_target_pairs={{0,12},{4,0},{8,4},{12,8},{1,13},{5,1},{9,5},{13,9},{2,14},{6,2},{... | collective-permute-start | bytes 589832 | tf_op jit(solution)/shard_map/ppermute | solution.py:67
  295.4 18.6 %collective-permute-start.17 = (f32[96,512]{1,0:T(8,128)S(1)}, f32[96,512]{1,0:T(8,128)}, u32[]{:S(2)}, u32[]{:S(2)}) collective-permute-start(f32[96,512]{1,0:T(8,128)S(1)} %get-tuple-element.146), channel_id=1, source_target_pairs={{0,8},{4,12},{8,0},{12,4},{1,9},{5,13},{9,1},{13,5},{2,10},{6,14},... | collective-permute-start | bytes 589832 | tf_op jit(solution)/shard_map/ppermute | solution.py:67
  315.1 14.0 %collective-permute-start.19 = (f32[24,512]{1,0:T(8,128)S(1)}, f32[24,512]{1,0:T(8,128)S(1)}, u32[]{:S(2)}, u32[]{:S(2)}) collective-permute-start(f32[24,512]{1,0:T(8,128)S(1)} %get-tuple-element.147), channel_id=1, source_target_pairs={{0,1},{1,2},{2,3},{3,0},{4,5},{5,6},{6,7},{7,4},{8,9},{9,10},{10,1... | collective-permute-start | bytes 147464 | tf_op jit(solution)/shard_map/ppermute | solution.py:67
  327.7 23.0 %collective-permute-start.8 = (f32[2,512,512]{2,1,0:T(8,128)}, f32[2,512,512]{2,1,0:T(8,128)S(1)}, u32[]{:S(2)}, u32[]{:S(2)}) collective-permute-start(f32[2,512,512]{2,1,0:T(8,128)} %get-tuple-element.122), channel_id=1, source_target_pairs={{0,16},{16,32},{32,48},{48,64},{64,80},{80,96},{96,112},{1,17},{17... | collective-permute-start | bytes 6291464 | tf_op jit(solution)/shard_map/ppermute | solution.py:17
  336.4 12.2 %collective-permute-start.27 = (f32[96,512]{1,0:T(8,128)S(1)}, f32[96,512]{1,0:T(8,128)S(1)}, u32[]{:S(2)}, u32[]{:S(2)}) collective-permute-start(f32[96,512]{1,0:T(8,128)S(1)} %bitcast.196), channel_id=1, source_target_pairs={{0,12},{4,0},{8,4},{12,8},{1,13},{5,1},{9,5},{13,9},{2,14},{6,2},{... | collective-permute-start | bytes 589832 | tf_op jit(solution)/shard_map/ppermute | solution.py:78
  349.4 22.1 %collective-permute-start.28 = (f32[384,512]{1,0:T(8,128)}, f32[384,512]{1,0:T(8,128)}, u32[]{:S(2)}, u32[]{:S(2)}) collective-permute-start(f32[384,512]{1,0:T(8,128)} %bitcast.62), channel_id=1, source_target_pairs={{0,32},{32,64},{64,96},{96,0},{1,33},{33,65},{65,97},{97,1},{2,34}... | collective-permute-start | bytes 2359304 | tf_op jit(solution)/shard_map/ppermute | solution.py:78
  349.7 36.5 %collective-permute-start.29 = (f32[384,512]{1,0:T(8,128)}, f32[384,512]{1,0:T(8,128)}, u32[]{:S(2)}, u32[]{:S(2)}) collective-permute-start(f32[384,512]{1,0:T(8,128)} %bitcast.62), channel_id=1, source_target_pairs={{0,64},{32,96},{64,0},{96,32},{1,65},{33,97},{65,1},{97,33},{2,66}... | collective-permute-start | bytes 2359304 | tf_op jit(solution)/shard_map/ppermute | solution.py:78
  350.7 37.1 %collective-permute-start.30 = (f32[384,512]{1,0:T(8,128)}, f32[384,512]{1,0:T(8,128)S(1)}, u32[]{:S(2)}, u32[]{:S(2)}) collective-permute-start(f32[384,512]{1,0:T(8,128)} %bitcast.62), channel_id=1, source_target_pairs={{0,96},{32,0},{64,32},{96,64},{1,97},{33,1},{65,33},{97,65},{2,98}... | collective-permute-start | bytes 2359304 | tf_op jit(solution)/shard_map/ppermute | solution.py:78
  363.1 48.1 %collective-permute-start.10 = (f32[2,512,512]{2,1,0:T(8,128)S(1)}, f32[2,512,512]{2,1,0:T(8,128)S(1)}, u32[]{:S(2)}, u32[]{:S(2)}) collective-permute-start(f32[2,512,512]{2,1,0:T(8,128)S(1)} %slice_add_fusion.3), channel_id=1, source_target_pairs={{0,1},{1,2},{2,3},{3,4},{4,5},{5,6},{6,7},{7,8},{8,9},{9,10},{10,1... | collective-permute-start | bytes 6291464 | tf_op jit(solution)/shard_map/ppermute | solution.py:17
  366.6 44.5 %collective-permute-start.9 = (f32[2,512,512]{2,1,0:T(8,128)S(1)}, f32[2,512,512]{2,1,0:T(8,128)S(1)}, u32[]{:S(2)}, u32[]{:S(2)}) collective-permute-start(f32[2,512,512]{2,1,0:T(8,128)S(1)} %copy-done.10), channel_id=1, source_target_pairs={{0,16},{16,32},{32,48},{48,64},{64,80},{80,96},{96,112},{1,17},{17... | collective-permute-start | bytes 6291464 | tf_op jit(solution)/shard_map/ppermute | solution.py:17
  387.9 31.7 %collective-permute-start.31 = (f32[1536,512]{1,0:T(8,128)S(1)}, f32[1536,512]{1,0:T(8,128)}, u32[]{:S(2)}, u32[]{:S(2)}) collective-permute-start(f32[1536,512]{1,0:T(8,128)S(1)} %bitcast.184), channel_id=1, source_target_pairs={{0,16},{16,0},{1,17},{17,1},{2,18},{18,2},{3,19},{19,3},{4,20},{20... | collective-permute-start | bytes 9437192 | tf_op jit(solution)/shard_map/ppermute | solution.py:78
  416.4 51.1 %collective-permute-start.11 = (f32[2,512,512]{2,1,0:T(8,128)}, f32[2,512,512]{2,1,0:T(8,128)}, u32[]{:S(2)}, u32[]{:S(2)}) collective-permute-start(f32[2,512,512]{2,1,0:T(8,128)} %get-tuple-element.121), channel_id=1, source_target_pairs={{0,1},{1,2},{2,3},{3,4},{4,5},{5,6},{6,7},{7,8},{8,9},{9,10},{10,1... | collective-permute-start | bytes 6291464 | tf_op jit(solution)/shard_map/ppermute | solution.py:17
  (28 other events, 393.9 us)

commit v2 on v1

--- a/solution.py
+++ b/solution.py
@@ -136,79 +136,80 @@
     return (jnp.stack([grad_re, grad_im]), jnp.stack([mode_re, mode_im]))
 
 
+def shifted(value, axis, pairs):
+    return lax.ppermute(value, axis, [(a, b) for a, b in pairs if 0 <= b < lax.axis_size(axis)])
+
+
 def local(specimen, probe_modes, amplitude, offsets, live_slots):
     tile_h = specimen.shape[1]
-    tile_w = specimen.shape[2]
     width = probe_modes.shape[2]
     slots = live_slots.shape[0]
     devices_all = lax.axis_size(TY) * lax.axis_size(TX)
+    count = lax.axis_size(TX)
+    evens = range(0, count, 2)
+    odds = range(1, count, 2)
     anchor = jnp.zeros((), jnp.int32)
-    right_top = passed_along(specimen[:, :width, :], TX, -1)
-    later_rows, right_top = lax.optimization_barrier((specimen[:, width:, :], right_top))
-    right_bottom = passed_along(later_rows, TX, -1)
-    below_own = passed_along(specimen[:, :width, :], TY, -1)
-    below_right = passed_along(right_top, TY, -1)
-    upper_rows = jnp.concatenate(
-        [specimen, jnp.concatenate([right_top, right_bottom], axis=1)], axis=2
+    cos_table, sin_table = tables(width)
+
+    alive_own = live_slots.astype(jnp.float32)
+    live_count = jnp.sum(alive_own)
+    got_measured, got_count, got_offset = partner((amplitude[1:], live_count, offsets[1]), TX, 0)
+    use_own = live_count >= 1.0
+    is_odd = lax.axis_index(TX) % 2 == 1
+    shift = jnp.where(use_own, 0, jnp.where(is_odd, -1, 1))
+    row_at = jnp.where(use_own, offsets[0, 0], got_offset[0])
+    col_at = jnp.where(use_own, offsets[0, 1], got_offset[1])
+    measured = jnp.where(use_own, amplitude[0], got_measured[0])
+    alive = jnp.where(use_own, alive_own[0], (1.0 < got_count).astype(jnp.float32))
+
+    row_left = shifted(row_at, TX, [(s, s + 1) for s in range(count)])
+    row_right = shifted(row_at, TX, [(s, s - 1) for s in range(count)])
+    row_left2 = shifted(row_at, TX, [(s, s + 2) for s in evens])
+
+    below = passed_along(specimen[:, :width, :], TY, -1)
+    column = jnp.concatenate([specimen, below], axis=1)
+
+    def strip(source, at):
+        return lax.dynamic_slice(source, (anchor, at, anchor), (2, width, width))
+
+    own_strip = strip(column, row_at)
+    from_right = shifted(strip(column, row_left), TX, [(s, s - 1) for s in range(count)])
+    from_left = shifted(strip(column, row_right), TX, [(s, s + 1) for s in evens])
+    from_right2 = shifted(strip(column, row_left2), TX, [(s, s - 2) for s in evens])
+    left_strip = jnp.where(shift == 0, own_strip, jnp.where(shift < 0, from_left, from_right))
+    right_strip = jnp.where(shift == 0, from_right, jnp.where(shift < 0, own_strip, from_right2))
+    pair_strip = jnp.concatenate([left_strip, right_strip], axis=2)
+    window = lax.dynamic_slice(pair_strip, (anchor, anchor, col_at), (2, width, width))
+
+    grad_term, probe_term = slot_terms(window, probe_modes, measured, alive, cos_table, sin_table)
+
+    probe_grad = all_sum(probe_term, ("ty_1", "ty_0", "tx_0", "tx_1"), 1.0 / math.sqrt(slots * devices_all))
+
+    placed = lax.dynamic_update_slice(
+        jnp.zeros((2, width, 2 * width), jnp.float32), grad_term, (anchor, anchor, col_at)
     )
-    lower_rows = jnp.concatenate([below_own, below_right], axis=2)
-    extended = jnp.concatenate([upper_rows, lower_rows], axis=1)
-    cos_table, sin_table = tables(width)
-
-    def crop(row_at, col_at):
-        return lax.dynamic_slice(extended, (anchor, row_at, col_at), (2, width, width))
-
-    windows = jnp.stack([crop(offsets[k, 0], offsets[k, 1]) for k in range(slots)])
-    alive_own = live_slots.astype(jnp.float32)
-
-    def process(slot_items):
-        window, measured, alive_mask = slot_items
-        return slot_terms(window, probe_modes, measured, alive_mask, cos_table, sin_table)
-
-    half_slots = slots // 2
-    live_count = jnp.sum(alive_own)
-    got_windows, got_measured, got_count = partner(
-        (windows[half_slots:], amplitude[half_slots:], live_count), TX, 0
-    )
-    position = jnp.arange(half_slots, dtype=jnp.int32)
-    taken = jnp.minimum(live_count, float(half_slots)).astype(jnp.int32)
-    got_alive = ((position + half_slots).astype(jnp.float32) < got_count).astype(jnp.float32)
-    pool_windows = jnp.concatenate([windows[:half_slots], got_windows], axis=0)
-    pool_measured = jnp.concatenate([amplitude[:half_slots], got_measured], axis=0)
-    pool_alive = jnp.concatenate([alive_own[:half_slots], got_alive], axis=0)
-    order_index = jnp.where(position < taken, position, half_slots + position - taken)
-    work_windows = jnp.take(pool_windows, order_index, axis=0)
-    work_measured = jnp.take(pool_measured, order_index, axis=0)
-    work_alive = jnp.take(pool_alive, order_index, axis=0)
-    grad_terms, probe_terms = lax.map(process, (work_windows, work_measured, work_alive))
-    padded_terms = jnp.concatenate([grad_terms, jnp.zeros_like(grad_terms)], axis=0)
-    returned = jnp.take(padded_terms, taken + position, axis=0)
-    got_back = partner(returned, TX, 0)
-    kept = jnp.where((position < taken)[:, None, None, None], grad_terms, 0.0)
-    own_terms = jnp.concatenate([kept, got_back], axis=0)
-    probe_grad = all_sum(
-        jnp.sum(probe_terms, axis=0), ("ty_1", "ty_0", "tx_0", "tx_1"), 1.0 / math.sqrt(slots * devices_all)
-    )
-
-    def place(slot_index, grad_ext):
-        row_at = offsets[slot_index, 0]
-        col_at = offsets[slot_index, 1]
-        current = lax.dynamic_slice(grad_ext, (anchor, row_at, col_at), (2, width, width))
-        return lax.dynamic_update_slice(
-            grad_ext, current + own_terms[slot_index], (anchor, row_at, col_at)
-        )
-
-    grad_ext = jnp.zeros(extended.shape, jnp.float32)
-    for k in range(slots):
-        grad_ext = place(k, grad_ext)
-    corner_above = passed_along(grad_ext[:, tile_h:, tile_w:], TY, 1)
-    below_part, corner_above = lax.optimization_barrier((grad_ext[:, tile_h:, :tile_w], corner_above))
-    below_above = passed_along(below_part, TY, 1)
-    left_bottom = passed_along(grad_ext[:, width:tile_h, tile_w:], TX, 1)
-    left_top = passed_along(grad_ext[:, :width, tile_w:] + corner_above, TX, 1)
-    top = (grad_ext[:, :width, :tile_w] + below_above).at[:, :, :width].add(left_top)
-    bottom = grad_ext[:, width:tile_h, :tile_w].at[:, :, :width].add(left_bottom)
-    core_grad = jnp.concatenate([top, bottom], axis=1)
+    grad_left = placed[:, :, :width]
+    grad_right = placed[:, :, width:]
+    zeros = jnp.zeros_like(grad_left)
+    send_right = jnp.where(shift == 0, grad_right, jnp.where(shift > 0, grad_left, zeros))
+    send_right2 = jnp.where(shift > 0, grad_right, zeros)
+    send_left = jnp.where(shift < 0, grad_left, zeros)
+    keep = jnp.where(shift == 0, grad_left, jnp.where(shift < 0, grad_right, zeros))
+    got_left = shifted(send_right, TX, [(s, s + 1) for s in range(count)])
+    got_left2 = shifted(send_right2, TX, [(s, s + 2) for s in evens])
+    got_right = shifted(send_left, TX, [(s, s - 1) for s in odds])
+
+    def add_strip(total, piece, at):
+        current = lax.dynamic_slice(total, (anchor, at, anchor), (2, width, width))
+        return lax.dynamic_update_slice(total, current + piece, (anchor, at, anchor))
+
+    grad_column = jnp.zeros(column.shape, jnp.float32)
+    grad_column = add_strip(grad_column, keep, row_at)
+    grad_column = add_strip(grad_column, got_left, row_left)
+    grad_column = add_strip(grad_column, got_left2, row_left2)
+    grad_column = add_strip(grad_column, got_right, row_right)
+    from_above = passed_along(grad_column[:, tile_h:, :], TY, 1)
+    core_grad = grad_column[:, :tile_h, :].at[:, :width, :].add(from_above)
     return (core_grad, probe_grad)
 
 

time: 479 us -> 514 us (1.073)
  the two profiles are of different devices: /device:TPU:4 before, /device:TPU:48 now
where the time goes in v2:
time: 514 us; the launch traced here: 507 us
  waiting for transfers between devices  237 us (46%)
  local copies, waits for them, and re-layouts  93.2 us (18%)
  starting transfers between devices  68.5 us (13%)
  other arithmetic  50.9 us (10%)
  matrix products  46 us (9%)
  between operations  11 us (2%)
    ppermute x10, waiting for transfers between devices, gather_axis(): got = lax.ppermute(piece, axis, pairs)  93.1 us
    ppermute x3, waiting for transfers between devices, partner(): return lax.ppermute(value, axis, pairs)  79.7 us
    ppermute x10, waiting for transfers between devices, scatter_axis(): total = total + lax.ppermute(sent, axis, pairs)  40.8 us
    ppermute x9, starting transfers between devices, shifted(): lax.ppermute(value, axis, [(a, b) for a, b in pairs if 0 <= b < lax.axis_...  29 us
    dynamic_update_slice x4, local copies, waits for them, and re-layouts, add_strip(): lax.dynamic_update_slice(total, current + piece, (anchor, at, anchor))  27.9 us
    ppermute x2, waiting for transfers between devices, passed_along(): lax.ppermute(value, axis, [(source, source + steps) for source in range(i...  22.3 us
    ppermute x10, starting transfers between devices, gather_axis(): got = lax.ppermute(piece, axis, pairs)  16.6 us
    unnamed x41, local copies, waits for them, and re-layouts  15.4 us
  transfers between devices with their start and end apart: 34, of which 11 were waited for; matrix products, arithmetic and copies ran while one was open for 24% of the time, Pallas kernels for 0%

profile of v2, /device:TPU:48, one launch (start us, length us, event | category | flops | bytes accessed | tf_op | source)
XLA Modules:
  0.0 507.0 jit_solution(6036556289836186287)
XLA Ops:
  18.7 5.2 %collective-permute-start.4 = (s32[]{:T(128)}, s32[]{:T(128)}, u32[]{:S(2)}, u32[]{:S(2)}) collective-permute-start(s32[]{:T(128)} %select_n.293), channel_id=1, source_target_pairs={{0,1},{1,2},{2,3},{3,4},{4,5},{5,6},{6,7},{7,8},{8,9},{9,10},{10,1... | collective-permute-start | bytes 20 | tf_op jit(solution)/shard_map/ppermute | solution.py:140
  36.0 6.0 %constant_dynamic-slice_fusion = (f32[2,512,512]{2,1,0:T(8,128)}, f32[2,512,512]{2,1,0:T(8,128)}, f32[2,512,512]{2,1,0:T(8,128)}) fusion(f32[2,1536,512]{2,1,0:T(8,128)} %constant_dynamic-update-slice_fusion, s32[]{:T(128)S(6)} %select_n.300, s32[]{:T(128)S(6)} %select_n.297, s32[]{:T(128)S(6)} %select_n.296), kind=kLoop, calls=%fused_computation.134 | loop fusion | bytes 12582924 | tf_op jit(solution)/shard_map/dynamic_slice | solution.py:173
  54.8 79.7 %collective-permute-done.9 = f32[]{:T(128)} collective-permute-done((f32[]{:T(128)}, f32[]{:T(128)}, u32[]{:S(2)}, u32[]{:S(2)}) %collective-permute-start.9) | collective-permute-done | bytes 36 | tf_op jit(solution)/shard_map/ppermute | solution.py:23
  144.7 5.4 %convolution_bitcast_fusion.1 = f32[3,512,1024]{2,1,0:T(8,128)S(1)} fusion(bf16[3,512,512]{2,1,0:T(8,128)(2,1)S(1)} %get-tuple-element.28, bf16[3,512,512]{2,1,0:T(8,128)(2,1)S(1)} %get-tuple-element.27), kind=kOutput, calls=%fused_computation.57 | convolution fusion | flops 1621098496 | bytes 9437184 | tf_op jit(solution)/shard_map/ij,mjk->mik/dot_general | solution.py:107
  150.1 5.7 %convolution_bitcast_fusion = f32[3,512,1024]{2,1,0:T(8,128)S(1)} fusion(bf16[3,512,512]{2,1,0:T(8,128)(2,1)S(1)} %get-tuple-element.28, bf16[3,512,512]{2,1,0:T(8,128)(2,1)S(1)} %get-tuple-element.27), kind=kOutput, calls=%fused_computation.56 | convolution fusion | flops 1621098496 | bytes 9437184 | tf_op jit(solution)/shard_map/ij,mjk->mik/dot_general | solution.py:108
  157.6 5.5 %fusion.28 = f32[3,1024,512]{1,2,0:T(8,128)S(1)} fusion(bf16[3,512,512]{2,1,0:T(8,128)(2,1)S(1)} %get-tuple-element.26, bf16[3,512,512]{2,1,0:T(8,128)(2,1)S(1)} %get-tuple-element.25), kind=kOutput, calls=%fused_computation.74 | convolution fusion | flops 1621098496 | bytes 9437184 | tf_op jit(solution)/shard_map/mij,jk->mik/dot_general | solution.py:112
  163.1 5.9 %fusion.27 = f32[3,1024,512]{1,2,0:T(8,128)S(1)} fusion(bf16[3,512,512]{2,1,0:T(8,128)(2,1)S(1)} %get-tuple-element.26, bf16[3,512,512]{2,1,0:T(8,128)(2,1)S(1)} %get-tuple-element.25), kind=kOutput, calls=%fused_computation.73 | convolution fusion | flops 1621098496 | bytes 9437184 | tf_op jit(solution)/shard_map/mij,jk->mik/dot_general | solution.py:113
  173.0 5.6 %convolution_bitcast_fusion.3 = f32[3,512,1024]{2,1,0:T(8,128)S(1)} fusion(bf16[3,512,512]{1,2,0:T(8,128)(2,1)S(1)} %get-tuple-element.22, bf16[3,512,512]{1,2,0:T(8,128)(2,1)S(1)} %get-tuple-element.21), kind=kOutput, calls=%fused_computation.59 | convolution fusion | flops 1621098496 | bytes 9437184 | tf_op jit(solution)/shard_map/ij,mjk->mik/dot_general | solution.py:107
  178.6 5.5 %convolution_bitcast_fusion.2 = f32[3,512,1024]{2,1,0:T(8,128)S(1)} fusion(bf16[3,512,512]{1,2,0:T(8,128)(2,1)S(1)} %get-tuple-element.22, bf16[3,512,512]{1,2,0:T(8,128)(2,1)S(1)} %get-tuple-element.21), kind=kOutput, calls=%fused_computation.58 | convolution fusion | flops 1621098496 | bytes 9437184 | tf_op jit(solution)/shard_map/ij,mjk->mik/dot_general | solution.py:108
  187.5 5.0 fusion.26
  192.5 7.5 %fusion.25 = f32[3,1024,512]{2,1,0:T(8,128)S(1)} fusion(bf16[3,512,512]{2,1,0:T(8,128)(2,1)} %copy-done.12, bf16[3,512,512]{2,1,0:T(8,128)(2,1)} %copy-done.11), kind=kOutput, calls=%fused_computation.71 | convolution fusion | flops 1621098496 | bytes 9437184 | tf_op jit(solution)/shard_map/mij,jk->mik/dot_general | solution.py:113
  209.7 6.0 %collective-permute-done.14 = f32[1536,512]{1,0:T(8,128)} collective-permute-done((f32[1536,512]{1,0:T(8,128)}, f32[1536,512]{1,0:T(8,128)}, u32[]{:S(2)}, u32[]{:S(2)}) %collective-permute-start.14) | collective-permute-done | bytes 3145760 | tf_op jit(solution)/shard_map/ppermute | solution.py:67
  227.6 14.8 %collective-permute-done.15 = f32[384,512]{1,0:T(8,128)S(1)} collective-permute-done((f32[384,512]{1,0:T(8,128)}, f32[384,512]{1,0:T(8,128)S(1)}, u32[]{:S(2)}, u32[]{:S(2)}) %collective-permute-start.15) | collective-permute-done | bytes 786464 | tf_op jit(solution)/shard_map/ppermute | solution.py:67
  246.0 16.5 %collective-permute-done.17 = f32[384,512]{1,0:T(8,128)} collective-permute-done((f32[384,512]{1,0:T(8,128)}, f32[384,512]{1,0:T(8,128)}, u32[]{:S(2)}, u32[]{:S(2)}) %collective-permute-start.17) | collective-permute-done | bytes 786464 | tf_op jit(solution)/shard_map/ppermute | solution.py:67
  275.3 11.2 %dynamic_update_slice.61 = f32[2,512,1024]{2,1,0:T(8,128)} dynamic-update-slice(f32[2,512,1024]{2,1,0:T(8,128)} %broadcast_in_dim.65, f32[2,512,512]{2,1,0:T(8,128)S(1)} %pad_maximum_fusion.4, s32[]{:T(128)} %constant.248.clone.1, s32[]{:T(128)} %constant.248.clone.1, s32[]{:T(128)S(6)} %select_n.304) | dynamic-update-slice | bytes 4194308 | tf_op jit(solution)/shard_map/dynamic_update_slice | solution.py:188
  291.1 5.8 %slice_select_fusion.1 = (f32[2,512,512]{2,1,0:T(8,128)}, f32[2,512,512]{2,1,0:T(8,128)}, f32[2,512,512]{2,1,0:T(8,128)}, f32[2,512,512]{2,1,0:T(8,128)S(1)}) fusion(f32[2,512,1024]{2,1,0:T(8,128)} %dynamic_update_slice.61, pred[]{:T(512)S(6)} %lt.221, pred[]{:T(512)S(6)} %gt.8, pred[]{:T(512)S(6)} %eq.34), kind=kLoop, calls=%fused_computation.76 | loop fusion | flops 3145728 | bytes 12582915 | tf_op jit(solution)/shard_map/jit(_where)/select_n | solution.py:196
  306.5 40.2 %collective-permute-done.24 = f32[24,512]{1,0:T(8,128)S(1)} collective-permute-done((f32[24,512]{1,0:T(8,128)S(1)}, f32[24,512]{1,0:T(8,128)S(1)}, u32[]{:S(2)}, u32[]{:S(2)}) %collective-permute-start.24) | collective-permute-done | bytes 49184 | tf_op jit(solution)/shard_map/ppermute | solution.py:78
  361.2 43.0 %collective-permute-done.28 = f32[96,512]{1,0:T(8,128)S(1)} collective-permute-done((f32[96,512]{1,0:T(8,128)S(1)}, f32[96,512]{1,0:T(8,128)S(1)}, u32[]{:S(2)}, u32[]{:S(2)}) %collective-permute-start.28) | collective-permute-done | bytes 196640 | tf_op jit(solution)/shard_map/ppermute | solution.py:78
  411.1 6.7 %dynamic_update_slice.62 = f32[2,1536,512]{2,1,0:T(8,128)} dynamic-update-slice(f32[2,1536,512]{2,1,0:T(8,128)} %broadcast.80.clone, f32[2,512,512]{2,1,0:T(8,128)S(1)} %get-tuple-element.38, s32[]{:T(128)} %constant.248.clone.1, s32[]{:T(128)S(6)} %select_n.294, s32[]{:T(128)} %constant.248.clone.1) | dynamic-update-slice | bytes 4194308 | tf_op jit(solution)/shard_map/dynamic_update_slice | solution.py:204
  423.1 7.1 %dynamic_update_slice.63 = f32[2,1536,512]{2,1,0:T(8,128)} dynamic-update-slice(f32[2,1536,512]{2,1,0:T(8,128)} %dynamic_update_slice.62, f32[2,512,512]{2,1,0:T(8,128)S(1)} %dynamic-slice_add_fusion.2, s32[]{:T(128)} %constant.248.clone.1, s32[]{:T(128)S(6)} %select_n.297, s32[]{:T(128)} %constant.248.clone.1) | dynamic-update-slice | bytes 4194308 | tf_op jit(solution)/shard_map/dynamic_update_slice | solution.py:204
  434.2 8.1 %collective-permute-done.32 = f32[384,512]{1,0:T(8,128)} collective-permute-done((f32[384,512]{1,0:T(8,128)}, f32[384,512]{1,0:T(8,128)}, u32[]{:S(2)}, u32[]{:S(2)}) %collective-permute-start.32) | collective-permute-done | bytes 786464 | tf_op jit(solution)/shard_map/ppermute | solution.py:78
  447.7 7.1 %dynamic_update_slice.64 = f32[2,1536,512]{2,1,0:T(8,128)} dynamic-update-slice(f32[2,1536,512]{2,1,0:T(8,128)} %dynamic_update_slice.63, f32[2,512,512]{2,1,0:T(8,128)} %dynamic-slice_add_fusion.1, s32[]{:T(128)} %constant.248.clone.1, s32[]{:T(128)S(6)} %select_n.300, s32[]{:T(128)} %constant.248.clone.1) | dynamic-update-slice | bytes 4194308 | tf_op jit(solution)/shard_map/dynamic_update_slice | solution.py:204
  458.8 7.1 %dynamic_update_slice.65 = f32[2,1536,512]{2,1,0:T(8,128)} dynamic-update-slice(f32[2,1536,512]{2,1,0:T(8,128)} %dynamic_update_slice.64, f32[2,512,512]{2,1,0:T(8,128)} %dynamic-slice_add_fusion, s32[]{:T(128)} %constant.248.clone.1, s32[]{:T(128)S(6)} %select_n.296, s32[]{:T(128)} %constant.248.clone.1) | dynamic-update-slice | bytes 4194308 | tf_op jit(solution)/shard_map/dynamic_update_slice | solution.py:204
  474.4 22.3 %collective-permute-done.13 = f32[2,512,512]{2,1,0:T(8,128)} collective-permute-done((f32[2,512,512]{2,1,0:T(8,128)}, f32[2,512,512]{2,1,0:T(8,128)}, u32[]{:S(2)}, u32[]{:S(2)}) %collective-permute-start.13) | collective-permute-done | bytes 2097184 | tf_op jit(solution)/shard_map/ppermute | solution.py:17
  (155 shorter events, 163.3 us)
Async XLA Ops:
  3.7 30.7 %collective-permute-start = (f32[2,512,512]{2,1,0:T(8,128)}, f32[2,512,512]{2,1,0:T(8,128)S(1)}, u32[]{:S(2)}, u32[]{:S(2)}) collective-permute-start(f32[2,512,512]{2,1,0:T(8,128)} %slice.125), channel_id=1, source_target_pairs={{16,0},{32,16},{48,32},{64,48},{80,64},{96,80},{112,96},{17,1},{33... | collective-permute-start | bytes 6291464 | tf_op jit(solution)/shard_map/ppermute | solution.py:17
  42.0 94.6 %collective-permute-start.3 = (f32[2,512,512]{2,1,0:T(8,128)}, f32[2,512,512]{2,1,0:T(8,128)}, u32[]{:S(2)}, u32[]{:S(2)}) collective-permute-start(f32[2,512,512]{2,1,0:T(8,128)} %get-tuple-element.34), channel_id=1, source_target_pairs={{0,1},{2,3},{4,5},{6,7},{8,9},{10,11},{12,13},{14,15},{16,17},{18,... | collective-permute-start | bytes 6291464 | tf_op jit(solution)/shard_map/ppermute | solution.py:140
  44.7 91.9 %collective-permute-start.5 = (f32[2,512,512]{2,1,0:T(8,128)}, f32[2,512,512]{2,1,0:T(8,128)}, u32[]{:S(2)}, u32[]{:S(2)}) collective-permute-start(f32[2,512,512]{2,1,0:T(8,128)} %get-tuple-element.33), channel_id=1, source_target_pairs={{1,0},{2,1},{3,2},{4,3},{5,4},{6,5},{7,6},{8,7},{9,8},{10,9},{11,1... | collective-permute-start | bytes 6291464 | tf_op jit(solution)/shard_map/ppermute | solution.py:140
  46.6 91.5 %collective-permute-start.7 = (f32[2,512,512]{2,1,0:T(8,128)}, f32[2,512,512]{2,1,0:T(8,128)}, u32[]{:S(2)}, u32[]{:S(2)}) collective-permute-start(f32[2,512,512]{2,1,0:T(8,128)} %get-tuple-element.32), channel_id=1, source_target_pairs={{2,0},{4,2},{6,4},{8,6},{10,8},{12,10},{14,12},{18,16},{20,18},{22... | collective-permute-start | bytes 6291464 | tf_op jit(solution)/shard_map/ppermute | solution.py:140
  49.7 84.8 %collective-permute-start.9 = (f32[]{:T(128)}, f32[]{:T(128)}, u32[]{:S(2)}, u32[]{:S(2)}) collective-permute-start(f32[]{:T(128)} %convert_reduce_fusion), channel_id=1, source_target_pairs={{0,1},{1,0},{2,3},{3,2},{4,5},{5,4},{6,7},{7,6},{8,9},{9,8},{10,11... | collective-permute-start | bytes 20 | tf_op jit(solution)/shard_map/ppermute | solution.py:23
  52.1 118.6 %collective-permute-start.8 = (f32[1,512,512]{1,2,0:T(8,128)}, f32[1,512,512]{1,2,0:T(8,128)}, u32[]{:S(2)}, u32[]{:S(2)}) collective-permute-start(f32[1,512,512]{1,2,0:T(8,128)} %copy.25), channel_id=1, source_target_pairs={{0,1},{1,0},{2,3},{3,2},{4,5},{5,4},{6,7},{7,6},{8,9},{9,8},{10,11... | collective-permute-start | bytes 3145736 | tf_op jit(solution)/shard_map/ppermute | solution.py:23
  221.9 20.5 %collective-permute-start.15 = (f32[384,512]{1,0:T(8,128)}, f32[384,512]{1,0:T(8,128)S(1)}, u32[]{:S(2)}, u32[]{:S(2)}) collective-permute-start(f32[384,512]{1,0:T(8,128)} %get-tuple-element.39), channel_id=1, source_target_pairs={{0,32},{32,64},{64,96},{96,0},{1,33},{33,65},{65,97},{97,1},{2,34}... | collective-permute-start | bytes 2359304 | tf_op jit(solution)/shard_map/ppermute | solution.py:67
  223.8 22.2 %collective-permute-start.16 = (f32[384,512]{1,0:T(8,128)}, f32[384,512]{1,0:T(8,128)S(1)}, u32[]{:S(2)}, u32[]{:S(2)}) collective-permute-start(f32[384,512]{1,0:T(8,128)} %get-tuple-element.41), channel_id=1, source_target_pairs={{0,64},{32,96},{64,0},{96,32},{1,65},{33,97},{65,1},{97,33},{2,66}... | collective-permute-start | bytes 2359304 | tf_op jit(solution)/shard_map/ppermute | solution.py:67
  225.0 37.4 %collective-permute-start.17 = (f32[384,512]{1,0:T(8,128)}, f32[384,512]{1,0:T(8,128)}, u32[]{:S(2)}, u32[]{:S(2)}) collective-permute-start(f32[384,512]{1,0:T(8,128)} %get-tuple-element.40), channel_id=1, source_target_pairs={{0,96},{32,0},{64,32},{96,64},{1,97},{33,1},{65,33},{97,65},{2,98}... | collective-permute-start | bytes 2359304 | tf_op jit(solution)/shard_map/ppermute | solution.py:67
  265.8 20.7 %collective-permute-start.18 = (f32[96,512]{1,0:T(8,128)}, f32[96,512]{1,0:T(8,128)S(1)}, u32[]{:S(2)}, u32[]{:S(2)}) collective-permute-start(f32[96,512]{1,0:T(8,128)} %get-tuple-element.46), channel_id=1, source_target_pairs={{0,4},{4,8},{8,12},{12,0},{1,5},{5,9},{9,13},{13,1},{2,6},{6,10},{... | collective-permute-start | bytes 589832 | tf_op jit(solution)/shard_map/ppermute | solution.py:67
  267.3 19.3 %collective-permute-start.19 = (f32[96,512]{1,0:T(8,128)}, f32[96,512]{1,0:T(8,128)}, u32[]{:S(2)}, u32[]{:S(2)}) collective-permute-start(f32[96,512]{1,0:T(8,128)} %get-tuple-element.48), channel_id=1, source_target_pairs={{0,8},{4,12},{8,0},{12,4},{1,9},{5,13},{9,1},{13,5},{2,10},{6,14},... | collective-permute-start | bytes 589832 | tf_op jit(solution)/shard_map/ppermute | solution.py:67
  296.9 120.8 %collective-permute-start.10 = (f32[2,512,512]{2,1,0:T(8,128)}, f32[2,512,512]{2,1,0:T(8,128)}, u32[]{:S(2)}, u32[]{:S(2)}) collective-permute-start(f32[2,512,512]{2,1,0:T(8,128)} %get-tuple-element.36), channel_id=1, source_target_pairs={{0,1},{1,2},{2,3},{3,4},{4,5},{5,6},{6,7},{7,8},{8,9},{9,10},{10,1... | collective-permute-start | bytes 6291464 | tf_op jit(solution)/shard_map/ppermute | solution.py:140
  299.7 47.0 %collective-permute-start.24 = (f32[24,512]{1,0:T(8,128)S(1)}, f32[24,512]{1,0:T(8,128)S(1)}, u32[]{:S(2)}, u32[]{:S(2)}) collective-permute-start(f32[24,512]{1,0:T(8,128)S(1)} %get-tuple-element.17), channel_id=1, source_target_pairs={{0,1},{1,2},{2,3},{3,0},{4,5},{5,6},{6,7},{7,4},{8,9},{9,10},{10,1... | collective-permute-start | bytes 147464 | tf_op jit(solution)/shard_map/ppermute | solution.py:78
  302.2 46.1 %collective-permute-start.25 = (f32[24,512]{1,0:T(8,128)S(1)}, f32[24,512]{1,0:T(8,128)S(1)}, u32[]{:S(2)}, u32[]{:S(2)}) collective-permute-start(f32[24,512]{1,0:T(8,128)S(1)} %get-tuple-element.17), channel_id=1, source_target_pairs={{0,2},{1,3},{2,0},{3,1},{4,6},{5,7},{6,4},{7,5},{8,10},{9,11},{10,... | collective-permute-start | bytes 147464 | tf_op jit(solution)/shard_map/ppermute | solution.py:78
  304.0 44.4 %collective-permute-start.26 = (f32[24,512]{1,0:T(8,128)S(1)}, f32[24,512]{1,0:T(8,128)S(1)}, u32[]{:S(2)}, u32[]{:S(2)}) collective-permute-start(f32[24,512]{1,0:T(8,128)S(1)} %get-tuple-element.17), channel_id=1, source_target_pairs={{0,3},{1,0},{2,1},{3,2},{4,7},{5,4},{6,5},{7,6},{8,11},{9,8},{10,9... | collective-permute-start | bytes 147464 | tf_op jit(solution)/shard_map/ppermute | solution.py:78
  349.7 93.9 %collective-permute-start.11 = (f32[2,512,512]{2,1,0:T(8,128)}, f32[2,512,512]{2,1,0:T(8,128)}, u32[]{:S(2)}, u32[]{:S(2)}) collective-permute-start(f32[2,512,512]{2,1,0:T(8,128)} %get-tuple-element.37), channel_id=1, source_target_pairs={{0,2},{2,4},{4,6},{6,8},{8,10},{10,12},{12,14},{16,18},{18,20},{20... | collective-permute-start | bytes 6291464 | tf_op jit(solution)/shard_map/ppermute | solution.py:140
  353.7 101.1 %collective-permute-start.12 = (f32[2,512,512]{2,1,0:T(8,128)}, f32[2,512,512]{2,1,0:T(8,128)}, u32[]{:S(2)}, u32[]{:S(2)}) collective-permute-start(f32[2,512,512]{2,1,0:T(8,128)} %get-tuple-element.35), channel_id=1, source_target_pairs={{1,0},{3,2},{5,4},{7,6},{9,8},{11,10},{13,12},{15,14},{17,16},{19,... | collective-permute-start | bytes 6291464 | tf_op jit(solution)/shard_map/ppermute | solution.py:140
  355.0 49.3 %collective-permute-start.28 = (f32[96,512]{1,0:T(8,128)S(1)}, f32[96,512]{1,0:T(8,128)S(1)}, u32[]{:S(2)}, u32[]{:S(2)}) collective-permute-start(f32[96,512]{1,0:T(8,128)S(1)} %bitcast.183), channel_id=1, source_target_pairs={{0,8},{4,12},{8,0},{12,4},{1,9},{5,13},{9,1},{13,5},{2,10},{6,14},... | collective-permute-start | bytes 589832 | tf_op jit(solution)/shard_map/ppermute | solution.py:78
  358.7 46.2 %collective-permute-start.29 = (f32[96,512]{1,0:T(8,128)S(1)}, f32[96,512]{1,0:T(8,128)S(1)}, u32[]{:S(2)}, u32[]{:S(2)}) collective-permute-start(f32[96,512]{1,0:T(8,128)S(1)} %bitcast.185), channel_id=1, source_target_pairs={{0,12},{4,0},{8,4},{12,8},{1,13},{5,1},{9,5},{13,9},{2,14},{6,2},{... | collective-permute-start | bytes 589832 | tf_op jit(solution)/shard_map/ppermute | solution.py:78
  405.6 26.1 %collective-permute-start.30 = (f32[384,512]{1,0:T(8,128)}, f32[384,512]{1,0:T(8,128)}, u32[]{:S(2)}, u32[]{:S(2)}) collective-permute-start(f32[384,512]{1,0:T(8,128)} %bitcast.51), channel_id=1, source_target_pairs={{0,32},{32,64},{64,96},{96,0},{1,33},{33,65},{65,97},{97,1},{2,34}... | collective-permute-start | bytes 2359304 | tf_op jit(solution)/shard_map/ppermute | solution.py:78
  405.6 27.3 %collective-permute-start.31 = (f32[384,512]{1,0:T(8,128)}, f32[384,512]{1,0:T(8,128)}, u32[]{:S(2)}, u32[]{:S(2)}) collective-permute-start(f32[384,512]{1,0:T(8,128)} %bitcast.51), channel_id=1, source_target_pairs={{0,64},{32,96},{64,0},{96,32},{1,65},{33,97},{65,1},{97,33},{2,66}... | collective-permute-start | bytes 2359304 | tf_op jit(solution)/shard_map/ppermute | solution.py:78
  417.7 24.6 %collective-permute-start.32 = (f32[384,512]{1,0:T(8,128)}, f32[384,512]{1,0:T(8,128)}, u32[]{:S(2)}, u32[]{:S(2)}) collective-permute-start(f32[384,512]{1,0:T(8,128)} %bitcast.51), channel_id=1, source_target_pairs={{0,96},{32,0},{64,32},{96,64},{1,97},{33,1},{65,33},{97,65},{2,98}... | collective-permute-start | bytes 2359304 | tf_op jit(solution)/shard_map/ppermute | solution.py:78
  443.5 58.3 %collective-permute-start.33 = (f32[1536,512]{1,0:T(8,128)S(1)}, f32[1536,512]{1,0:T(8,128)}, u32[]{:S(2)}, u32[]{:S(2)}) collective-permute-start(f32[1536,512]{1,0:T(8,128)S(1)} %bitcast.171), channel_id=1, source_target_pairs={{0,16},{16,0},{1,17},{17,1},{2,18},{18,2},{3,19},{19,3},{4,20},{20... | collective-permute-start | bytes 9437192 | tf_op jit(solution)/shard_map/ppermute | solution.py:78
  469.0 27.7 %collective-permute-start.13 = (f32[2,512,512]{2,1,0:T(8,128)}, f32[2,512,512]{2,1,0:T(8,128)}, u32[]{:S(2)}, u32[]{:S(2)}) collective-permute-start(f32[2,512,512]{2,1,0:T(8,128)} %slice.180), channel_id=1, source_target_pairs={{0,16},{16,32},{32,48},{48,64},{64,80},{80,96},{96,112},{1,17},{17... | collective-permute-start | bytes 6291464 | tf_op jit(solution)/shard_map/ppermute | solution.py:17
  (29 other events, 374.2 us)

commit v3 on v2

--- a/solution.py
+++ b/solution.py
@@ -185,8 +185,8 @@
 
     probe_grad = all_sum(probe_term, ("ty_1", "ty_0", "tx_0", "tx_1"), 1.0 / math.sqrt(slots * devices_all))
 
-    placed = lax.dynamic_update_slice(
-        jnp.zeros((2, width, 2 * width), jnp.float32), grad_term, (anchor, anchor, col_at)
+    placed = lax.dynamic_slice(
+        jnp.pad(grad_term, ((0, 0), (0, 0), (width, width))), (anchor, anchor, width - col_at), (2, width, 2 * width)
     )
     grad_left = placed[:, :, :width]
     grad_right = placed[:, :, width:]
@@ -199,15 +199,15 @@
     got_left2 = shifted(send_right2, TX, [(s, s + 2) for s in evens])
     got_right = shifted(send_left, TX, [(s, s - 1) for s in odds])
 
-    def add_strip(total, piece, at):
-        current = lax.dynamic_slice(total, (anchor, at, anchor), (2, width, width))
-        return lax.dynamic_update_slice(total, current + piece, (anchor, at, anchor))
-
-    grad_column = jnp.zeros(column.shape, jnp.float32)
-    grad_column = add_strip(grad_column, keep, row_at)
-    grad_column = add_strip(grad_column, got_left, row_left)
-    grad_column = add_strip(grad_column, got_left2, row_left2)
-    grad_column = add_strip(grad_column, got_right, row_right)
+    rows_all = column.shape[1]
+
+    def spread(piece, at):
+        padded = jnp.pad(piece, ((0, 0), (rows_all, rows_all), (0, 0)))
+        return lax.dynamic_slice(padded, (anchor, rows_all - at, anchor), (2, rows_all, width))
+
+    grad_column = (
+        (spread(keep, row_at) + spread(got_left, row_left)) + spread(got_left2, row_left2)
+    ) + spread(got_right, row_right)
     from_above = passed_along(grad_column[:, tile_h:, :], TY, 1)
     core_grad = grad_column[:, :tile_h, :].at[:, :width, :].add(from_above)
     return (core_grad, probe_grad)

time: 514 us -> 490 us (0.953)
  local copies, waits for them, and re-layouts: 93.2 us -> 44.8 us
  waiting for transfers between devices: 237 us -> 266 us
    dynamic_update_slice x5 -> x0, local copies, waits for them, and re-layouts: 39.1 us -> none  [the longest x4 27.9 us: add_strip(): lax.dynamic_update_slice(total, current + piece, (anchor, at, anchor))]
    ppermute x10, waiting for transfers between devices: 93.1 us -> 107 us  [gather_axis(): got = lax.ppermute(piece, axis, pairs)]
    ppermute x10, waiting for transfers between devices: 40.8 us -> 52.4 us  [scatter_axis(): total = total + lax.ppermute(sent, axis, pairs)]
    add x3 -> x1, other arithmetic: 10.8 us -> 8.46 us  [local(): spread(keep, row_at) + spread(got_left, row_left) + spread(got_left2, row...]
    unnamed x41 -> x47, local copies, waits for them, and re-layouts: 15.4 us -> 16.1 us
  transfers between devices with their start and end apart: 34 -> 34, of which waited for: 11 -> 15; matrix products, arithmetic and copies ran while one was open for 24% -> 14% of each run, Pallas kernels for 0% -> 0%
where the time goes in v3:
time: 490 us; the launch traced here: 485 us
  waiting for transfers between devices  266 us (54%)
  starting transfers between devices  67.1 us (14%)
  other arithmetic  46.7 us (10%)
  matrix products  45.8 us (9%)
  local copies, waits for them, and re-layouts  44.8 us (9%)
  between operations  15 us (3%)
    ppermute x10, waiting for transfers between devices, gather_axis(): got = lax.ppermute(piece, axis, pairs)  107 us
    ppermute x3, waiting for transfers between devices, partner(): return lax.ppermute(value, axis, pairs)  79.8 us
    ppermute x10, waiting for transfers between devices, scatter_axis(): total = total + lax.ppermute(sent, axis, pairs)  52.4 us
    ppermute x9, starting transfers between devices, shifted(): lax.ppermute(value, axis, [(a, b) for a, b in pairs if 0 <= b < lax.axis_...  29.8 us
    ppermute x2, waiting for transfers between devices, passed_along(): lax.ppermute(value, axis, [(source, source + steps) for source in range(i...  25.2 us
    unnamed x47, local copies, waits for them, and re-layouts  16.1 us
    ppermute x10, starting transfers between devices, gather_axis(): got = lax.ppermute(piece, axis, pairs)  14.8 us
    ppermute x10, starting transfers between devices, scatter_axis(): total = total + lax.ppermute(sent, axis, pairs)  14.6 us
  transfers between devices with their start and end apart: 34, of which 15 were waited for; matrix products, arithmetic and copies ran while one was open for 14% of the time, Pallas kernels for 0%

profile of v3, /device:TPU:48, one launch (start us, length us, event | category | flops | bytes accessed | tf_op | source)
XLA Modules:
  0.0 485.2 jit_solution(8811184149647699726)
XLA Ops:
  8.9 4.6 constant_dynamic-update-slice_fusion.1
  18.8 5.2 %collective-permute-start.4 = (s32[]{:T(128)}, s32[]{:T(128)}, u32[]{:S(2)}, u32[]{:S(2)}) collective-permute-start(s32[]{:T(128)} %select_n.300), channel_id=1, source_target_pairs={{0,1},{1,2},{2,3},{3,4},{4,5},{5,6},{6,7},{7,8},{8,9},{9,10},{10,1... | collective-permute-start | bytes 20 | tf_op jit(solution)/shard_map/ppermute | solution.py:140
  24.0 4.9 %collective-permute-start.6 = (s32[]{:T(128)}, s32[]{:T(128)}, u32[]{:S(2)}, u32[]{:S(2)}) collective-permute-start(s32[]{:T(128)} %select_n.300), channel_id=1, source_target_pairs={{0,2},{2,4},{4,6},{6,8},{8,10},{10,12},{12,14},{16,18},{18,20},{20... | collective-permute-start | bytes 20 | tf_op jit(solution)/shard_map/ppermute | solution.py:140
  36.1 6.0 %constant_dynamic-slice_fusion = (f32[2,512,512]{2,1,0:T(8,128)}, f32[2,512,512]{2,1,0:T(8,128)}, f32[2,512,512]{2,1,0:T(8,128)}) fusion(f32[2,1536,512]{2,1,0:T(8,128)} %constant_dynamic-update-slice_fusion, s32[]{:T(128)S(6)} %select_n.307, s32[]{:T(128)S(6)} %select_n.304, s32[]{:T(128)S(6)} %select_n.303), kind=kLoop, calls=%fused_computation.146 | loop fusion | bytes 12582924 | tf_op jit(solution)/shard_map/dynamic_slice | solution.py:173
  54.9 79.8 %collective-permute-done.9 = f32[]{:T(128)} collective-permute-done((f32[]{:T(128)}, f32[]{:T(128)}, u32[]{:S(2)}, u32[]{:S(2)}) %collective-permute-start.9) | collective-permute-done | bytes 36 | tf_op jit(solution)/shard_map/ppermute | solution.py:23
  144.9 5.4 %convolution_bitcast_fusion.1 = f32[3,512,1024]{2,1,0:T(8,128)S(1)} fusion(bf16[3,512,512]{2,1,0:T(8,128)(2,1)S(1)} %get-tuple-element.28, bf16[3,512,512]{2,1,0:T(8,128)(2,1)S(1)} %get-tuple-element.27), kind=kOutput, calls=%fused_computation.73 | convolution fusion | flops 1621098496 | bytes 9437184 | tf_op jit(solution)/shard_map/ij,mjk->mik/dot_general | solution.py:107
  150.3 5.7 %convolution_bitcast_fusion = f32[3,512,1024]{2,1,0:T(8,128)S(1)} fusion(bf16[3,512,512]{2,1,0:T(8,128)(2,1)S(1)} %get-tuple-element.28, bf16[3,512,512]{2,1,0:T(8,128)(2,1)S(1)} %get-tuple-element.27), kind=kOutput, calls=%fused_computation.72 | convolution fusion | flops 1621098496 | bytes 9437184 | tf_op jit(solution)/shard_map/ij,mjk->mik/dot_general | solution.py:108
  157.8 5.5 %fusion.37 = f32[3,1024,512]{1,2,0:T(8,128)S(1)} fusion(bf16[3,512,512]{2,1,0:T(8,128)(2,1)S(1)} %get-tuple-element.26, bf16[3,512,512]{2,1,0:T(8,128)(2,1)S(1)} %get-tuple-element.25), kind=kOutput, calls=%fused_computation.86 | convolution fusion | flops 1621098496 | bytes 9437184 | tf_op jit(solution)/shard_map/mij,jk->mik/dot_general | solution.py:112
  163.3 5.9 %fusion.36 = f32[3,1024,512]{1,2,0:T(8,128)S(1)} fusion(bf16[3,512,512]{2,1,0:T(8,128)(2,1)S(1)} %get-tuple-element.26, bf16[3,512,512]{2,1,0:T(8,128)(2,1)S(1)} %get-tuple-element.25), kind=kOutput, calls=%fused_computation.85 | convolution fusion | flops 1621098496 | bytes 9437184 | tf_op jit(solution)/shard_map/mij,jk->mik/dot_general | solution.py:113
  173.2 5.6 %convolution_bitcast_fusion.3 = f32[3,512,1024]{2,1,0:T(8,128)S(1)} fusion(bf16[3,512,512]{1,2,0:T(8,128)(2,1)S(1)} %get-tuple-element.22, bf16[3,512,512]{1,2,0:T(8,128)(2,1)S(1)} %get-tuple-element.21), kind=kOutput, calls=%fused_computation.75 | convolution fusion | flops 1621098496 | bytes 9437184 | tf_op jit(solution)/shard_map/ij,mjk->mik/dot_general | solution.py:107
  178.8 5.5 %convolution_bitcast_fusion.2 = f32[3,512,1024]{2,1,0:T(8,128)S(1)} fusion(bf16[3,512,512]{1,2,0:T(8,128)(2,1)S(1)} %get-tuple-element.22, bf16[3,512,512]{1,2,0:T(8,128)(2,1)S(1)} %get-tuple-element.21), kind=kOutput, calls=%fused_computation.74 | convolution fusion | flops 1621098496 | bytes 9437184 | tf_op jit(solution)/shard_map/ij,mjk->mik/dot_general | solution.py:108
  187.7 5.0 %fusion.35 = f32[3,1024,512]{2,1,0:T(8,128)S(1)} fusion(bf16[3,512,512]{2,1,0:T(8,128)(2,1)S(1)} %get-tuple-element.24, bf16[3,512,512]{2,1,0:T(8,128)(2,1)S(1)} %get-tuple-element.23), kind=kOutput, calls=%fused_computation.84 | convolution fusion | flops 1621098496 | bytes 9437184 | tf_op jit(solution)/shard_map/mij,jk->mik/dot_general | solution.py:112
  192.7 7.3 %fusion.34 = f32[3,1024,512]{2,1,0:T(8,128)S(1)} fusion(bf16[3,512,512]{2,1,0:T(8,128)(2,1)} %copy-done.14, bf16[3,512,512]{2,1,0:T(8,128)(2,1)} %copy-done.13), kind=kOutput, calls=%fused_computation.83 | convolution fusion | flops 1621098496 | bytes 9437184 | tf_op jit(solution)/shard_map/mij,jk->mik/dot_general | solution.py:113
  202.2 4.9 %fusion.31 = (f32[512,512]{1,0:T(8,128)}, f32[512,512]{1,0:T(8,128)}, f32[3,512,512]{2,1,0:T(8,128)S(1)}) fusion(f32[3,512,512]{2,1,0:T(8,128)S(1)} %get-tuple-element.20, f32[3,512,512]{2,1,0:T(8,128)S(1)} %get-tuple-element.19, f32[2,3,512,512]{3,2,1,0:T(8,128)S(1)} %bitcast.170, f32[512,512]{1,0:T(8,128)S(1)} %copy-done.5, f32[512,512]{1,0:T(8,128)} %copy-done.3), kind=kLoop, calls=%fused_computation.62 | loop fusion | flops 8126464 | bytes 19922944 | tf_op jit(solution)/shard_map/reduce_sum | solution.py:133
  209.6 6.0 %collective-permute-done.14 = f32[1536,512]{1,0:T(8,128)} collective-permute-done((f32[1536,512]{1,0:T(8,128)}, f32[1536,512]{1,0:T(8,128)}, u32[]{:S(2)}, u32[]{:S(2)}) %collective-permute-start.14) | collective-permute-done | bytes 3145760 | tf_op jit(solution)/shard_map/ppermute | solution.py:67
  227.4 14.9 %collective-permute-done.15 = f32[384,512]{1,0:T(8,128)S(1)} collective-permute-done((f32[384,512]{1,0:T(8,128)}, f32[384,512]{1,0:T(8,128)S(1)}, u32[]{:S(2)}, u32[]{:S(2)}) %collective-permute-start.15) | collective-permute-done | bytes 786464 | tf_op jit(solution)/shard_map/ppermute | solution.py:67
  246.0 16.2 %collective-permute-done.17 = f32[384,512]{1,0:T(8,128)} collective-permute-done((f32[384,512]{1,0:T(8,128)}, f32[384,512]{1,0:T(8,128)}, u32[]{:S(2)}, u32[]{:S(2)}) %collective-permute-start.17) | collective-permute-done | bytes 786464 | tf_op jit(solution)/shard_map/ppermute | solution.py:67
  270.9 6.7 %collective-permute-done.18 = f32[96,512]{1,0:T(8,128)S(1)} collective-permute-done((f32[96,512]{1,0:T(8,128)}, f32[96,512]{1,0:T(8,128)S(1)}, u32[]{:S(2)}, u32[]{:S(2)}) %collective-permute-start.18) | collective-permute-done | bytes 196640 | tf_op jit(solution)/shard_map/ppermute | solution.py:67
  305.2 4.2 collective-permute-start.11
  316.0 72.9 %collective-permute-done.28 = f32[96,512]{1,0:T(8,128)S(1)} collective-permute-done((f32[96,512]{1,0:T(8,128)S(1)}, f32[96,512]{1,0:T(8,128)S(1)}, u32[]{:S(2)}, u32[]{:S(2)}) %collective-permute-start.28) | collective-permute-done | bytes 196640 | tf_op jit(solution)/shard_map/ppermute | solution.py:78
  393.3 17.7 %collective-permute-done.30 = f32[384,512]{1,0:T(8,128)} collective-permute-done((f32[384,512]{1,0:T(8,128)}, f32[384,512]{1,0:T(8,128)}, u32[]{:S(2)}, u32[]{:S(2)}) %collective-permute-start.30) | collective-permute-done | bytes 786464 | tf_op jit(solution)/shard_map/ppermute | solution.py:78
  421.0 13.0 %collective-permute-done.32 = f32[384,512]{1,0:T(8,128)} collective-permute-done((f32[384,512]{1,0:T(8,128)}, f32[384,512]{1,0:T(8,128)}, u32[]{:S(2)}, u32[]{:S(2)}) %collective-permute-start.32) | collective-permute-done | bytes 786464 | tf_op jit(solution)/shard_map/ppermute | solution.py:78
  435.5 8.5 %fusion.2 = f32[2,1536,512]{2,1,0:T(8,128)S(1)} fusion(s32[]{:T(128)S(6)} %select_n.319, f32[2,512,512]{2,1,0:T(8,128)S(1)} %copy-done.7, s32[]{:T(128)S(6)} %select_n.323, f32[2,512,512]{2,1,0:T(8,128)} %collective-permute-done.10, s32[]{:T(128)S(6)} %select_n.325, f32[2,512,512]{2,1,0:T(8,128)} %collective-permute-done.11, s32[]{:T(128)S(6)} %select_n.327, ...), kind=kLoop, calls=%fused_computation.10 | loop fusion | flops 4718592 | bytes 14680080 | tf_op jit(solution)/shard_map/add | solution.py:208
  450.6 25.2 %collective-permute-done.13 = f32[2,512,512]{2,1,0:T(8,128)} collective-permute-done((f32[2,512,512]{2,1,0:T(8,128)}, f32[2,512,512]{2,1,0:T(8,128)}, u32[]{:S(2)}, u32[]{:S(2)}) %collective-permute-start.13) | collective-permute-done | bytes 2097184 | tf_op jit(solution)/shard_map/ppermute | solution.py:17
  (153 shorter events, 133.5 us)
Async XLA Ops:
  3.7 30.9 %collective-permute-start = (f32[2,512,512]{2,1,0:T(8,128)}, f32[2,512,512]{2,1,0:T(8,128)S(1)}, u32[]{:S(2)}, u32[]{:S(2)}) collective-permute-start(f32[2,512,512]{2,1,0:T(8,128)} %slice.125), channel_id=1, source_target_pairs={{16,0},{32,16},{48,32},{64,48},{80,64},{96,80},{112,96},{17,1},{33... | collective-permute-start | bytes 6291464 | tf_op jit(solution)/shard_map/ppermute | solution.py:17
  15.6 13.3 %collective-permute-start.2 = (s32[]{:T(128)}, s32[]{:T(128)}, u32[]{:S(2)}, u32[]{:S(2)}) collective-permute-start(s32[]{:T(128)} %select_n.300), channel_id=1, source_target_pairs={{1,0},{2,1},{3,2},{4,3},{5,4},{6,5},{7,6},{8,7},{9,8},{10,9},{11,1... | collective-permute-start | bytes 20 | tf_op jit(solution)/shard_map/ppermute | solution.py:140
  18.8 11.3 %collective-permute-start.4 = (s32[]{:T(128)}, s32[]{:T(128)}, u32[]{:S(2)}, u32[]{:S(2)}) collective-permute-start(s32[]{:T(128)} %select_n.300), channel_id=1, source_target_pairs={{0,1},{1,2},{2,3},{3,4},{4,5},{5,6},{6,7},{7,8},{8,9},{9,10},{10,1... | collective-permute-start | bytes 20 | tf_op jit(solution)/shard_map/ppermute | solution.py:140
  42.2 94.6 %collective-permute-start.3 = (f32[2,512,512]{2,1,0:T(8,128)}, f32[2,512,512]{2,1,0:T(8,128)}, u32[]{:S(2)}, u32[]{:S(2)}) collective-permute-start(f32[2,512,512]{2,1,0:T(8,128)} %get-tuple-element.34), channel_id=1, source_target_pairs={{0,1},{2,3},{4,5},{6,7},{8,9},{10,11},{12,13},{14,15},{16,17},{18,... | collective-permute-start | bytes 6291464 | tf_op jit(solution)/shard_map/ppermute | solution.py:140
  44.7 92.0 %collective-permute-start.5 = (f32[2,512,512]{2,1,0:T(8,128)}, f32[2,512,512]{2,1,0:T(8,128)}, u32[]{:S(2)}, u32[]{:S(2)}) collective-permute-start(f32[2,512,512]{2,1,0:T(8,128)} %get-tuple-element.33), channel_id=1, source_target_pairs={{1,0},{2,1},{3,2},{4,3},{5,4},{6,5},{7,6},{8,7},{9,8},{10,9},{11,1... | collective-permute-start | bytes 6291464 | tf_op jit(solution)/shard_map/ppermute | solution.py:140
  46.7 91.7 %collective-permute-start.7 = (f32[2,512,512]{2,1,0:T(8,128)}, f32[2,512,512]{2,1,0:T(8,128)}, u32[]{:S(2)}, u32[]{:S(2)}) collective-permute-start(f32[2,512,512]{2,1,0:T(8,128)} %get-tuple-element.32), channel_id=1, source_target_pairs={{2,0},{4,2},{6,4},{8,6},{10,8},{12,10},{14,12},{18,16},{20,18},{22... | collective-permute-start | bytes 6291464 | tf_op jit(solution)/shard_map/ppermute | solution.py:140
  49.8 84.9 %collective-permute-start.9 = (f32[]{:T(128)}, f32[]{:T(128)}, u32[]{:S(2)}, u32[]{:S(2)}) collective-permute-start(f32[]{:T(128)} %convert_reduce_fusion), channel_id=1, source_target_pairs={{0,1},{1,0},{2,3},{3,2},{4,5},{5,4},{6,7},{7,6},{8,9},{9,8},{10,11... | collective-permute-start | bytes 20 | tf_op jit(solution)/shard_map/ppermute | solution.py:23
  52.3 118.6 %collective-permute-start.8 = (f32[1,512,512]{1,2,0:T(8,128)}, f32[1,512,512]{1,2,0:T(8,128)}, u32[]{:S(2)}, u32[]{:S(2)}) collective-permute-start(f32[1,512,512]{1,2,0:T(8,128)} %copy.25), channel_id=1, source_target_pairs={{0,1},{1,0},{2,3},{3,2},{4,5},{5,4},{6,7},{7,6},{8,9},{9,8},{10,11... | collective-permute-start | bytes 3145736 | tf_op jit(solution)/shard_map/ppermute | solution.py:23
  221.8 20.5 %collective-permute-start.15 = (f32[384,512]{1,0:T(8,128)}, f32[384,512]{1,0:T(8,128)S(1)}, u32[]{:S(2)}, u32[]{:S(2)}) collective-permute-start(f32[384,512]{1,0:T(8,128)} %get-tuple-element.39), channel_id=1, source_target_pairs={{0,32},{32,64},{64,96},{96,0},{1,33},{33,65},{65,97},{97,1},{2,34}... | collective-permute-start | bytes 2359304 | tf_op jit(solution)/shard_map/ppermute | solution.py:67
  223.7 22.3 %collective-permute-start.16 = (f32[384,512]{1,0:T(8,128)}, f32[384,512]{1,0:T(8,128)}, u32[]{:S(2)}, u32[]{:S(2)}) collective-permute-start(f32[384,512]{1,0:T(8,128)} %get-tuple-element.41), channel_id=1, source_target_pairs={{0,64},{32,96},{64,0},{96,32},{1,65},{33,97},{65,1},{97,33},{2,66}... | collective-permute-start | bytes 2359304 | tf_op jit(solution)/shard_map/ppermute | solution.py:67
  224.8 37.4 %collective-permute-start.17 = (f32[384,512]{1,0:T(8,128)}, f32[384,512]{1,0:T(8,128)}, u32[]{:S(2)}, u32[]{:S(2)}) collective-permute-start(f32[384,512]{1,0:T(8,128)} %get-tuple-element.40), channel_id=1, source_target_pairs={{0,96},{32,0},{64,32},{96,64},{1,97},{33,1},{65,33},{97,65},{2,98}... | collective-permute-start | bytes 2359304 | tf_op jit(solution)/shard_map/ppermute | solution.py:67
  265.1 12.4 %collective-permute-start.18 = (f32[96,512]{1,0:T(8,128)}, f32[96,512]{1,0:T(8,128)S(1)}, u32[]{:S(2)}, u32[]{:S(2)}) collective-permute-start(f32[96,512]{1,0:T(8,128)} %get-tuple-element.46), channel_id=1, source_target_pairs={{0,4},{4,8},{8,12},{12,0},{1,5},{5,9},{9,13},{13,1},{2,6},{6,10},{... | collective-permute-start | bytes 589832 | tf_op jit(solution)/shard_map/ppermute | solution.py:67
  266.6 10.9 %collective-permute-start.19 = (f32[96,512]{1,0:T(8,128)S(1)}, f32[96,512]{1,0:T(8,128)}, u32[]{:S(2)}, u32[]{:S(2)}) collective-permute-start(f32[96,512]{1,0:T(8,128)S(1)} %get-tuple-element.48), channel_id=1, source_target_pairs={{0,8},{4,12},{8,0},{12,4},{1,9},{5,13},{9,1},{13,5},{2,10},{6,14},... | collective-permute-start | bytes 589832 | tf_op jit(solution)/shard_map/ppermute | solution.py:67
  296.0 17.5 %collective-permute-start.27 = (f32[96,512]{1,0:T(8,128)S(1)}, f32[96,512]{1,0:T(8,128)S(1)}, u32[]{:S(2)}, u32[]{:S(2)}) collective-permute-start(f32[96,512]{1,0:T(8,128)S(1)} %bitcast.182), channel_id=1, source_target_pairs={{0,4},{4,8},{8,12},{12,0},{1,5},{5,9},{9,13},{13,1},{2,6},{6,10},{... | collective-permute-start | bytes 589832 | tf_op jit(solution)/shard_map/ppermute | solution.py:78
  301.8 133.7 %collective-permute-start.10 = (f32[2,512,512]{2,1,0:T(8,128)}, f32[2,512,512]{2,1,0:T(8,128)}, u32[]{:S(2)}, u32[]{:S(2)}) collective-permute-start(f32[2,512,512]{2,1,0:T(8,128)} %get-tuple-element.36), channel_id=1, source_target_pairs={{0,1},{1,2},{2,3},{3,4},{4,5},{5,6},{6,7},{7,8},{8,9},{9,10},{10,1... | collective-permute-start | bytes 6291464 | tf_op jit(solution)/shard_map/ppermute | solution.py:140
  305.2 130.3 %collective-permute-start.11 = (f32[2,512,512]{2,1,0:T(8,128)}, f32[2,512,512]{2,1,0:T(8,128)}, u32[]{:S(2)}, u32[]{:S(2)}) collective-permute-start(f32[2,512,512]{2,1,0:T(8,128)} %get-tuple-element.37), channel_id=1, source_target_pairs={{0,2},{2,4},{4,6},{6,8},{8,10},{10,12},{12,14},{16,18},{18,20},{20... | collective-permute-start | bytes 6291464 | tf_op jit(solution)/shard_map/ppermute | solution.py:140
  309.4 126.1 %collective-permute-start.12 = (f32[2,512,512]{2,1,0:T(8,128)}, f32[2,512,512]{2,1,0:T(8,128)}, u32[]{:S(2)}, u32[]{:S(2)}) collective-permute-start(f32[2,512,512]{2,1,0:T(8,128)} %get-tuple-element.35), channel_id=1, source_target_pairs={{1,0},{3,2},{5,4},{7,6},{9,8},{11,10},{13,12},{15,14},{17,16},{19,... | collective-permute-start | bytes 6291464 | tf_op jit(solution)/shard_map/ppermute | solution.py:140
  310.7 78.2 %collective-permute-start.28 = (f32[96,512]{1,0:T(8,128)S(1)}, f32[96,512]{1,0:T(8,128)S(1)}, u32[]{:S(2)}, u32[]{:S(2)}) collective-permute-start(f32[96,512]{1,0:T(8,128)S(1)} %bitcast.183), channel_id=1, source_target_pairs={{0,8},{4,12},{8,0},{12,4},{1,9},{5,13},{9,1},{13,5},{2,10},{6,14},... | collective-permute-start | bytes 589832 | tf_op jit(solution)/shard_map/ppermute | solution.py:78
  313.4 76.2 %collective-permute-start.29 = (f32[96,512]{1,0:T(8,128)S(1)}, f32[96,512]{1,0:T(8,128)S(1)}, u32[]{:S(2)}, u32[]{:S(2)}) collective-permute-start(f32[96,512]{1,0:T(8,128)S(1)} %bitcast.185), channel_id=1, source_target_pairs={{0,12},{4,0},{8,4},{12,8},{1,13},{5,1},{9,5},{13,9},{2,14},{6,2},{... | collective-permute-start | bytes 589832 | tf_op jit(solution)/shard_map/ppermute | solution.py:78
  390.3 20.7 %collective-permute-start.30 = (f32[384,512]{1,0:T(8,128)}, f32[384,512]{1,0:T(8,128)}, u32[]{:S(2)}, u32[]{:S(2)}) collective-permute-start(f32[384,512]{1,0:T(8,128)} %bitcast.51), channel_id=1, source_target_pairs={{0,32},{32,64},{64,96},{96,0},{1,33},{33,65},{65,97},{97,1},{2,34}... | collective-permute-start | bytes 2359304 | tf_op jit(solution)/shard_map/ppermute | solution.py:78
  391.9 27.9 %collective-permute-start.31 = (f32[384,512]{1,0:T(8,128)}, f32[384,512]{1,0:T(8,128)}, u32[]{:S(2)}, u32[]{:S(2)}) collective-permute-start(f32[384,512]{1,0:T(8,128)} %bitcast.51), channel_id=1, source_target_pairs={{0,64},{32,96},{64,0},{96,32},{1,65},{33,97},{65,1},{97,33},{2,66}... | collective-permute-start | bytes 2359304 | tf_op jit(solution)/shard_map/ppermute | solution.py:78
  411.0 23.0 %collective-permute-start.32 = (f32[384,512]{1,0:T(8,128)}, f32[384,512]{1,0:T(8,128)}, u32[]{:S(2)}, u32[]{:S(2)}) collective-permute-start(f32[384,512]{1,0:T(8,128)} %bitcast.51), channel_id=1, source_target_pairs={{0,96},{32,0},{64,32},{96,64},{1,97},{33,1},{65,33},{97,65},{2,98}... | collective-permute-start | bytes 2359304 | tf_op jit(solution)/shard_map/ppermute | solution.py:78
  435.2 44.6 %collective-permute-start.33 = (f32[1536,512]{1,0:T(8,128)S(1)}, f32[1536,512]{1,0:T(8,128)}, u32[]{:S(2)}, u32[]{:S(2)}) collective-permute-start(f32[1536,512]{1,0:T(8,128)S(1)} %bitcast.171), channel_id=1, source_target_pairs={{0,16},{16,0},{1,17},{17,1},{2,18},{18,2},{3,19},{19,3},{4,20},{20... | collective-permute-start | bytes 9437192 | tf_op jit(solution)/shard_map/ppermute | solution.py:78
  448.2 27.7 %collective-permute-start.13 = (f32[2,512,512]{2,1,0:T(8,128)}, f32[2,512,512]{2,1,0:T(8,128)}, u32[]{:S(2)}, u32[]{:S(2)}) collective-permute-start(f32[2,512,512]{2,1,0:T(8,128)} %slice.180), channel_id=1, source_target_pairs={{0,16},{16,32},{32,48},{48,64},{64,80},{80,96},{96,112},{1,17},{17... | collective-permute-start | bytes 6291464 | tf_op jit(solution)/shard_map/ppermute | solution.py:17
  (33 other events, 454.6 us)

commit v4 on v3

--- a/solution.py
+++ b/solution.py
@@ -5,6 +5,7 @@
 from jax import lax
 from jax.sharding import Mesh
 from jax.sharding import PartitionSpec as P
+
 
 TY = ("ty_0", "ty_1")
 TX = ("tx_0", "tx_1")
@@ -21,39 +22,6 @@
     mask = 2**apart
     pairs = [(source, source ^ mask) for source in range(lax.axis_size(axis))]
     return lax.ppermute(value, axis, pairs)
-
-
-def filled_up(lines, devices):
-    spare = -len(lines) % devices
-    return jnp.pad(lines, [(0, spare)] + [(0, 0)] * (lines.ndim - 1))
-
-
-def sum_in_order(parts, axes, sequence):
-    dims = [lax.axis_size(a) for a in axes]
-    parts = parts.reshape(*dims, *parts.shape[1:])
-    parts = parts.transpose(*sequence, *range(len(axes), parts.ndim))
-    parts = parts.reshape(-1, *parts.shape[len(axes) :])
-    for k in sequence:
-        parts = lax.psum_scatter(parts, axes[k], scatter_dimension=0, tiled=True)
-    return parts[0]
-
-
-def gather_in_order(shard, axes, sequence):
-    parts = shard
-    for k in sequence:
-        parts = lax.all_gather(parts, axes[k])
-    done = sequence[::-1]
-    back = [done.index(k) for k in range(len(axes))]
-    parts = parts.transpose(*back, *range(len(axes), parts.ndim))
-    return parts.reshape(-1, *shard.shape)
-
-
-def sum_in_two_steps(shard, axes, sequence):
-    devices, lines = (lax.axis_size(axes), shard.reshape(-1, *shard.shape[1:][-1:]))
-    parts = filled_up(lines, devices).reshape(devices, -1, *lines.shape[1:])
-    own = sum_in_order(parts, axes, sequence)
-    whole = gather_in_order(own, axes, sequence[::-1]).reshape(-1, *lines.shape[1:])
-    return whole[: len(lines)].reshape(shard.shape)
 
 
 def scatter_axis(lines, axis):
@@ -216,6 +184,7 @@
 def solution(mesh):
     finer = Mesh(mesh.devices.reshape(4, 2, 4, 4), ("ty_0", "ty_1", "tx_0", "tx_1"))
     placed = (P(None, TY, TX), P(), P(TY_TX, None, None), P(TY_TX, None), P(TY_TX))
+
     return jax.shard_map(
         local, mesh=finer, in_specs=placed, out_specs=(P(None, TY, TX), P()), check_vma=False
     )

time: 490 us -> 491 us (level)
  the two profiles are of different devices: /device:TPU:48 before, /device:TPU:56 now
where the time goes in v4:
time: 491 us; the launch traced here: 486 us
  waiting for transfers between devices  266 us (54%)
  starting transfers between devices  67.2 us (14%)
  other arithmetic  46.9 us (10%)
  local copies, waits for them, and re-layouts  45.7 us (9%)
  matrix products  45.7 us (9%)
  between operations  15.1 us (3%)
    ppermute x10, waiting for transfers between devices, gather_axis(): got = lax.ppermute(piece, axis, pairs)  107 us
    ppermute x3, waiting for transfers between devices, partner(): return lax.ppermute(value, axis, pairs)  81.1 us
    ppermute x10, waiting for transfers between devices, scatter_axis(): total = total + lax.ppermute(sent, axis, pairs)  52.2 us
    ppermute x9, starting transfers between devices, shifted(): lax.ppermute(value, axis, [(a, b) for a, b in pairs if 0 <= b < lax.axis_...  31.8 us
    ppermute x2, waiting for transfers between devices, passed_along(): lax.ppermute(value, axis, [(source, source + steps) for source in range(i...  25.2 us
    unnamed x47, local copies, waits for them, and re-layouts  17 us
    ppermute x10, starting transfers between devices, scatter_axis(): total = total + lax.ppermute(sent, axis, pairs)  14.6 us
    ppermute x10, starting transfers between devices, gather_axis(): got = lax.ppermute(piece, axis, pairs)  13.1 us
  transfers between devices with their start and end apart: 34, of which 17 were waited for; matrix products, arithmetic and copies ran while one was open for 14% of the time, Pallas kernels for 0%

profile of v4, /device:TPU:56, one launch (start us, length us, event | category | flops | bytes accessed | tf_op | source)
XLA Modules:
  0.0 486.4 jit_solution(8811184149647699726)
XLA Ops:
  8.4 4.6 constant_dynamic-update-slice_fusion.1
  15.0 4.5 collective-permute-start.2
  19.5 6.0 %collective-permute-start.4 = (s32[]{:T(128)}, s32[]{:T(128)}, u32[]{:S(2)}, u32[]{:S(2)}) collective-permute-start(s32[]{:T(128)} %select_n.300), channel_id=1, source_target_pairs={{0,1},{1,2},{2,3},{3,4},{4,5},{5,6},{6,7},{7,8},{8,9},{9,10},{10,1... | collective-permute-start | bytes 20 | tf_op jit(solution)/shard_map/ppermute | solution.py:108
  34.1 6.0 %constant_dynamic-slice_fusion = (f32[2,512,512]{2,1,0:T(8,128)}, f32[2,512,512]{2,1,0:T(8,128)}, f32[2,512,512]{2,1,0:T(8,128)}) fusion(f32[2,1536,512]{2,1,0:T(8,128)} %constant_dynamic-update-slice_fusion, s32[]{:T(128)S(6)} %select_n.307, s32[]{:T(128)S(6)} %select_n.304, s32[]{:T(128)S(6)} %select_n.303), kind=kLoop, calls=%fused_computation.146 | loop fusion | bytes 12582924 | tf_op jit(solution)/shard_map/dynamic_slice | solution.py:141
  41.4 6.1 %collective-permute-start.5 = (f32[2,512,512]{2,1,0:T(8,128)}, f32[2,512,512]{2,1,0:T(8,128)}, u32[]{:S(2)}, u32[]{:S(2)}) collective-permute-start(f32[2,512,512]{2,1,0:T(8,128)} %get-tuple-element.33), channel_id=1, source_target_pairs={{1,0},{2,1},{3,2},{4,3},{5,4},{6,5},{7,6},{8,7},{9,8},{10,9},{11,1... | collective-permute-start | bytes 6291464 | tf_op jit(solution)/shard_map/ppermute | solution.py:108
  55.0 81.1 %collective-permute-done.9 = f32[]{:T(128)} collective-permute-done((f32[]{:T(128)}, f32[]{:T(128)}, u32[]{:S(2)}, u32[]{:S(2)}) %collective-permute-start.9) | collective-permute-done | bytes 36 | tf_op jit(solution)/shard_map/ppermute | solution.py:24
  144.8 5.4 %convolution_bitcast_fusion.1 = f32[3,512,1024]{2,1,0:T(8,128)S(1)} fusion(bf16[3,512,512]{2,1,0:T(8,128)(2,1)S(1)} %get-tuple-element.28, bf16[3,512,512]{2,1,0:T(8,128)(2,1)S(1)} %get-tuple-element.27), kind=kOutput, calls=%fused_computation.73 | convolution fusion | flops 1621098496 | bytes 9437184 | tf_op jit(solution)/shard_map/ij,mjk->mik/dot_general | solution.py:75
  150.2 5.6 %convolution_bitcast_fusion = f32[3,512,1024]{2,1,0:T(8,128)S(1)} fusion(bf16[3,512,512]{2,1,0:T(8,128)(2,1)S(1)} %get-tuple-element.28, bf16[3,512,512]{2,1,0:T(8,128)(2,1)S(1)} %get-tuple-element.27), kind=kOutput, calls=%fused_computation.72 | convolution fusion | flops 1621098496 | bytes 9437184 | tf_op jit(solution)/shard_map/ij,mjk->mik/dot_general | solution.py:76
  157.7 5.5 %fusion.37 = f32[3,1024,512]{1,2,0:T(8,128)S(1)} fusion(bf16[3,512,512]{2,1,0:T(8,128)(2,1)S(1)} %get-tuple-element.26, bf16[3,512,512]{2,1,0:T(8,128)(2,1)S(1)} %get-tuple-element.25), kind=kOutput, calls=%fused_computation.86 | convolution fusion | flops 1621098496 | bytes 9437184 | tf_op jit(solution)/shard_map/mij,jk->mik/dot_general | solution.py:80
  163.1 5.7 %fusion.36 = f32[3,1024,512]{1,2,0:T(8,128)S(1)} fusion(bf16[3,512,512]{2,1,0:T(8,128)(2,1)S(1)} %get-tuple-element.26, bf16[3,512,512]{2,1,0:T(8,128)(2,1)S(1)} %get-tuple-element.25), kind=kOutput, calls=%fused_computation.85 | convolution fusion | flops 1621098496 | bytes 9437184 | tf_op jit(solution)/shard_map/mij,jk->mik/dot_general | solution.py:81
  172.9 5.8 %convolution_bitcast_fusion.3 = f32[3,512,1024]{2,1,0:T(8,128)S(1)} fusion(bf16[3,512,512]{1,2,0:T(8,128)(2,1)S(1)} %get-tuple-element.22, bf16[3,512,512]{1,2,0:T(8,128)(2,1)S(1)} %get-tuple-element.21), kind=kOutput, calls=%fused_computation.75 | convolution fusion | flops 1621098496 | bytes 9437184 | tf_op jit(solution)/shard_map/ij,mjk->mik/dot_general | solution.py:75
  178.7 5.5 %convolution_bitcast_fusion.2 = f32[3,512,1024]{2,1,0:T(8,128)S(1)} fusion(bf16[3,512,512]{1,2,0:T(8,128)(2,1)S(1)} %get-tuple-element.22, bf16[3,512,512]{1,2,0:T(8,128)(2,1)S(1)} %get-tuple-element.21), kind=kOutput, calls=%fused_computation.74 | convolution fusion | flops 1621098496 | bytes 9437184 | tf_op jit(solution)/shard_map/ij,mjk->mik/dot_general | solution.py:76
  187.6 5.0 %fusion.35 = f32[3,1024,512]{2,1,0:T(8,128)S(1)} fusion(bf16[3,512,512]{2,1,0:T(8,128)(2,1)S(1)} %get-tuple-element.24, bf16[3,512,512]{2,1,0:T(8,128)(2,1)S(1)} %get-tuple-element.23), kind=kOutput, calls=%fused_computation.84 | convolution fusion | flops 1621098496 | bytes 9437184 | tf_op jit(solution)/shard_map/mij,jk->mik/dot_general | solution.py:80
  192.6 7.2 %fusion.34 = f32[3,1024,512]{2,1,0:T(8,128)S(1)} fusion(bf16[3,512,512]{2,1,0:T(8,128)(2,1)} %copy-done.14, bf16[3,512,512]{2,1,0:T(8,128)(2,1)} %copy-done.13), kind=kOutput, calls=%fused_computation.83 | convolution fusion | flops 1621098496 | bytes 9437184 | tf_op jit(solution)/shard_map/mij,jk->mik/dot_general | solution.py:81
  202.1 4.9 %fusion.31 = (f32[512,512]{1,0:T(8,128)}, f32[512,512]{1,0:T(8,128)}, f32[3,512,512]{2,1,0:T(8,128)S(1)}) fusion(f32[3,512,512]{2,1,0:T(8,128)S(1)} %get-tuple-element.20, f32[3,512,512]{2,1,0:T(8,128)S(1)} %get-tuple-element.19, f32[2,3,512,512]{3,2,1,0:T(8,128)S(1)} %bitcast.170, f32[512,512]{1,0:T(8,128)S(1)} %copy-done.5, f32[512,512]{1,0:T(8,128)} %copy-done.3), kind=kLoop, calls=%fused_computation.62 | loop fusion | flops 8126464 | bytes 19922944 | tf_op jit(solution)/shard_map/reduce_sum | solution.py:101
  209.5 6.0 %collective-permute-done.14 = f32[1536,512]{1,0:T(8,128)} collective-permute-done((f32[1536,512]{1,0:T(8,128)}, f32[1536,512]{1,0:T(8,128)}, u32[]{:S(2)}, u32[]{:S(2)}) %collective-permute-start.14) | collective-permute-done | bytes 3145760 | tf_op jit(solution)/shard_map/ppermute | solution.py:35
  228.4 31.3 %collective-permute-done.15 = f32[384,512]{1,0:T(8,128)S(1)} collective-permute-done((f32[384,512]{1,0:T(8,128)}, f32[384,512]{1,0:T(8,128)S(1)}, u32[]{:S(2)}, u32[]{:S(2)}) %collective-permute-start.15) | collective-permute-done | bytes 786464 | tf_op jit(solution)/shard_map/ppermute | solution.py:35
  274.8 4.3 collective-permute-done.19
  291.7 4.4 collective-permute-done.25
  307.7 5.4 %collective-permute-start.12 = (f32[2,512,512]{2,1,0:T(8,128)}, f32[2,512,512]{2,1,0:T(8,128)}, u32[]{:S(2)}, u32[]{:S(2)}) collective-permute-start(f32[2,512,512]{2,1,0:T(8,128)} %get-tuple-element.35), channel_id=1, source_target_pairs={{1,0},{3,2},{5,4},{7,6},{9,8},{11,10},{13,12},{15,14},{17,16},{19,... | collective-permute-start | bytes 6291464 | tf_op jit(solution)/shard_map/ppermute | solution.py:108
  319.2 79.8 %collective-permute-done.28 = f32[96,512]{1,0:T(8,128)S(1)} collective-permute-done((f32[96,512]{1,0:T(8,128)S(1)}, f32[96,512]{1,0:T(8,128)S(1)}, u32[]{:S(2)}, u32[]{:S(2)}) %collective-permute-start.28) | collective-permute-done | bytes 196640 | tf_op jit(solution)/shard_map/ppermute | solution.py:46
  403.3 17.8 %collective-permute-done.30 = f32[384,512]{1,0:T(8,128)} collective-permute-done((f32[384,512]{1,0:T(8,128)}, f32[384,512]{1,0:T(8,128)}, u32[]{:S(2)}, u32[]{:S(2)}) %collective-permute-start.30) | collective-permute-done | bytes 786464 | tf_op jit(solution)/shard_map/ppermute | solution.py:46
  436.6 8.5 %fusion.2 = f32[2,1536,512]{2,1,0:T(8,128)S(1)} fusion(s32[]{:T(128)S(6)} %select_n.319, f32[2,512,512]{2,1,0:T(8,128)S(1)} %copy-done.7, s32[]{:T(128)S(6)} %select_n.323, f32[2,512,512]{2,1,0:T(8,128)} %collective-permute-done.10, s32[]{:T(128)S(6)} %select_n.325, f32[2,512,512]{2,1,0:T(8,128)} %collective-permute-done.11, s32[]{:T(128)S(6)} %select_n.327, ...), kind=kLoop, calls=%fused_computation.10 | loop fusion | flops 4718592 | bytes 14680080 | tf_op jit(solution)/shard_map/add | solution.py:176
  451.7 25.2 %collective-permute-done.13 = f32[2,512,512]{2,1,0:T(8,128)} collective-permute-done((f32[2,512,512]{2,1,0:T(8,128)}, f32[2,512,512]{2,1,0:T(8,128)}, u32[]{:S(2)}, u32[]{:S(2)}) %collective-permute-start.13) | collective-permute-done | bytes 2097184 | tf_op jit(solution)/shard_map/ppermute | solution.py:18
  (153 shorter events, 129.4 us)
Async XLA Ops:
  3.7 28.8 %collective-permute-start = (f32[2,512,512]{2,1,0:T(8,128)}, f32[2,512,512]{2,1,0:T(8,128)S(1)}, u32[]{:S(2)}, u32[]{:S(2)}) collective-permute-start(f32[2,512,512]{2,1,0:T(8,128)} %slice.125), channel_id=1, source_target_pairs={{16,0},{32,16},{48,32},{64,48},{80,64},{96,80},{112,96},{17,1},{33... | collective-permute-start | bytes 6291464 | tf_op jit(solution)/shard_map/ppermute | solution.py:18
  15.0 11.7 %collective-permute-start.2 = (s32[]{:T(128)}, s32[]{:T(128)}, u32[]{:S(2)}, u32[]{:S(2)}) collective-permute-start(s32[]{:T(128)} %select_n.300), channel_id=1, source_target_pairs={{1,0},{2,1},{3,2},{4,3},{5,4},{6,5},{7,6},{8,7},{9,8},{10,9},{11,1... | collective-permute-start | bytes 20 | tf_op jit(solution)/shard_map/ppermute | solution.py:108
  40.1 98.0 %collective-permute-start.3 = (f32[2,512,512]{2,1,0:T(8,128)}, f32[2,512,512]{2,1,0:T(8,128)}, u32[]{:S(2)}, u32[]{:S(2)}) collective-permute-start(f32[2,512,512]{2,1,0:T(8,128)} %get-tuple-element.34), channel_id=1, source_target_pairs={{0,1},{2,3},{4,5},{6,7},{8,9},{10,11},{12,13},{14,15},{16,17},{18,... | collective-permute-start | bytes 6291464 | tf_op jit(solution)/shard_map/ppermute | solution.py:108
  41.4 96.7 %collective-permute-start.5 = (f32[2,512,512]{2,1,0:T(8,128)}, f32[2,512,512]{2,1,0:T(8,128)}, u32[]{:S(2)}, u32[]{:S(2)}) collective-permute-start(f32[2,512,512]{2,1,0:T(8,128)} %get-tuple-element.33), channel_id=1, source_target_pairs={{1,0},{2,1},{3,2},{4,3},{5,4},{6,5},{7,6},{8,7},{9,8},{10,9},{11,1... | collective-permute-start | bytes 6291464 | tf_op jit(solution)/shard_map/ppermute | solution.py:108
  47.5 90.5 %collective-permute-start.7 = (f32[2,512,512]{2,1,0:T(8,128)}, f32[2,512,512]{2,1,0:T(8,128)}, u32[]{:S(2)}, u32[]{:S(2)}) collective-permute-start(f32[2,512,512]{2,1,0:T(8,128)} %get-tuple-element.32), channel_id=1, source_target_pairs={{2,0},{4,2},{6,4},{8,6},{10,8},{12,10},{14,12},{18,16},{20,18},{22... | collective-permute-start | bytes 6291464 | tf_op jit(solution)/shard_map/ppermute | solution.py:108
  49.6 86.5 %collective-permute-start.9 = (f32[]{:T(128)}, f32[]{:T(128)}, u32[]{:S(2)}, u32[]{:S(2)}) collective-permute-start(f32[]{:T(128)} %convert_reduce_fusion), channel_id=1, source_target_pairs={{0,1},{1,0},{2,3},{3,2},{4,5},{5,4},{6,7},{7,6},{8,9},{9,8},{10,11... | collective-permute-start | bytes 20 | tf_op jit(solution)/shard_map/ppermute | solution.py:24
  52.2 118.4 %collective-permute-start.8 = (f32[1,512,512]{1,2,0:T(8,128)}, f32[1,512,512]{1,2,0:T(8,128)}, u32[]{:S(2)}, u32[]{:S(2)}) collective-permute-start(f32[1,512,512]{1,2,0:T(8,128)} %copy.25), channel_id=1, source_target_pairs={{0,1},{1,0},{2,3},{3,2},{4,5},{5,4},{6,7},{7,6},{8,9},{9,8},{10,11... | collective-permute-start | bytes 3145736 | tf_op jit(solution)/shard_map/ppermute | solution.py:24
  221.7 38.0 %collective-permute-start.15 = (f32[384,512]{1,0:T(8,128)}, f32[384,512]{1,0:T(8,128)S(1)}, u32[]{:S(2)}, u32[]{:S(2)}) collective-permute-start(f32[384,512]{1,0:T(8,128)} %get-tuple-element.39), channel_id=1, source_target_pairs={{0,32},{32,64},{64,96},{96,0},{1,33},{33,65},{65,97},{97,1},{2,34}... | collective-permute-start | bytes 2359304 | tf_op jit(solution)/shard_map/ppermute | solution.py:35
  224.7 35.0 %collective-permute-start.16 = (f32[384,512]{1,0:T(8,128)}, f32[384,512]{1,0:T(8,128)}, u32[]{:S(2)}, u32[]{:S(2)}) collective-permute-start(f32[384,512]{1,0:T(8,128)} %get-tuple-element.41), channel_id=1, source_target_pairs={{0,64},{32,96},{64,0},{96,32},{1,65},{33,97},{65,1},{97,33},{2,66}... | collective-permute-start | bytes 2359304 | tf_op jit(solution)/shard_map/ppermute | solution.py:35
  225.7 37.4 %collective-permute-start.17 = (f32[384,512]{1,0:T(8,128)}, f32[384,512]{1,0:T(8,128)}, u32[]{:S(2)}, u32[]{:S(2)}) collective-permute-start(f32[384,512]{1,0:T(8,128)} %get-tuple-element.40), channel_id=1, source_target_pairs={{0,96},{32,0},{64,32},{96,64},{1,97},{33,1},{65,33},{97,65},{2,98}... | collective-permute-start | bytes 2359304 | tf_op jit(solution)/shard_map/ppermute | solution.py:35
  266.1 8.7 %collective-permute-start.18 = (f32[96,512]{1,0:T(8,128)}, f32[96,512]{1,0:T(8,128)S(1)}, u32[]{:S(2)}, u32[]{:S(2)}) collective-permute-start(f32[96,512]{1,0:T(8,128)} %get-tuple-element.46), channel_id=1, source_target_pairs={{0,4},{4,8},{8,12},{12,0},{1,5},{5,9},{9,13},{13,1},{2,6},{6,10},{... | collective-permute-start | bytes 589832 | tf_op jit(solution)/shard_map/ppermute | solution.py:35
  266.5 12.6 %collective-permute-start.19 = (f32[96,512]{1,0:T(8,128)S(1)}, f32[96,512]{1,0:T(8,128)}, u32[]{:S(2)}, u32[]{:S(2)}) collective-permute-start(f32[96,512]{1,0:T(8,128)S(1)} %get-tuple-element.48), channel_id=1, source_target_pairs={{0,8},{4,12},{8,0},{12,4},{1,9},{5,13},{9,1},{13,5},{2,10},{6,14},... | collective-permute-start | bytes 589832 | tf_op jit(solution)/shard_map/ppermute | solution.py:35
  270.0 9.1 %collective-permute-start.20 = (f32[96,512]{1,0:T(8,128)S(1)}, f32[96,512]{1,0:T(8,128)}, u32[]{:S(2)}, u32[]{:S(2)}) collective-permute-start(f32[96,512]{1,0:T(8,128)S(1)} %get-tuple-element.47), channel_id=1, source_target_pairs={{0,12},{4,0},{8,4},{12,8},{1,13},{5,1},{9,5},{13,9},{2,14},{6,2},{... | collective-permute-start | bytes 589832 | tf_op jit(solution)/shard_map/ppermute | solution.py:35
  296.7 19.8 %collective-permute-start.27 = (f32[96,512]{1,0:T(8,128)S(1)}, f32[96,512]{1,0:T(8,128)S(1)}, u32[]{:S(2)}, u32[]{:S(2)}) collective-permute-start(f32[96,512]{1,0:T(8,128)S(1)} %bitcast.182), channel_id=1, source_target_pairs={{0,4},{4,8},{8,12},{12,0},{1,5},{5,9},{9,13},{13,1},{2,6},{6,10},{... | collective-permute-start | bytes 589832 | tf_op jit(solution)/shard_map/ppermute | solution.py:46
  302.5 134.1 %collective-permute-start.10 = (f32[2,512,512]{2,1,0:T(8,128)}, f32[2,512,512]{2,1,0:T(8,128)}, u32[]{:S(2)}, u32[]{:S(2)}) collective-permute-start(f32[2,512,512]{2,1,0:T(8,128)} %get-tuple-element.36), channel_id=1, source_target_pairs={{0,1},{1,2},{2,3},{3,4},{4,5},{5,6},{6,7},{7,8},{8,9},{9,10},{10,1... | collective-permute-start | bytes 6291464 | tf_op jit(solution)/shard_map/ppermute | solution.py:108
  305.7 130.9 %collective-permute-start.11 = (f32[2,512,512]{2,1,0:T(8,128)}, f32[2,512,512]{2,1,0:T(8,128)}, u32[]{:S(2)}, u32[]{:S(2)}) collective-permute-start(f32[2,512,512]{2,1,0:T(8,128)} %get-tuple-element.37), channel_id=1, source_target_pairs={{0,2},{2,4},{4,6},{6,8},{8,10},{10,12},{12,14},{16,18},{18,20},{20... | collective-permute-start | bytes 6291464 | tf_op jit(solution)/shard_map/ppermute | solution.py:108
  307.7 128.9 %collective-permute-start.12 = (f32[2,512,512]{2,1,0:T(8,128)}, f32[2,512,512]{2,1,0:T(8,128)}, u32[]{:S(2)}, u32[]{:S(2)}) collective-permute-start(f32[2,512,512]{2,1,0:T(8,128)} %get-tuple-element.35), channel_id=1, source_target_pairs={{1,0},{3,2},{5,4},{7,6},{9,8},{11,10},{13,12},{15,14},{17,16},{19,... | collective-permute-start | bytes 6291464 | tf_op jit(solution)/shard_map/ppermute | solution.py:108
  313.1 85.9 %collective-permute-start.28 = (f32[96,512]{1,0:T(8,128)S(1)}, f32[96,512]{1,0:T(8,128)S(1)}, u32[]{:S(2)}, u32[]{:S(2)}) collective-permute-start(f32[96,512]{1,0:T(8,128)S(1)} %bitcast.183), channel_id=1, source_target_pairs={{0,8},{4,12},{8,0},{12,4},{1,9},{5,13},{9,1},{13,5},{2,10},{6,14},... | collective-permute-start | bytes 589832 | tf_op jit(solution)/shard_map/ppermute | solution.py:46
  316.4 83.3 %collective-permute-start.29 = (f32[96,512]{1,0:T(8,128)S(1)}, f32[96,512]{1,0:T(8,128)S(1)}, u32[]{:S(2)}, u32[]{:S(2)}) collective-permute-start(f32[96,512]{1,0:T(8,128)S(1)} %bitcast.185), channel_id=1, source_target_pairs={{0,12},{4,0},{8,4},{12,8},{1,13},{5,1},{9,5},{13,9},{2,14},{6,2},{... | collective-permute-start | bytes 589832 | tf_op jit(solution)/shard_map/ppermute | solution.py:46
  400.4 20.7 %collective-permute-start.30 = (f32[384,512]{1,0:T(8,128)}, f32[384,512]{1,0:T(8,128)}, u32[]{:S(2)}, u32[]{:S(2)}) collective-permute-start(f32[384,512]{1,0:T(8,128)} %bitcast.51), channel_id=1, source_target_pairs={{0,32},{32,64},{64,96},{96,0},{1,33},{33,65},{65,97},{97,1},{2,34}... | collective-permute-start | bytes 2359304 | tf_op jit(solution)/shard_map/ppermute | solution.py:46
  401.4 28.1 %collective-permute-start.31 = (f32[384,512]{1,0:T(8,128)}, f32[384,512]{1,0:T(8,128)}, u32[]{:S(2)}, u32[]{:S(2)}) collective-permute-start(f32[384,512]{1,0:T(8,128)} %bitcast.51), channel_id=1, source_target_pairs={{0,64},{32,96},{64,0},{96,32},{1,65},{33,97},{65,1},{97,33},{2,66}... | collective-permute-start | bytes 2359304 | tf_op jit(solution)/shard_map/ppermute | solution.py:46
  421.2 13.9 %collective-permute-start.32 = (f32[384,512]{1,0:T(8,128)}, f32[384,512]{1,0:T(8,128)}, u32[]{:S(2)}, u32[]{:S(2)}) collective-permute-start(f32[384,512]{1,0:T(8,128)} %bitcast.51), channel_id=1, source_target_pairs={{0,96},{32,0},{64,32},{96,64},{1,97},{33,1},{65,33},{97,65},{2,98}... | collective-permute-start | bytes 2359304 | tf_op jit(solution)/shard_map/ppermute | solution.py:46
  436.3 44.6 %collective-permute-start.33 = (f32[1536,512]{1,0:T(8,128)S(1)}, f32[1536,512]{1,0:T(8,128)}, u32[]{:S(2)}, u32[]{:S(2)}) collective-permute-start(f32[1536,512]{1,0:T(8,128)S(1)} %bitcast.171), channel_id=1, source_target_pairs={{0,16},{16,0},{1,17},{17,1},{2,18},{18,2},{3,19},{19,3},{4,20},{20... | collective-permute-start | bytes 9437192 | tf_op jit(solution)/shard_map/ppermute | solution.py:46
  449.3 27.7 %collective-permute-start.13 = (f32[2,512,512]{2,1,0:T(8,128)}, f32[2,512,512]{2,1,0:T(8,128)}, u32[]{:S(2)}, u32[]{:S(2)}) collective-permute-start(f32[2,512,512]{2,1,0:T(8,128)} %slice.180), channel_id=1, source_target_pairs={{0,16},{16,32},{32,48},{48,64},{64,80},{80,96},{96,112},{1,17},{17... | collective-permute-start | bytes 6291464 | tf_op jit(solution)/shard_map/ppermute | solution.py:18
  (33 other events, 433.6 us)

commit v5 on v4

--- a/solution.py
+++ b/solution.py
@@ -36,25 +36,12 @@
     return total
 
 
-def gather_axis(piece, axis):
-    count = lax.axis_size(axis)
-    me = lax.axis_index(axis)
-    whole = jnp.zeros((count,) + piece.shape, piece.dtype)
-    whole = lax.dynamic_update_index_in_dim(whole, piece, me, 0)
-    for step in range(1, count):
-        pairs = [(source, (source + step) % count) for source in range(count)]
-        got = lax.ppermute(piece, axis, pairs)
-        whole = lax.dynamic_update_index_in_dim(whole, got, (me - step) % count, 0)
-    return whole.reshape(-1, piece.shape[-1])
-
-
 def all_sum(value, axes, scale):
     lines = value.reshape(-1, value.shape[-1])
     for axis in axes:
         lines = scatter_axis(lines, axis)
     lines = lines * scale
-    for axis in axes[::-1]:
-        lines = gather_axis(lines, axis)
+    lines = lax.all_gather(lines, tuple(axes), tiled=True)
     return lines.reshape(value.shape)
 
 
@@ -121,18 +108,28 @@
 
     alive_own = live_slots.astype(jnp.float32)
     live_count = jnp.sum(alive_own)
-    got_measured, got_count, got_offset = partner((amplitude[1:], live_count, offsets[1]), TX, 0)
+    got_measured = partner(amplitude[1:], TX, 0)
+    info = jnp.concatenate([jnp.sum(live_slots)[None], offsets[0], offsets[1]])
+    info_l1 = shifted(info, TX, [(s, s + 1) for s in range(count)])
+    info_r1 = shifted(info, TX, [(s, s - 1) for s in range(count)])
+    info_l2 = shifted(info, TX, [(s, s + 2) for s in range(count)])
+    info_r2 = shifted(info, TX, [(s, s - 2) for s in range(count)])
+    is_odd = lax.axis_index(TX) % 2 == 1
+
+    def processed_row(own, other):
+        return jnp.where(own[0] >= 1, own[1], other[3])
+
+    got_info = jnp.where(is_odd, info_l1, info_r1)
     use_own = live_count >= 1.0
-    is_odd = lax.axis_index(TX) % 2 == 1
     shift = jnp.where(use_own, 0, jnp.where(is_odd, -1, 1))
-    row_at = jnp.where(use_own, offsets[0, 0], got_offset[0])
-    col_at = jnp.where(use_own, offsets[0, 1], got_offset[1])
+    row_at = jnp.where(use_own, offsets[0, 0], got_info[3])
+    col_at = jnp.where(use_own, offsets[0, 1], got_info[4])
     measured = jnp.where(use_own, amplitude[0], got_measured[0])
-    alive = jnp.where(use_own, alive_own[0], (1.0 < got_count).astype(jnp.float32))
+    alive = jnp.where(use_own, alive_own[0], (1 < got_info[0]).astype(jnp.float32))
 
-    row_left = shifted(row_at, TX, [(s, s + 1) for s in range(count)])
-    row_right = shifted(row_at, TX, [(s, s - 1) for s in range(count)])
-    row_left2 = shifted(row_at, TX, [(s, s + 2) for s in evens])
+    row_left = processed_row(info_l1, jnp.where(is_odd, info, info_l2))
+    row_right = processed_row(info_r1, jnp.where(is_odd, info_r2, info))
+    row_left2 = processed_row(info_l2, info_l1)
 
     below = passed_along(specimen[:, :width, :], TY, -1)
     column = jnp.concatenate([specimen, below], axis=1)

time: 491 us -> 469 us (0.955)
  the two profiles are of different devices: /device:TPU:56 before, /device:TPU:48 now
where the time goes in v5:
time: 469 us; the launch traced here: 461 us
  waiting for transfers between devices  252 us (54%)
  starting transfers between devices  52.6 us (11%)
  other arithmetic  49 us (10%)
  matrix products  46.6 us (10%)
  local copies, waits for them, and re-layouts  37.3 us (8%)
  between operations  24.4 us (5%)
    ppermute x10, waiting for transfers between devices, shifted(): lax.ppermute(value, axis, [(a, b) for a, b in pairs if 0 <= b < lax.axis_...  161 us
    ppermute x10, waiting for transfers between devices, scatter_axis(): total = total + lax.ppermute(sent, axis, pairs)  52.9 us
    ppermute x10, starting transfers between devices, shifted(): lax.ppermute(value, axis, [(a, b) for a, b in pairs if 0 <= b < lax.axis_...  33 us
    ppermute x2, waiting for transfers between devices, passed_along(): lax.ppermute(value, axis, [(source, source + steps) for source in range(i...  27.2 us
    unnamed x34, local copies, waits for them, and re-layouts  16.2 us
    dot_general x2, matrix products, transform(): jnp.einsum('mij,jk->mik', stacked, sin_table, preferred_element_type=jnp....  13.9 us
    ppermute x10, starting transfers between devices, scatter_axis(): total = total + lax.ppermute(sent, axis, pairs)  13.4 us
    dot_general x2, matrix products, transform(): jnp.einsum('ij,mjk->mik', sin_table, stacked, preferred_element_type=jnp....  11.1 us
  transfers between devices with their start and end apart: 24, of which 16 were waited for; matrix products, arithmetic and copies ran while one was open for 14% of the time, Pallas kernels for 0%

profile of v5, /device:TPU:48, one launch (start us, length us, event | category | flops | bytes accessed | tf_op | source)
XLA Modules:
  0.0 461.4 jit_solution(1047751755009026275)
XLA Ops:
  41.5 6.0 %constant_dynamic-slice_fusion = (f32[2,512,512]{2,1,0:T(8,128)}, f32[2,512,512]{2,1,0:T(8,128)}, f32[2,512,512]{2,1,0:T(8,128)}) fusion(f32[2,1536,512]{2,1,0:T(8,128)} %constant_dynamic-update-slice_fusion, s32[]{:T(128)S(6)} %select_n.273, s32[]{:T(128)S(6)} %select_n.268, s32[]{:T(128)S(6)} %select_n.264), kind=kLoop, calls=%fused_computation.132 | loop fusion | bytes 12582924 | tf_op jit(solution)/shard_map/dynamic_slice | solution.py:138
  68.3 28.8 %collective-permute-done.4 = f32[2,512,512]{2,1,0:T(8,128)} collective-permute-done((f32[2,512,512]{2,1,0:T(8,128)}, f32[2,512,512]{2,1,0:T(8,128)}, u32[]{:S(2)}, u32[]{:S(2)}) %collective-permute-start.4) | collective-permute-done | bytes 2097184 | tf_op jit(solution)/shard_map/ppermute | solution.py:95
  97.1 5.7 %collective-permute-done.6 = f32[2,512,512]{2,1,0:T(8,128)} collective-permute-done((f32[2,512,512]{2,1,0:T(8,128)}, f32[2,512,512]{2,1,0:T(8,128)}, u32[]{:S(2)}, u32[]{:S(2)}) %collective-permute-start.6) | collective-permute-done | bytes 2097184 | tf_op jit(solution)/shard_map/ppermute | solution.py:95
  102.8 44.1 %collective-permute-done.7 = f32[2,512,512]{2,1,0:T(8,128)} collective-permute-done((f32[2,512,512]{2,1,0:T(8,128)}, f32[2,512,512]{2,1,0:T(8,128)}, u32[]{:S(2)}, u32[]{:S(2)}) %collective-permute-start.7) | collective-permute-done | bytes 2097184 | tf_op jit(solution)/shard_map/ppermute | solution.py:95
  153.4 5.4 %convolution_bitcast_fusion.1 = f32[3,512,1024]{2,1,0:T(8,128)S(1)} fusion(bf16[3,512,512]{2,1,0:T(8,128)(2,1)S(1)} %get-tuple-element.26, bf16[3,512,512]{2,1,0:T(8,128)(2,1)S(1)} %get-tuple-element.25), kind=kOutput, calls=%fused_computation.71 | convolution fusion | flops 1621098496 | bytes 9437184 | tf_op jit(solution)/shard_map/ij,mjk->mik/dot_general | solution.py:62
  158.8 5.7 %convolution_bitcast_fusion = f32[3,512,1024]{2,1,0:T(8,128)S(1)} fusion(bf16[3,512,512]{2,1,0:T(8,128)(2,1)S(1)} %get-tuple-element.26, bf16[3,512,512]{2,1,0:T(8,128)(2,1)S(1)} %get-tuple-element.25), kind=kOutput, calls=%fused_computation.70 | convolution fusion | flops 1621098496 | bytes 9437184 | tf_op jit(solution)/shard_map/ij,mjk->mik/dot_general | solution.py:63
  166.3 5.5 %fusion.37 = f32[3,1024,512]{1,2,0:T(8,128)S(1)} fusion(bf16[3,512,512]{2,1,0:T(8,128)(2,1)S(1)} %get-tuple-element.24, bf16[3,512,512]{2,1,0:T(8,128)(2,1)S(1)} %get-tuple-element.23), kind=kOutput, calls=%fused_computation.84 | convolution fusion | flops 1621098496 | bytes 9437184 | tf_op jit(solution)/shard_map/mij,jk->mik/dot_general | solution.py:67
  171.8 6.0 %fusion.36 = f32[3,1024,512]{1,2,0:T(8,128)S(1)} fusion(bf16[3,512,512]{2,1,0:T(8,128)(2,1)S(1)} %get-tuple-element.24, bf16[3,512,512]{2,1,0:T(8,128)(2,1)S(1)} %get-tuple-element.23), kind=kOutput, calls=%fused_computation.83 | convolution fusion | flops 1621098496 | bytes 9437184 | tf_op jit(solution)/shard_map/mij,jk->mik/dot_general | solution.py:68
  181.8 5.6 %convolution_bitcast_fusion.3 = f32[3,512,1024]{2,1,0:T(8,128)S(1)} fusion(bf16[3,512,512]{1,2,0:T(8,128)(2,1)S(1)} %get-tuple-element.20, bf16[3,512,512]{1,2,0:T(8,128)(2,1)S(1)} %get-tuple-element.19), kind=kOutput, calls=%fused_computation.73 | convolution fusion | flops 1621098496 | bytes 9437184 | tf_op jit(solution)/shard_map/ij,mjk->mik/dot_general | solution.py:62
  187.4 5.5 %convolution_bitcast_fusion.2 = f32[3,512,1024]{2,1,0:T(8,128)S(1)} fusion(bf16[3,512,512]{1,2,0:T(8,128)(2,1)S(1)} %get-tuple-element.20, bf16[3,512,512]{1,2,0:T(8,128)(2,1)S(1)} %get-tuple-element.19), kind=kOutput, calls=%fused_computation.72 | convolution fusion | flops 1621098496 | bytes 9437184 | tf_op jit(solution)/shard_map/ij,mjk->mik/dot_general | solution.py:63
  194.6 5.0 %fusion.35 = f32[3,1024,512]{2,1,0:T(8,128)S(1)} fusion(bf16[3,512,512]{2,1,0:T(8,128)(2,1)S(1)} %get-tuple-element.22, bf16[3,512,512]{2,1,0:T(8,128)(2,1)S(1)} %get-tuple-element.21), kind=kOutput, calls=%fused_computation.82 | convolution fusion | flops 1621098496 | bytes 9437184 | tf_op jit(solution)/shard_map/mij,jk->mik/dot_general | solution.py:67
  199.6 8.0 %fusion.34 = f32[3,1024,512]{2,1,0:T(8,128)} fusion(bf16[3,512,512]{2,1,0:T(8,128)(2,1)S(1)} %get-tuple-element.22, bf16[3,512,512]{2,1,0:T(8,128)(2,1)S(1)} %get-tuple-element.21), kind=kOutput, calls=%fused_computation.81 | convolution fusion | flops 1621098496 | bytes 9437184 | tf_op jit(solution)/shard_map/mij,jk->mik/dot_general | solution.py:68
  211.6 5.0 %fusion.31 = (f32[512,512]{1,0:T(8,128)}, f32[512,512]{1,0:T(8,128)}, f32[3,512,512]{2,1,0:T(8,128)S(1)}) fusion(f32[3,512,512]{2,1,0:T(8,128)S(1)} %get-tuple-element.18, f32[3,512,512]{2,1,0:T(8,128)S(1)} %get-tuple-element.17, f32[2,3,512,512]{3,2,1,0:T(8,128)S(1)} %bitcast.142, f32[512,512]{1,0:T(8,128)S(1)} %copy-done.3, f32[512,512]{1,0:T(8,128)} %copy-done.1), kind=kLoop, calls=%fused_computation.60 | loop fusion | flops 8126464 | bytes 19922944 | tf_op jit(solution)/shard_map/reduce_sum | solution.py:88
  219.1 6.0 %collective-permute-done.13 = f32[1536,512]{1,0:T(8,128)} collective-permute-done((f32[1536,512]{1,0:T(8,128)}, f32[1536,512]{1,0:T(8,128)}, u32[]{:S(2)}, u32[]{:S(2)}) %collective-permute-start.13) | collective-permute-done | bytes 3145760 | tf_op jit(solution)/shard_map/ppermute | solution.py:35
  237.0 14.8 %collective-permute-done.14 = f32[384,512]{1,0:T(8,128)S(1)} collective-permute-done((f32[384,512]{1,0:T(8,128)}, f32[384,512]{1,0:T(8,128)S(1)}, u32[]{:S(2)}, u32[]{:S(2)}) %collective-permute-start.14) | collective-permute-done | bytes 786464 | tf_op jit(solution)/shard_map/ppermute | solution.py:35
  255.5 16.3 %collective-permute-done.16 = f32[384,512]{1,0:T(8,128)} collective-permute-done((f32[384,512]{1,0:T(8,128)}, f32[384,512]{1,0:T(8,128)}, u32[]{:S(2)}, u32[]{:S(2)}) %collective-permute-start.16) | collective-permute-done | bytes 786464 | tf_op jit(solution)/shard_map/ppermute | solution.py:35
  280.3 6.8 %collective-permute-done.17 = f32[96,512]{1,0:T(8,128)S(1)} collective-permute-done((f32[96,512]{1,0:T(8,128)}, f32[96,512]{1,0:T(8,128)S(1)}, u32[]{:S(2)}, u32[]{:S(2)}) %collective-permute-start.17) | collective-permute-done | bytes 196640 | tf_op jit(solution)/shard_map/ppermute | solution.py:35
  306.5 5.9 %collective-permute-start.9 = (f32[2,512,512]{2,1,0:T(8,128)}, f32[2,512,512]{2,1,0:T(8,128)}, u32[]{:S(2)}, u32[]{:S(2)}) collective-permute-start(f32[2,512,512]{2,1,0:T(8,128)} %get-tuple-element.34), channel_id=1, source_target_pairs={{0,1},{1,2},{2,3},{3,4},{4,5},{5,6},{6,7},{7,8},{8,9},{9,10},{10,1... | collective-permute-start | bytes 6291464 | tf_op jit(solution)/shard_map/ppermute | solution.py:95
  312.4 67.0 %collective-permute-done.10 = f32[2,512,512]{2,1,0:T(8,128)} collective-permute-done((f32[2,512,512]{2,1,0:T(8,128)}, f32[2,512,512]{2,1,0:T(8,128)}, u32[]{:S(2)}, u32[]{:S(2)}) %collective-permute-start.10) | collective-permute-done | bytes 2097184 | tf_op jit(solution)/shard_map/ppermute | solution.py:95
  379.4 15.8 %collective-permute-done.9 = f32[2,512,512]{2,1,0:T(8,128)} collective-permute-done((f32[2,512,512]{2,1,0:T(8,128)}, f32[2,512,512]{2,1,0:T(8,128)}, u32[]{:S(2)}, u32[]{:S(2)}) %collective-permute-start.9) | collective-permute-done | bytes 2097184 | tf_op jit(solution)/shard_map/ppermute | solution.py:95
  395.2 8.4 %fusion.2 = f32[2,1536,512]{2,1,0:T(8,128)S(1)} fusion(s32[]{:T(128)S(6)} %select_n.285, f32[2,512,512]{2,1,0:T(8,128)S(1)} %get-tuple-element.36, s32[]{:T(128)S(6)} %select_n.289, f32[2,512,512]{2,1,0:T(8,128)} %collective-permute-done.9, s32[]{:T(128)S(6)} %select_n.291, f32[2,512,512]{2,1,0:T(8,128)} %collective-permute-done.10, s32[]{:T(128)S(6)} %select_n.293, ...), kind=kLoop, calls=%fused_computation.10 | loop fusion | flops 4718592 | bytes 14680080 | tf_op jit(solution)/shard_map/add | solution.py:173
  408.3 27.2 %collective-permute-done.12 = f32[2,512,512]{2,1,0:T(8,128)S(1)} collective-permute-done((f32[2,512,512]{2,1,0:T(8,128)S(1)}, f32[2,512,512]{2,1,0:T(8,128)S(1)}, u32[]{:S(2)}, u32[]{:S(2)}) %collective-permute-start.12) | collective-permute-done | bytes 2097184 | tf_op jit(solution)/shard_map/ppermute | solution.py:18
  437.3 10.0 %all-gather.2.cloned.1.call-done = f32[3072,512]{1,0:T(8,128)} async-done(((f32[24,512]{1,0:T(8,128)}), f32[3072,512]{1,0:T(8,128)}) %all-gather.2.cloned.1.call-update) | async-done | bytes 6291472 | tf_op jit(solution)/shard_map/all_gather | solution.py:44
  447.3 6.9 %copy.29 = f32[2,3,512,512]{3,2,1,0:T(8,128)} copy(f32[2,3,512,512]{3,2,1,0:T(8,128)} %bitcast.145) | data formatting | bytes 12582912
  (111 shorter events, 115.9 us)
Async XLA Ops:
  7.2 440.1 %all-gather.2.cloned.1.call-start = ((), (), s32[]{:S(2)}) async-start(), calls=%async_computation | async-start | bytes 6340608 | tf_op jit(solution)/shard_map/all_gather | solution.py:44
  10.3 29.7 %collective-permute-start = (f32[2,512,512]{2,1,0:T(8,128)}, f32[2,512,512]{2,1,0:T(8,128)S(1)}, u32[]{:S(2)}, u32[]{:S(2)}) collective-permute-start(f32[2,512,512]{2,1,0:T(8,128)} %slice.158), channel_id=1, source_target_pairs={{16,0},{32,16},{48,32},{64,48},{80,64},{96,80},{112,96},{17,1},{33... | collective-permute-start | bytes 6291464 | tf_op jit(solution)/shard_map/ppermute | solution.py:18
  13.6 17.9 %collective-permute-start.5 = (s32[5]{0:T(128)S(1)}, s32[5]{0:T(128)S(1)}, u32[]{:S(2)}, u32[]{:S(2)}) collective-permute-start(s32[5]{0:T(128)S(1)} %pad_add_fusion), channel_id=1, source_target_pairs={{0,2},{1,3},{2,4},{3,5},{4,6},{5,7},{6,8},{7,9},{8,10},{9,11},{10,... | collective-permute-start | bytes 68 | tf_op jit(solution)/shard_map/ppermute | solution.py:95
  16.8 14.7 %collective-permute-start.3 = (s32[5]{0:T(128)S(1)}, s32[5]{0:T(128)S(1)}, u32[]{:S(2)}, u32[]{:S(2)}) collective-permute-start(s32[5]{0:T(128)S(1)} %pad_add_fusion), channel_id=1, source_target_pairs={{2,0},{3,1},{4,2},{5,3},{6,4},{7,5},{8,6},{9,7},{10,8},{11,9},{12,... | collective-permute-start | bytes 68 | tf_op jit(solution)/shard_map/ppermute | solution.py:95
  20.9 11.1 %collective-permute-start.1 = (s32[5]{0:T(128)S(1)}, s32[5]{0:T(128)S(1)}, u32[]{:S(2)}, u32[]{:S(2)}) collective-permute-start(s32[5]{0:T(128)S(1)} %pad_add_fusion), channel_id=1, source_target_pairs={{0,1},{1,2},{2,3},{3,4},{4,5},{5,6},{6,7},{7,8},{8,9},{9,10},{10,1... | collective-permute-start | bytes 68 | tf_op jit(solution)/shard_map/ppermute | solution.py:95
  24.1 11.0 %collective-permute-start.2 = (s32[5]{0:T(128)S(1)}, s32[5]{0:T(128)S(1)}, u32[]{:S(2)}, u32[]{:S(2)}) collective-permute-start(s32[5]{0:T(128)S(1)} %pad_add_fusion), channel_id=1, source_target_pairs={{1,0},{2,1},{3,2},{4,3},{5,4},{6,5},{7,6},{8,7},{9,8},{10,9},{11,1... | collective-permute-start | bytes 68 | tf_op jit(solution)/shard_map/ppermute | solution.py:95
  47.5 49.5 %collective-permute-start.4 = (f32[2,512,512]{2,1,0:T(8,128)}, f32[2,512,512]{2,1,0:T(8,128)}, u32[]{:S(2)}, u32[]{:S(2)}) collective-permute-start(f32[2,512,512]{2,1,0:T(8,128)} %get-tuple-element.32), channel_id=1, source_target_pairs={{0,1},{2,3},{4,5},{6,7},{8,9},{10,11},{12,13},{14,15},{16,17},{18,... | collective-permute-start | bytes 6291464 | tf_op jit(solution)/shard_map/ppermute | solution.py:95
  52.1 50.7 %collective-permute-start.6 = (f32[2,512,512]{2,1,0:T(8,128)}, f32[2,512,512]{2,1,0:T(8,128)}, u32[]{:S(2)}, u32[]{:S(2)}) collective-permute-start(f32[2,512,512]{2,1,0:T(8,128)} %get-tuple-element.31), channel_id=1, source_target_pairs={{1,0},{2,1},{3,2},{4,3},{5,4},{6,5},{7,6},{8,7},{9,8},{10,9},{11,1... | collective-permute-start | bytes 6291464 | tf_op jit(solution)/shard_map/ppermute | solution.py:95
  54.0 92.8 %collective-permute-start.7 = (f32[2,512,512]{2,1,0:T(8,128)}, f32[2,512,512]{2,1,0:T(8,128)}, u32[]{:S(2)}, u32[]{:S(2)}) collective-permute-start(f32[2,512,512]{2,1,0:T(8,128)} %get-tuple-element.30), channel_id=1, source_target_pairs={{2,0},{4,2},{6,4},{8,6},{10,8},{12,10},{14,12},{18,16},{20,18},{22... | collective-permute-start | bytes 6291464 | tf_op jit(solution)/shard_map/ppermute | solution.py:95
  58.4 121.1 %collective-permute-start.8 = (f32[1,512,512]{1,2,0:T(8,128)}, f32[1,512,512]{1,2,0:T(8,128)}, u32[]{:S(2)}, u32[]{:S(2)}) collective-permute-start(f32[1,512,512]{1,2,0:T(8,128)} %copy.25), channel_id=1, source_target_pairs={{0,1},{1,0},{2,3},{3,2},{4,5},{5,4},{6,7},{7,6},{8,9},{9,8},{10,11... | collective-permute-start | bytes 3145736 | tf_op jit(solution)/shard_map/ppermute | solution.py:24
  219.1 6.0 %collective-permute-start.13 = (f32[1536,512]{1,0:T(8,128)}, f32[1536,512]{1,0:T(8,128)}, u32[]{:S(2)}, u32[]{:S(2)}) collective-permute-start(f32[1536,512]{1,0:T(8,128)} %fusion.10), channel_id=1, source_target_pairs={{0,16},{16,0},{1,17},{17,1},{2,18},{18,2},{3,19},{19,3},{4,20},{20... | collective-permute-start | bytes 9437192 | tf_op jit(solution)/shard_map/ppermute | solution.py:35
  231.3 20.5 %collective-permute-start.14 = (f32[384,512]{1,0:T(8,128)}, f32[384,512]{1,0:T(8,128)S(1)}, u32[]{:S(2)}, u32[]{:S(2)}) collective-permute-start(f32[384,512]{1,0:T(8,128)} %get-tuple-element.37), channel_id=1, source_target_pairs={{0,32},{32,64},{64,96},{96,0},{1,33},{33,65},{65,97},{97,1},{2,34}... | collective-permute-start | bytes 2359304 | tf_op jit(solution)/shard_map/ppermute | solution.py:35
  233.2 22.3 %collective-permute-start.15 = (f32[384,512]{1,0:T(8,128)}, f32[384,512]{1,0:T(8,128)}, u32[]{:S(2)}, u32[]{:S(2)}) collective-permute-start(f32[384,512]{1,0:T(8,128)} %get-tuple-element.39), channel_id=1, source_target_pairs={{0,64},{32,96},{64,0},{96,32},{1,65},{33,97},{65,1},{97,33},{2,66}... | collective-permute-start | bytes 2359304 | tf_op jit(solution)/shard_map/ppermute | solution.py:35
  234.4 37.4 %collective-permute-start.16 = (f32[384,512]{1,0:T(8,128)}, f32[384,512]{1,0:T(8,128)}, u32[]{:S(2)}, u32[]{:S(2)}) collective-permute-start(f32[384,512]{1,0:T(8,128)} %get-tuple-element.38), channel_id=1, source_target_pairs={{0,96},{32,0},{64,32},{96,64},{1,97},{33,1},{65,33},{97,65},{2,98}... | collective-permute-start | bytes 2359304 | tf_op jit(solution)/shard_map/ppermute | solution.py:35
  274.7 12.4 %collective-permute-start.17 = (f32[96,512]{1,0:T(8,128)}, f32[96,512]{1,0:T(8,128)S(1)}, u32[]{:S(2)}, u32[]{:S(2)}) collective-permute-start(f32[96,512]{1,0:T(8,128)} %get-tuple-element.44), channel_id=1, source_target_pairs={{0,4},{4,8},{8,12},{12,0},{1,5},{5,9},{9,13},{13,1},{2,6},{6,10},{... | collective-permute-start | bytes 589832 | tf_op jit(solution)/shard_map/ppermute | solution.py:35
  276.2 10.9 %collective-permute-start.18 = (f32[96,512]{1,0:T(8,128)S(1)}, f32[96,512]{1,0:T(8,128)}, u32[]{:S(2)}, u32[]{:S(2)}) collective-permute-start(f32[96,512]{1,0:T(8,128)S(1)} %get-tuple-element.46), channel_id=1, source_target_pairs={{0,8},{4,12},{8,0},{12,4},{1,9},{5,13},{9,1},{13,5},{2,10},{6,14},... | collective-permute-start | bytes 589832 | tf_op jit(solution)/shard_map/ppermute | solution.py:35
  277.7 10.1 %collective-permute-start.19 = (f32[96,512]{1,0:T(8,128)S(1)}, f32[96,512]{1,0:T(8,128)}, u32[]{:S(2)}, u32[]{:S(2)}) collective-permute-start(f32[96,512]{1,0:T(8,128)S(1)} %get-tuple-element.45), channel_id=1, source_target_pairs={{0,12},{4,0},{8,4},{12,8},{1,13},{5,1},{9,5},{13,9},{2,14},{6,2},{... | collective-permute-start | bytes 589832 | tf_op jit(solution)/shard_map/ppermute | solution.py:35
  288.9 4.2 collective-permute-start.20
  289.0 5.7 %collective-permute-start.21 = (f32[24,512]{1,0:T(8,128)S(1)}, f32[24,512]{1,0:T(8,128)S(1)}, u32[]{:S(2)}, u32[]{:S(2)}) collective-permute-start(f32[24,512]{1,0:T(8,128)S(1)} %get-tuple-element.49), channel_id=1, source_target_pairs={{0,2},{1,3},{2,0},{3,1},{4,6},{5,7},{6,4},{7,5},{8,10},{9,11},{10,... | collective-permute-start | bytes 147464 | tf_op jit(solution)/shard_map/ppermute | solution.py:35
  289.1 6.6 %collective-permute-start.22 = (f32[24,512]{1,0:T(8,128)S(1)}, f32[24,512]{1,0:T(8,128)S(1)}, u32[]{:S(2)}, u32[]{:S(2)}) collective-permute-start(f32[24,512]{1,0:T(8,128)S(1)} %get-tuple-element.48), channel_id=1, source_target_pairs={{0,3},{1,0},{2,1},{3,2},{4,7},{5,4},{6,5},{7,6},{8,11},{9,8},{10,9... | collective-permute-start | bytes 147464 | tf_op jit(solution)/shard_map/ppermute | solution.py:35
  300.9 78.5 %collective-permute-start.10 = (f32[2,512,512]{2,1,0:T(8,128)}, f32[2,512,512]{2,1,0:T(8,128)}, u32[]{:S(2)}, u32[]{:S(2)}) collective-permute-start(f32[2,512,512]{2,1,0:T(8,128)} %get-tuple-element.35), channel_id=1, source_target_pairs={{0,2},{2,4},{4,6},{6,8},{8,10},{10,12},{12,14},{16,18},{18,20},{20... | collective-permute-start | bytes 6291464 | tf_op jit(solution)/shard_map/ppermute | solution.py:95
  305.2 74.2 %collective-permute-start.11 = (f32[2,512,512]{2,1,0:T(8,128)}, f32[2,512,512]{2,1,0:T(8,128)}, u32[]{:S(2)}, u32[]{:S(2)}) collective-permute-start(f32[2,512,512]{2,1,0:T(8,128)} %get-tuple-element.33), channel_id=1, source_target_pairs={{1,0},{3,2},{5,4},{7,6},{9,8},{11,10},{13,12},{15,14},{17,16},{19,... | collective-permute-start | bytes 6291464 | tf_op jit(solution)/shard_map/ppermute | solution.py:95
  306.5 88.7 %collective-permute-start.9 = (f32[2,512,512]{2,1,0:T(8,128)}, f32[2,512,512]{2,1,0:T(8,128)}, u32[]{:S(2)}, u32[]{:S(2)}) collective-permute-start(f32[2,512,512]{2,1,0:T(8,128)} %get-tuple-element.34), channel_id=1, source_target_pairs={{0,1},{1,2},{2,3},{3,4},{4,5},{5,6},{6,7},{7,8},{8,9},{9,10},{10,1... | collective-permute-start | bytes 6291464 | tf_op jit(solution)/shard_map/ppermute | solution.py:95
  403.8 31.6 %collective-permute-start.12 = (f32[2,512,512]{2,1,0:T(8,128)S(1)}, f32[2,512,512]{2,1,0:T(8,128)S(1)}, u32[]{:S(2)}, u32[]{:S(2)}) collective-permute-start(f32[2,512,512]{2,1,0:T(8,128)S(1)} %slice.224), channel_id=1, source_target_pairs={{0,16},{16,32},{32,48},{48,64},{64,80},{80,96},{96,112},{1,17},{17... | collective-permute-start | bytes 6291464 | tf_op jit(solution)/shard_map/ppermute | solution.py:18
  (15 other events, 408.9 us)
Sparse Core Ops, SparseCore 0:
  296.5 150.7 all-gather.1

commit v6 on v5

--- a/solution.py
+++ b/solution.py
@@ -131,18 +131,27 @@
     row_right = processed_row(info_r1, jnp.where(is_odd, info_r2, info))
     row_left2 = processed_row(info_l2, info_l1)
 
-    below = passed_along(specimen[:, :width, :], TY, -1)
-    column = jnp.concatenate([specimen, below], axis=1)
+    half = width // 2
+    below_first = passed_along(specimen[:, :width, :half], TY, -1)
+    second_cols, below_first = lax.optimization_barrier((specimen[:, :width, half:], below_first))
+    below_second = passed_along(second_cols, TY, -1)
 
-    def strip(source, at):
-        return lax.dynamic_slice(source, (anchor, at, anchor), (2, width, width))
+    def strips(column):
+        def strip(at):
+            return lax.dynamic_slice(column, (anchor, at, anchor), (2, width, column.shape[2]))
 
-    own_strip = strip(column, row_at)
-    from_right = shifted(strip(column, row_left), TX, [(s, s - 1) for s in range(count)])
-    from_left = shifted(strip(column, row_right), TX, [(s, s + 1) for s in evens])
-    from_right2 = shifted(strip(column, row_left2), TX, [(s, s - 2) for s in evens])
-    left_strip = jnp.where(shift == 0, own_strip, jnp.where(shift < 0, from_left, from_right))
-    right_strip = jnp.where(shift == 0, from_right, jnp.where(shift < 0, own_strip, from_right2))
+        own_strip = strip(row_at)
+        from_right = shifted(strip(row_left), TX, [(s, s - 1) for s in range(count)])
+        from_left = shifted(strip(row_right), TX, [(s, s + 1) for s in evens])
+        from_right2 = shifted(strip(row_left2), TX, [(s, s - 2) for s in evens])
+        left_strip = jnp.where(shift == 0, own_strip, jnp.where(shift < 0, from_left, from_right))
+        right_strip = jnp.where(shift == 0, from_right, jnp.where(shift < 0, own_strip, from_right2))
+        return left_strip, right_strip
+
+    left_first, right_first = strips(jnp.concatenate([specimen[:, :, :half], below_first], axis=1))
+    left_second, right_second = strips(jnp.concatenate([specimen[:, :, half:], below_second], axis=1))
+    left_strip = jnp.concatenate([left_first, left_second], axis=2)
+    right_strip = jnp.concatenate([right_first, right_second], axis=2)
     pair_strip = jnp.concatenate([left_strip, right_strip], axis=2)
     window = lax.dynamic_slice(pair_strip, (anchor, anchor, col_at), (2, width, width))
 
@@ -164,12 +173,11 @@
     got_left2 = shifted(send_right2, TX, [(s, s + 2) for s in evens])
     got_right = shifted(send_left, TX, [(s, s - 1) for s in odds])
 
-    rows_all = column.shape[1]
-
     def spread(piece, at):
         padded = jnp.pad(piece, ((0, 0), (rows_all, rows_all), (0, 0)))
         return lax.dynamic_slice(padded, (anchor, rows_all - at, anchor), (2, rows_all, width))
 
+    rows_all = tile_h + width
     grad_column = (
         (spread(keep, row_at) + spread(got_left, row_left)) + spread(got_left2, row_left2)
     ) + spread(got_right, row_right)

time: 469 us -> 472 us (level)
  waiting for transfers between devices: 252 us -> 231 us
  starting transfers between devices: 52.6 us -> 65.8 us
  other arithmetic: 49 us -> 61.1 us
  local copies, waits for them, and re-layouts: 37.3 us -> 32.4 us
    ppermute x10 -> x13, waiting for transfers between devices: 161 us -> 140 us  [shifted(): lax.ppermute(value, axis, [(a, b) for a, b in pairs if 0 <= b < lax.axis_...]
    concatenate x0 -> x2, other arithmetic: none -> 7.54 us  [the longest x1 4.34 us: local(): jnp.concatenate([specimen[:, :, half:], below_second], axis=1)]
    ppermute x10, starting transfers between devices: 13.4 us -> 20.4 us  [scatter_axis(): total = total + lax.ppermute(sent, axis, pairs)]
    dynamic_slice x1 -> x0, local copies, waits for them, and re-layouts: 6.01 us -> none  [strip(): return lax.dynamic_slice(source, (anchor, at, anchor), (2, width, width))]
    ppermute x10 -> x13, starting transfers between devices: 33 us -> 36.6 us  [shifted(): lax.ppermute(value, axis, [(a, b) for a, b in pairs if 0 <= b < lax.axis_...]
    ppermute x2 -> x3, waiting for transfers between devices: 27.2 us -> 25.4 us  [passed_along(): lax.ppermute(value, axis, [(source, source + steps) for source in range(i...]
    unnamed x34 -> x37, local copies, waits for them, and re-layouts: 16.2 us -> 14.5 us
  transfers between devices with their start and end apart: 24 -> 28, of which waited for: 16 -> 16; matrix products, arithmetic and copies ran while one was open for 14% -> 17% of each run, Pallas kernels for 0% -> 0%
where the time goes in v6:
time: 472 us; the launch traced here: 463 us
  waiting for transfers between devices  231 us (49%)
  starting transfers between devices  65.8 us (14%)
  other arithmetic  61.1 us (13%)
  matrix products  48.7 us (10%)
  local copies, waits for them, and re-layouts  32.4 us (7%)
  between operations  24.2 us (5%)
    ppermute x13, waiting for transfers between devices, shifted(): lax.ppermute(value, axis, [(a, b) for a, b in pairs if 0 <= b < lax.axis_...  140 us
    ppermute x10, waiting for transfers between devices, scatter_axis(): total = total + lax.ppermute(sent, axis, pairs)  51.4 us
    ppermute x13, starting transfers between devices, shifted(): lax.ppermute(value, axis, [(a, b) for a, b in pairs if 0 <= b < lax.axis_...  36.6 us
    ppermute x3, waiting for transfers between devices, passed_along(): lax.ppermute(value, axis, [(source, source + steps) for source in range(i...  25.4 us
    ppermute x10, starting transfers between devices, scatter_axis(): total = total + lax.ppermute(sent, axis, pairs)  20.4 us
    unnamed x37, local copies, waits for them, and re-layouts  14.5 us
    all_gather x1, waiting for transfers between devices, all_sum(): lines = lax.all_gather(lines, tuple(axes), tiled=True)  13.7 us
    dot_general x2, matrix products, transform(): jnp.einsum('mij,jk->mik', stacked, sin_table, preferred_element_type=jnp....  13.5 us
  transfers between devices with their start and end apart: 28, of which 16 were waited for; matrix products, arithmetic and copies ran while one was open for 17% of the time, Pallas kernels for 0%

profile of v6, /device:TPU:48, one launch (start us, length us, event | category | flops | bytes accessed | tf_op | source)
XLA Modules:
  0.0 462.8 jit_solution(17094752777941911388)
XLA Ops:
  53.9 4.3 fusion.43
  60.1 4.3 collective-permute-start.8
  64.5 10.7 %collective-permute-done.10 = f32[2,512,256]{2,1,0:T(8,128)} collective-permute-done((f32[2,512,256]{2,1,0:T(8,128)}, f32[2,512,256]{2,1,0:T(8,128)}, u32[]{:S(2)}, u32[]{:S(2)}) %collective-permute-start.10) | collective-permute-done | bytes 1048608 | tf_op jit(solution)/shard_map/ppermute | solution.py:95
  97.8 22.4 %collective-permute-done.11 = f32[2,512,256]{2,1,0:T(8,128)} collective-permute-done((f32[2,512,256]{2,1,0:T(8,128)}, f32[2,512,256]{2,1,0:T(8,128)}, u32[]{:S(2)}, u32[]{:S(2)}) %collective-permute-start.11) | collective-permute-done | bytes 1048608 | tf_op jit(solution)/shard_map/ppermute | solution.py:95
  120.1 17.3 %collective-permute-done.8 = f32[2,512,256]{2,1,0:T(8,128)} collective-permute-done((f32[2,512,256]{2,1,0:T(8,128)}, f32[2,512,256]{2,1,0:T(8,128)}, u32[]{:S(2)}, u32[]{:S(2)}) %collective-permute-start.8) | collective-permute-done | bytes 1048608 | tf_op jit(solution)/shard_map/ppermute | solution.py:95
  144.0 5.4 %convolution_bitcast_fusion.1 = f32[3,512,1024]{2,1,0:T(8,128)S(1)} fusion(bf16[3,512,512]{2,1,0:T(8,128)(2,1)S(1)} %get-tuple-element.30, bf16[3,512,512]{2,1,0:T(8,128)(2,1)S(1)} %get-tuple-element.29), kind=kOutput, calls=%fused_computation.89 | convolution fusion | flops 1621098496 | bytes 9437184 | tf_op jit(solution)/shard_map/ij,mjk->mik/dot_general | solution.py:62
  149.4 5.6 %convolution_bitcast_fusion = f32[3,512,1024]{2,1,0:T(8,128)S(1)} fusion(bf16[3,512,512]{2,1,0:T(8,128)(2,1)S(1)} %get-tuple-element.30, bf16[3,512,512]{2,1,0:T(8,128)(2,1)S(1)} %get-tuple-element.29), kind=kOutput, calls=%fused_computation.88 | convolution fusion | flops 1621098496 | bytes 9437184 | tf_op jit(solution)/shard_map/ij,mjk->mik/dot_general | solution.py:63
  156.9 5.5 %fusion.39 = f32[3,1024,512]{1,2,0:T(8,128)S(1)} fusion(bf16[3,512,512]{2,1,0:T(8,128)(2,1)S(1)} %get-tuple-element.28, bf16[3,512,512]{2,1,0:T(8,128)(2,1)S(1)} %get-tuple-element.27), kind=kOutput, calls=%fused_computation.102 | convolution fusion | flops 1621098496 | bytes 9437184 | tf_op jit(solution)/shard_map/mij,jk->mik/dot_general | solution.py:67
  162.4 5.8 %fusion.38 = f32[3,1024,512]{1,2,0:T(8,128)S(1)} fusion(bf16[3,512,512]{2,1,0:T(8,128)(2,1)S(1)} %get-tuple-element.28, bf16[3,512,512]{2,1,0:T(8,128)(2,1)S(1)} %get-tuple-element.27), kind=kOutput, calls=%fused_computation.101 | convolution fusion | flops 1621098496 | bytes 9437184 | tf_op jit(solution)/shard_map/mij,jk->mik/dot_general | solution.py:68
  171.3 4.7 %multiply_convert_fusion.1 = (bf16[3,512,512]{1,2,0:T(8,128)(2,1)}, bf16[3,512,512]{1,2,0:T(8,128)(2,1)}) fusion(f32[512,512]{0,1:T(8,128)} %fusion.52, f32[3,1024,512]{1,2,0:T(8,128)S(1)} %fusion.38, f32[3,1024,512]{1,2,0:T(8,128)S(1)} %fusion.39), kind=kLoop, calls=%fused_computation.86 | loop fusion | flops 4718592 | bytes 16777216 | tf_op jit(solution)/shard_map/convert_element_type | solution.py:82
  176.0 7.9 %convolution_bitcast_fusion.3 = f32[3,512,1024]{2,1,0:T(8,128)S(1)} fusion(bf16[3,512,512]{1,2,0:T(8,128)(2,1)} %get-tuple-element.24, bf16[3,512,512]{1,2,0:T(8,128)(2,1)} %get-tuple-element.23), kind=kOutput, calls=%fused_computation.91 | convolution fusion | flops 1621098496 | bytes 9437184 | tf_op jit(solution)/shard_map/ij,mjk->mik/dot_general | solution.py:62
  183.9 5.5 %convolution_bitcast_fusion.2 = f32[3,512,1024]{2,1,0:T(8,128)S(1)} fusion(bf16[3,512,512]{1,2,0:T(8,128)(2,1)S(1)} %copy-done.11, bf16[3,512,512]{1,2,0:T(8,128)(2,1)S(1)} %copy-done.10), kind=kOutput, calls=%fused_computation.90 | convolution fusion | flops 1621098496 | bytes 9437184 | tf_op jit(solution)/shard_map/ij,mjk->mik/dot_general | solution.py:63
  191.1 5.3 %fusion.37 = f32[3,1024,512]{2,1,0:T(8,128)S(1)} fusion(bf16[3,512,512]{2,1,0:T(8,128)(2,1)S(1)} %get-tuple-element.26, bf16[3,512,512]{2,1,0:T(8,128)(2,1)S(1)} %get-tuple-element.25), kind=kOutput, calls=%fused_computation.100 | convolution fusion | flops 1621098496 | bytes 9437184 | tf_op jit(solution)/shard_map/mij,jk->mik/dot_general | solution.py:67
  196.4 7.8 %fusion.36 = f32[3,1024,512]{2,1,0:T(8,128)} fusion(bf16[3,512,512]{2,1,0:T(8,128)(2,1)S(1)} %get-tuple-element.26, bf16[3,512,512]{2,1,0:T(8,128)(2,1)S(1)} %get-tuple-element.25), kind=kOutput, calls=%fused_computation.99 | convolution fusion | flops 1621098496 | bytes 9437184 | tf_op jit(solution)/shard_map/mij,jk->mik/dot_general | solution.py:68
  214.6 5.6 %collective-permute-done.17 = f32[1536,512]{1,0:T(8,128)} collective-permute-done((f32[1536,512]{1,0:T(8,128)}, f32[1536,512]{1,0:T(8,128)}, u32[]{:S(2)}, u32[]{:S(2)}) %collective-permute-start.17) | collective-permute-done | bytes 3145760 | tf_op jit(solution)/shard_map/ppermute | solution.py:35
  233.2 30.4 %collective-permute-done.18 = f32[384,512]{1,0:T(8,128)S(1)} collective-permute-done((f32[384,512]{1,0:T(8,128)}, f32[384,512]{1,0:T(8,128)S(1)}, u32[]{:S(2)}, u32[]{:S(2)}) %collective-permute-start.18) | collective-permute-done | bytes 786464 | tf_op jit(solution)/shard_map/ppermute | solution.py:35
  270.6 4.8 %collective-permute-start.21 = (f32[96,512]{1,0:T(8,128)}, f32[96,512]{1,0:T(8,128)S(1)}, u32[]{:S(2)}, u32[]{:S(2)}) collective-permute-start(f32[96,512]{1,0:T(8,128)} %get-tuple-element.57), channel_id=1, source_target_pairs={{0,4},{4,8},{8,12},{12,0},{1,5},{5,9},{9,13},{13,1},{2,6},{6,10},{... | collective-permute-start | bytes 589832 | tf_op jit(solution)/shard_map/ppermute | solution.py:35
  282.4 5.5 %collective-permute-done.22 = f32[96,512]{1,0:T(8,128)} collective-permute-done((f32[96,512]{1,0:T(8,128)S(1)}, f32[96,512]{1,0:T(8,128)}, u32[]{:S(2)}, u32[]{:S(2)}) %collective-permute-start.22) | collective-permute-done | bytes 196640 | tf_op jit(solution)/shard_map/ppermute | solution.py:35
  309.8 43.4 %collective-permute-done.13 = f32[2,512,512]{2,1,0:T(8,128)} collective-permute-done((f32[2,512,512]{2,1,0:T(8,128)}, f32[2,512,512]{2,1,0:T(8,128)}, u32[]{:S(2)}, u32[]{:S(2)}) %collective-permute-start.13) | collective-permute-done | bytes 2097184 | tf_op jit(solution)/shard_map/ppermute | solution.py:95
  353.2 42.0 %collective-permute-done.14 = f32[2,512,512]{2,1,0:T(8,128)} collective-permute-done((f32[2,512,512]{2,1,0:T(8,128)}, f32[2,512,512]{2,1,0:T(8,128)}, u32[]{:S(2)}, u32[]{:S(2)}) %collective-permute-start.14) | collective-permute-done | bytes 2097184 | tf_op jit(solution)/shard_map/ppermute | solution.py:95
  395.2 8.4 %fusion.2 = f32[2,1536,512]{2,1,0:T(8,128)S(1)} fusion(s32[]{:T(128)S(6)} %select_n.317, f32[2,512,512]{2,1,0:T(8,128)S(1)} %get-tuple-element.35, s32[]{:T(128)S(6)} %select_n.321, f32[2,512,512]{2,1,0:T(8,128)} %collective-permute-done.13, s32[]{:T(128)S(6)} %select_n.323, f32[2,512,512]{2,1,0:T(8,128)} %collective-permute-done.14, s32[]{:T(128)S(6)} %select_n.325, ...), kind=kLoop, calls=%fused_computation.10 | loop fusion | flops 4718592 | bytes 14680080 | tf_op jit(solution)/shard_map/add | solution.py:181
  408.2 25.1 %collective-permute-done.16 = f32[2,512,512]{2,1,0:T(8,128)S(1)} collective-permute-done((f32[2,512,512]{2,1,0:T(8,128)S(1)}, f32[2,512,512]{2,1,0:T(8,128)S(1)}, u32[]{:S(2)}, u32[]{:S(2)}) %collective-permute-start.16) | collective-permute-done | bytes 2097184 | tf_op jit(solution)/shard_map/ppermute | solution.py:18
  435.1 13.7 %all-gather.2.cloned.1.call-done = f32[3072,512]{1,0:T(8,128)} async-done(((f32[24,512]{1,0:T(8,128)}), f32[3072,512]{1,0:T(8,128)}) %all-gather.2.cloned.1.call-update) | async-done | bytes 6291472 | tf_op jit(solution)/shard_map/all_gather | solution.py:44
  448.8 6.9 %copy.28 = f32[2,3,512,512]{3,2,1,0:T(8,128)} copy(f32[2,3,512,512]{3,2,1,0:T(8,128)} %bitcast.143) | data formatting | bytes 12582912
  (123 shorter events, 140.2 us)
Async XLA Ops:
  7.2 441.6 %all-gather.2.cloned.1.call-start = ((), (), s32[]{:S(2)}) async-start(), calls=%async_computation | async-start | bytes 6340608 | tf_op jit(solution)/shard_map/all_gather | solution.py:44
  10.3 29.1 %collective-permute-start = (f32[2,512,256]{2,1,0:T(8,128)}, f32[2,512,256]{2,1,0:T(8,128)S(1)}, u32[]{:S(2)}, u32[]{:S(2)}) collective-permute-start(f32[2,512,256]{2,1,0:T(8,128)} %get-tuple-element.42), channel_id=1, source_target_pairs={{16,0},{32,16},{48,32},{64,48},{80,64},{96,80},{112,96},{17,1},{33... | collective-permute-start | bytes 3145736 | tf_op jit(solution)/shard_map/ppermute | solution.py:18
  13.5 17.2 %collective-permute-start.5 = (s32[5]{0:T(128)S(1)}, s32[5]{0:T(128)S(1)}, u32[]{:S(2)}, u32[]{:S(2)}) collective-permute-start(s32[5]{0:T(128)S(1)} %pad_add_fusion), channel_id=1, source_target_pairs={{0,2},{1,3},{2,4},{3,5},{4,6},{5,7},{6,8},{7,9},{8,10},{9,11},{10,... | collective-permute-start | bytes 68 | tf_op jit(solution)/shard_map/ppermute | solution.py:95
  16.7 14.0 %collective-permute-start.3 = (s32[5]{0:T(128)S(1)}, s32[5]{0:T(128)S(1)}, u32[]{:S(2)}, u32[]{:S(2)}) collective-permute-start(s32[5]{0:T(128)S(1)} %pad_add_fusion), channel_id=1, source_target_pairs={{2,0},{3,1},{4,2},{5,3},{6,4},{7,5},{8,6},{9,7},{10,8},{11,9},{12,... | collective-permute-start | bytes 68 | tf_op jit(solution)/shard_map/ppermute | solution.py:95
  20.9 10.5 %collective-permute-start.1 = (s32[5]{0:T(128)S(1)}, s32[5]{0:T(128)S(1)}, u32[]{:S(2)}, u32[]{:S(2)}) collective-permute-start(s32[5]{0:T(128)S(1)} %pad_add_fusion), channel_id=1, source_target_pairs={{0,1},{1,2},{2,3},{3,4},{4,5},{5,6},{6,7},{7,8},{8,9},{9,10},{10,1... | collective-permute-start | bytes 68 | tf_op jit(solution)/shard_map/ppermute | solution.py:95
  24.1 10.4 %collective-permute-start.2 = (s32[5]{0:T(128)S(1)}, s32[5]{0:T(128)S(1)}, u32[]{:S(2)}, u32[]{:S(2)}) collective-permute-start(s32[5]{0:T(128)S(1)} %pad_add_fusion), channel_id=1, source_target_pairs={{1,0},{2,1},{3,2},{4,3},{5,4},{6,5},{7,6},{8,7},{9,8},{10,9},{11,1... | collective-permute-start | bytes 68 | tf_op jit(solution)/shard_map/ppermute | solution.py:95
  39.3 14.5 %collective-permute-start.7 = (f32[2,512,256]{2,1,0:T(8,128)}, f32[2,512,256]{2,1,0:T(8,128)}, u32[]{:S(2)}, u32[]{:S(2)}) collective-permute-start(f32[2,512,256]{2,1,0:T(8,128)} %get-tuple-element.17), channel_id=1, source_target_pairs={{16,0},{32,16},{48,32},{64,48},{80,64},{96,80},{112,96},{17,1},{33... | collective-permute-start | bytes 3145736 | tf_op jit(solution)/shard_map/ppermute | solution.py:18
  44.5 30.7 %collective-permute-start.10 = (f32[2,512,256]{2,1,0:T(8,128)}, f32[2,512,256]{2,1,0:T(8,128)}, u32[]{:S(2)}, u32[]{:S(2)}) collective-permute-start(f32[2,512,256]{2,1,0:T(8,128)} %get-tuple-element.50), channel_id=1, source_target_pairs={{2,0},{4,2},{6,4},{8,6},{10,8},{12,10},{14,12},{18,16},{20,18},{22... | collective-permute-start | bytes 3145736 | tf_op jit(solution)/shard_map/ppermute | solution.py:95
  46.4 46.1 %collective-permute-start.4 = (f32[2,512,256]{2,1,0:T(8,128)}, f32[2,512,256]{2,1,0:T(8,128)}, u32[]{:S(2)}, u32[]{:S(2)}) collective-permute-start(f32[2,512,256]{2,1,0:T(8,128)} %get-tuple-element.51), channel_id=1, source_target_pairs={{0,1},{2,3},{4,5},{6,7},{8,9},{10,11},{12,13},{14,15},{16,17},{18,... | collective-permute-start | bytes 3145736 | tf_op jit(solution)/shard_map/ppermute | solution.py:95
  50.4 45.1 %collective-permute-start.6 = (f32[2,512,256]{2,1,0:T(8,128)}, f32[2,512,256]{2,1,0:T(8,128)}, u32[]{:S(2)}, u32[]{:S(2)}) collective-permute-start(f32[2,512,256]{2,1,0:T(8,128)} %get-tuple-element.52), channel_id=1, source_target_pairs={{1,0},{2,1},{3,2},{4,3},{5,4},{6,5},{7,6},{8,7},{9,8},{10,9},{11,1... | collective-permute-start | bytes 3145736 | tf_op jit(solution)/shard_map/ppermute | solution.py:95
  58.2 61.9 %collective-permute-start.11 = (f32[2,512,256]{2,1,0:T(8,128)}, f32[2,512,256]{2,1,0:T(8,128)}, u32[]{:S(2)}, u32[]{:S(2)}) collective-permute-start(f32[2,512,256]{2,1,0:T(8,128)} %get-tuple-element.47), channel_id=1, source_target_pairs={{2,0},{4,2},{6,4},{8,6},{10,8},{12,10},{14,12},{18,16},{20,18},{22... | collective-permute-start | bytes 3145736 | tf_op jit(solution)/shard_map/ppermute | solution.py:95
  60.1 77.3 %collective-permute-start.8 = (f32[2,512,256]{2,1,0:T(8,128)}, f32[2,512,256]{2,1,0:T(8,128)}, u32[]{:S(2)}, u32[]{:S(2)}) collective-permute-start(f32[2,512,256]{2,1,0:T(8,128)} %get-tuple-element.48), channel_id=1, source_target_pairs={{0,1},{2,3},{4,5},{6,7},{8,9},{10,11},{12,13},{14,15},{16,17},{18,... | collective-permute-start | bytes 3145736 | tf_op jit(solution)/shard_map/ppermute | solution.py:95
  75.2 62.3 %collective-permute-start.9 = (f32[2,512,256]{2,1,0:T(8,128)}, f32[2,512,256]{2,1,0:T(8,128)}, u32[]{:S(2)}, u32[]{:S(2)}) collective-permute-start(f32[2,512,256]{2,1,0:T(8,128)} %get-tuple-element.49), channel_id=1, source_target_pairs={{1,0},{2,1},{3,2},{4,3},{5,4},{6,5},{7,6},{8,7},{9,8},{10,9},{11,1... | collective-permute-start | bytes 3145736 | tf_op jit(solution)/shard_map/ppermute | solution.py:95
  92.5 77.4 %collective-permute-start.12 = (f32[1,512,512]{1,2,0:T(8,128)}, f32[1,512,512]{1,2,0:T(8,128)}, u32[]{:S(2)}, u32[]{:S(2)}) collective-permute-start(f32[1,512,512]{1,2,0:T(8,128)} %copy.25), channel_id=1, source_target_pairs={{0,1},{1,0},{2,3},{3,2},{4,5},{5,4},{6,7},{7,6},{8,9},{9,8},{10,11... | collective-permute-start | bytes 3145736 | tf_op jit(solution)/shard_map/ppermute | solution.py:24
  226.4 37.2 %collective-permute-start.18 = (f32[384,512]{1,0:T(8,128)}, f32[384,512]{1,0:T(8,128)S(1)}, u32[]{:S(2)}, u32[]{:S(2)}) collective-permute-start(f32[384,512]{1,0:T(8,128)} %get-tuple-element.44), channel_id=1, source_target_pairs={{0,32},{32,64},{64,96},{96,0},{1,33},{33,65},{65,97},{97,1},{2,34}... | collective-permute-start | bytes 2359304 | tf_op jit(solution)/shard_map/ppermute | solution.py:35
  228.7 34.8 %collective-permute-start.19 = (f32[384,512]{1,0:T(8,128)}, f32[384,512]{1,0:T(8,128)}, u32[]{:S(2)}, u32[]{:S(2)}) collective-permute-start(f32[384,512]{1,0:T(8,128)} %get-tuple-element.46), channel_id=1, source_target_pairs={{0,64},{32,96},{64,0},{96,32},{1,65},{33,97},{65,1},{97,33},{2,66}... | collective-permute-start | bytes 2359304 | tf_op jit(solution)/shard_map/ppermute | solution.py:35
  230.4 37.3 %collective-permute-start.20 = (f32[384,512]{1,0:T(8,128)}, f32[384,512]{1,0:T(8,128)}, u32[]{:S(2)}, u32[]{:S(2)}) collective-permute-start(f32[384,512]{1,0:T(8,128)} %get-tuple-element.45), channel_id=1, source_target_pairs={{0,96},{32,0},{64,32},{96,64},{1,97},{33,1},{65,33},{97,65},{2,98}... | collective-permute-start | bytes 2359304 | tf_op jit(solution)/shard_map/ppermute | solution.py:35
  270.6 11.8 %collective-permute-start.21 = (f32[96,512]{1,0:T(8,128)}, f32[96,512]{1,0:T(8,128)S(1)}, u32[]{:S(2)}, u32[]{:S(2)}) collective-permute-start(f32[96,512]{1,0:T(8,128)} %get-tuple-element.57), channel_id=1, source_target_pairs={{0,4},{4,8},{8,12},{12,0},{1,5},{5,9},{9,13},{13,1},{2,6},{6,10},{... | collective-permute-start | bytes 589832 | tf_op jit(solution)/shard_map/ppermute | solution.py:35
  275.4 12.4 %collective-permute-start.22 = (f32[96,512]{1,0:T(8,128)S(1)}, f32[96,512]{1,0:T(8,128)}, u32[]{:S(2)}, u32[]{:S(2)}) collective-permute-start(f32[96,512]{1,0:T(8,128)S(1)} %get-tuple-element.59), channel_id=1, source_target_pairs={{0,8},{4,12},{8,0},{12,4},{1,9},{5,13},{9,1},{13,5},{2,10},{6,14},... | collective-permute-start | bytes 589832 | tf_op jit(solution)/shard_map/ppermute | solution.py:35
  278.4 9.4 %collective-permute-start.23 = (f32[96,512]{1,0:T(8,128)S(1)}, f32[96,512]{1,0:T(8,128)}, u32[]{:S(2)}, u32[]{:S(2)}) collective-permute-start(f32[96,512]{1,0:T(8,128)S(1)} %get-tuple-element.58), channel_id=1, source_target_pairs={{0,12},{4,0},{8,4},{12,8},{1,13},{5,1},{9,5},{13,9},{2,14},{6,2},{... | collective-permute-start | bytes 589832 | tf_op jit(solution)/shard_map/ppermute | solution.py:35
  302.2 51.0 %collective-permute-start.13 = (f32[2,512,512]{2,1,0:T(8,128)}, f32[2,512,512]{2,1,0:T(8,128)}, u32[]{:S(2)}, u32[]{:S(2)}) collective-permute-start(f32[2,512,512]{2,1,0:T(8,128)} %get-tuple-element.33), channel_id=1, source_target_pairs={{0,1},{1,2},{2,3},{3,4},{4,5},{5,6},{6,7},{7,8},{8,9},{9,10},{10,1... | collective-permute-start | bytes 6291464 | tf_op jit(solution)/shard_map/ppermute | solution.py:95
  305.6 89.7 %collective-permute-start.14 = (f32[2,512,512]{2,1,0:T(8,128)}, f32[2,512,512]{2,1,0:T(8,128)}, u32[]{:S(2)}, u32[]{:S(2)}) collective-permute-start(f32[2,512,512]{2,1,0:T(8,128)} %get-tuple-element.34), channel_id=1, source_target_pairs={{0,2},{2,4},{4,6},{6,8},{8,10},{10,12},{12,14},{16,18},{18,20},{20... | collective-permute-start | bytes 6291464 | tf_op jit(solution)/shard_map/ppermute | solution.py:95
  308.4 86.8 %collective-permute-start.15 = (f32[2,512,512]{2,1,0:T(8,128)}, f32[2,512,512]{2,1,0:T(8,128)}, u32[]{:S(2)}, u32[]{:S(2)}) collective-permute-start(f32[2,512,512]{2,1,0:T(8,128)} %get-tuple-element.32), channel_id=1, source_target_pairs={{1,0},{3,2},{5,4},{7,6},{9,8},{11,10},{13,12},{15,14},{17,16},{19,... | collective-permute-start | bytes 6291464 | tf_op jit(solution)/shard_map/ppermute | solution.py:95
  403.8 29.5 %collective-permute-start.16 = (f32[2,512,512]{2,1,0:T(8,128)S(1)}, f32[2,512,512]{2,1,0:T(8,128)S(1)}, u32[]{:S(2)}, u32[]{:S(2)}) collective-permute-start(f32[2,512,512]{2,1,0:T(8,128)S(1)} %slice.236), channel_id=1, source_target_pairs={{0,16},{16,32},{32,48},{48,64},{64,80},{80,96},{96,112},{1,17},{17... | collective-permute-start | bytes 6291464 | tf_op jit(solution)/shard_map/ppermute | solution.py:18
  (21 other events, 233.6 us)
Sparse Core Ops, SparseCore 0:
  297.8 150.9 all-gather.1

commit v7 on v5

--- a/solution.py
+++ b/solution.py
@@ -59,13 +59,19 @@
 def transform(real_part, imag_part, cos_table, sin_table, orient):
     length = real_part.shape[-1]
     stacked = jnp.concatenate([real_part, imag_part], axis=2)
-    cos_part = jnp.einsum("ij,mjk->mik", cos_table, stacked, preferred_element_type=jnp.float32)
-    sin_part = jnp.einsum("ij,mjk->mik", sin_table, stacked, preferred_element_type=jnp.float32)
+    both = jnp.einsum(
+        "ij,mjk->mik", jnp.concatenate([cos_table, sin_table], axis=0), stacked, preferred_element_type=jnp.float32
+    )
+    cos_part = both[:, :length, :]
+    sin_part = both[:, length:, :]
     middle_re = (cos_part[:, :, :length] + orient * sin_part[:, :, length:]).astype(jnp.bfloat16)
     middle_im = (cos_part[:, :, length:] - orient * sin_part[:, :, :length]).astype(jnp.bfloat16)
     stacked = jnp.concatenate([middle_re, middle_im], axis=1)
-    cos_part = jnp.einsum("mij,jk->mik", stacked, cos_table, preferred_element_type=jnp.float32)
-    sin_part = jnp.einsum("mij,jk->mik", stacked, sin_table, preferred_element_type=jnp.float32)
+    both = jnp.einsum(
+        "mij,jk->mik", stacked, jnp.concatenate([cos_table, sin_table], axis=1), preferred_element_type=jnp.float32
+    )
+    cos_part = both[:, :, :length]
+    sin_part = both[:, :, length:]
     result_re = cos_part[:, :length] + orient * sin_part[:, length:]
     result_im = cos_part[:, length:] - orient * sin_part[:, :length]
     return (result_re, result_im)
@@ -133,6 +139,7 @@
 
     below = passed_along(specimen[:, :width, :], TY, -1)
     column = jnp.concatenate([specimen, below], axis=1)
+    column, got_measured = lax.optimization_barrier((column, got_measured))
 
     def strip(source, at):
         return lax.dynamic_slice(source, (anchor, at, anchor), (2, width, width))

time: 469 us -> 449 us (0.957)
  matrix products: 46.6 us -> 13.9 us
  other arithmetic: 49 us -> 59.8 us
  waiting for transfers between devices: 252 us -> 262 us
  local copies, waits for them, and re-layouts: 37.3 us -> 27.6 us
    dot_general x8 -> x4, matrix products: 46.6 us -> 13.9 us  [the longest x2 7.07 us: transform(): jnp.einsum('mij,jk->mik', stacked, jnp.concatenate([cos_table, sin_table]...]
    ppermute x10, waiting for transfers between devices: 161 us -> 173 us  [shifted(): lax.ppermute(value, axis, [(a, b) for a, b in pairs if 0 <= b < lax.axis_...]
    convert_element_type x0 -> x1, other arithmetic: none -> 5.92 us  [tables(): (jnp.sin(angle) * scale).astype(jnp.bfloat16)]
    unnamed x34 -> x51, local copies, waits for them, and re-layouts: 16.2 us -> 11.6 us
  transfers between devices with their start and end apart: 24 -> 24, of which waited for: 16 -> 18; matrix products, arithmetic and copies ran while one was open for 14% -> 8% of each run, Pallas kernels for 0% -> 0%
where the time goes in v7:
time: 449 us; the launch traced here: 440 us
  waiting for transfers between devices  262 us (58%)
  other arithmetic  59.8 us (13%)
  starting transfers between devices  53.2 us (12%)
  local copies, waits for them, and re-layouts  27.6 us (6%)
  between operations  24.2 us (5%)
  matrix products  13.9 us (3%)
    ppermute x10, waiting for transfers between devices, shifted(): lax.ppermute(value, axis, [(a, b) for a, b in pairs if 0 <= b < lax.axis_...  173 us
    ppermute x10, waiting for transfers between devices, scatter_axis(): total = total + lax.ppermute(sent, axis, pairs)  52.2 us
    ppermute x10, starting transfers between devices, shifted(): lax.ppermute(value, axis, [(a, b) for a, b in pairs if 0 <= b < lax.axis_...  33.3 us
    ppermute x2, waiting for transfers between devices, passed_along(): lax.ppermute(value, axis, [(source, source + steps) for source in range(i...  27.7 us
    ppermute x10, starting transfers between devices, scatter_axis(): total = total + lax.ppermute(sent, axis, pairs)  14.4 us
    unnamed x51, local copies, waits for them, and re-layouts  11.6 us
    all_gather x1, waiting for transfers between devices, all_sum(): lines = lax.all_gather(lines, tuple(axes), tiled=True)  8.99 us
  transfers between devices with their start and end apart: 24, of which 18 were waited for; matrix products, arithmetic and copies ran while one was open for 8% of the time, Pallas kernels for 0%

profile of v7, /device:TPU:48, one launch (start us, length us, event | category | flops | bytes accessed | tf_op | source)
XLA Modules:
  0.0 440.3 jit_solution(17782283689165049457)
XLA Ops:
  19.2 3.9 collective-permute-start.4
  25.8 12.8 %collective-permute-done.6 = s32[5]{0:T(128)S(1)} collective-permute-done((s32[5]{0:T(128)S(1)}, s32[5]{0:T(128)S(1)}, u32[]{:S(2)}, u32[]{:S(2)}) %collective-permute-start.6) | collective-permute-done | bytes 52 | tf_op jit(solution)/shard_map/ppermute | solution.py:101
  49.2 3.5 pad_maximum_fusion
  57.7 6.1 %collective-permute-start.5 = (f32[2,512,512]{2,1,0:T(8,128)}, f32[2,512,512]{2,1,0:T(8,128)}, u32[]{:S(2)}, u32[]{:S(2)}) collective-permute-start(f32[2,512,512]{2,1,0:T(8,128)} %get-tuple-element.34), channel_id=1, source_target_pairs={{0,1},{2,3},{4,5},{6,7},{8,9},{10,11},{12,13},{14,15},{16,17},{18,... | collective-permute-start | bytes 6291464 | tf_op jit(solution)/shard_map/ppermute | solution.py:101
  70.0 5.9 %multiply_convert_fusion.2 = (bf16[512,512]{1,0:T(8,128)(2,1)}, bf16[512,512]{1,0:T(8,128)(2,1)}) fusion(), kind=kLoop, calls=%fused_computation.105 | loop fusion | flops 4718592 | bytes 1048576 | tf_op jit(solution)/shard_map/convert_element_type | solution.py:55
  79.5 29.4 %collective-permute-done.5 = f32[2,512,512]{2,1,0:T(8,128)} collective-permute-done((f32[2,512,512]{2,1,0:T(8,128)}, f32[2,512,512]{2,1,0:T(8,128)}, u32[]{:S(2)}, u32[]{:S(2)}) %collective-permute-start.5) | collective-permute-done | bytes 2097184 | tf_op jit(solution)/shard_map/ppermute | solution.py:101
  111.5 44.8 %collective-permute-done.8 = f32[2,512,512]{2,1,0:T(8,128)} collective-permute-done((f32[2,512,512]{2,1,0:T(8,128)}, f32[2,512,512]{2,1,0:T(8,128)}, u32[]{:S(2)}, u32[]{:S(2)}) %collective-permute-start.8) | collective-permute-done | bytes 2097184 | tf_op jit(solution)/shard_map/ppermute | solution.py:101
  156.3 3.9 select_select_fusion.2
  168.3 3.6 fusion.27
  184.9 3.7 multiply_subtract_fusion
  188.6 6.8 %fusion.45 = (f32[512,512]{1,0:T(8,128)}, f32[512,512]{1,0:T(8,128)}, f32[3,512,512]{2,1,0:T(8,128)S(1)}) fusion(f32[3,512,512]{2,1,0:T(8,128)} %get-tuple-element.20, f32[3,512,512]{2,1,0:T(8,128)} %get-tuple-element.19, f32[2,3,512,512]{3,2,1,0:T(8,128)S(1)} %bitcast.133, f32[512,512]{1,0:T(8,128)S(1)} %copy-done.4, f32[512,512]{1,0:T(8,128)} %copy-done.2), kind=kLoop, calls=%fused_computation.73 | loop fusion | flops 8126464 | bytes 19922944 | tf_op jit(solution)/shard_map/reduce_sum | solution.py:94
  197.8 6.0 %collective-permute-done.13 = f32[1536,512]{1,0:T(8,128)} collective-permute-done((f32[1536,512]{1,0:T(8,128)}, f32[1536,512]{1,0:T(8,128)}, u32[]{:S(2)}, u32[]{:S(2)}) %collective-permute-start.13) | collective-permute-done | bytes 3145760 | tf_op jit(solution)/shard_map/ppermute | solution.py:35
  216.6 13.9 %collective-permute-done.14 = f32[384,512]{1,0:T(8,128)S(1)} collective-permute-done((f32[384,512]{1,0:T(8,128)}, f32[384,512]{1,0:T(8,128)S(1)}, u32[]{:S(2)}, u32[]{:S(2)}) %collective-permute-start.14) | collective-permute-done | bytes 786464 | tf_op jit(solution)/shard_map/ppermute | solution.py:35
  230.5 3.7 collective-permute-done.15
  234.2 16.6 %collective-permute-done.16 = f32[384,512]{1,0:T(8,128)} collective-permute-done((f32[384,512]{1,0:T(8,128)}, f32[384,512]{1,0:T(8,128)}, u32[]{:S(2)}, u32[]{:S(2)}) %collective-permute-start.16) | collective-permute-done | bytes 786464 | tf_op jit(solution)/shard_map/ppermute | solution.py:35
  262.6 3.9 collective-permute-done.18
  279.9 4.3 collective-permute-start.10
  285.5 5.8 %collective-permute-start.9 = (f32[2,512,512]{2,1,0:T(8,128)}, f32[2,512,512]{2,1,0:T(8,128)}, u32[]{:S(2)}, u32[]{:S(2)}) collective-permute-start(f32[2,512,512]{2,1,0:T(8,128)} %get-tuple-element.36), channel_id=1, source_target_pairs={{0,1},{1,2},{2,3},{3,4},{4,5},{5,6},{6,7},{7,8},{8,9},{9,10},{10,1... | collective-permute-start | bytes 6291464 | tf_op jit(solution)/shard_map/ppermute | solution.py:101
  291.4 67.0 %collective-permute-done.10 = f32[2,512,512]{2,1,0:T(8,128)} collective-permute-done((f32[2,512,512]{2,1,0:T(8,128)}, f32[2,512,512]{2,1,0:T(8,128)}, u32[]{:S(2)}, u32[]{:S(2)}) %collective-permute-start.10) | collective-permute-done | bytes 2097184 | tf_op jit(solution)/shard_map/ppermute | solution.py:101
  358.4 16.2 %collective-permute-done.9 = f32[2,512,512]{2,1,0:T(8,128)} collective-permute-done((f32[2,512,512]{2,1,0:T(8,128)}, f32[2,512,512]{2,1,0:T(8,128)}, u32[]{:S(2)}, u32[]{:S(2)}) %collective-permute-start.9) | collective-permute-done | bytes 2097184 | tf_op jit(solution)/shard_map/ppermute | solution.py:101
  374.5 8.7 %fusion.2 = f32[2,1536,512]{2,1,0:T(8,128)S(1)} fusion(s32[]{:T(128)S(6)} %select_n.277, f32[2,512,512]{2,1,0:T(8,128)S(1)} %get-tuple-element.38, s32[]{:T(128)S(6)} %select_n.281, f32[2,512,512]{2,1,0:T(8,128)} %collective-permute-done.9, s32[]{:T(128)S(6)} %select_n.283, f32[2,512,512]{2,1,0:T(8,128)} %collective-permute-done.10, s32[]{:T(128)S(6)} %select_n.285, ...), kind=kLoop, calls=%fused_computation.10 | loop fusion | flops 4718592 | bytes 14680080 | tf_op jit(solution)/shard_map/add | solution.py:180
  387.9 27.7 %collective-permute-done.12 = f32[2,512,512]{2,1,0:T(8,128)S(1)} collective-permute-done((f32[2,512,512]{2,1,0:T(8,128)S(1)}, f32[2,512,512]{2,1,0:T(8,128)S(1)}, u32[]{:S(2)}, u32[]{:S(2)}) %collective-permute-start.12) | collective-permute-done | bytes 2097184 | tf_op jit(solution)/shard_map/ppermute | solution.py:18
  417.4 9.0 %all-gather.2.cloned.1.call-done = f32[3072,512]{1,0:T(8,128)} async-done(((f32[24,512]{1,0:T(8,128)}), f32[3072,512]{1,0:T(8,128)}) %all-gather.2.cloned.1.call-update) | async-done | bytes 6291472 | tf_op jit(solution)/shard_map/all_gather | solution.py:44
  426.3 6.9 %copy.21 = f32[2,3,512,512]{3,2,1,0:T(8,128)} copy(f32[2,3,512,512]{3,2,1,0:T(8,128)} %bitcast.136) | data formatting | bytes 12582912
  (125 shorter events, 102.0 us)
Async XLA Ops:
  7.2 419.2 %all-gather.2.cloned.1.call-start = ((), (), s32[]{:S(2)}) async-start(), calls=%async_computation | async-start | bytes 6340608 | tf_op jit(solution)/shard_map/all_gather | solution.py:44
  10.5 38.8 %collective-permute-start = (f32[2,512,512]{2,1,0:T(8,128)}, f32[2,512,512]{2,1,0:T(8,128)}, u32[]{:S(2)}, u32[]{:S(2)}) collective-permute-start(f32[2,512,512]{2,1,0:T(8,128)} %slice.182), channel_id=1, source_target_pairs={{16,0},{32,16},{48,32},{64,48},{80,64},{96,80},{112,96},{17,1},{33... | collective-permute-start | bytes 6291464 | tf_op jit(solution)/shard_map/ppermute | solution.py:18
  13.0 39.8 %collective-permute-start.1 = (f32[1,512,512]{1,2,0:T(8,128)S(1)}, f32[1,512,512]{1,2,0:T(8,128)S(1)}, u32[]{:S(2)}, u32[]{:S(2)}) collective-permute-start(f32[1,512,512]{1,2,0:T(8,128)S(1)} %copy.17), channel_id=1, source_target_pairs={{0,1},{1,0},{2,3},{3,2},{4,5},{5,4},{6,7},{7,6},{8,9},{9,8},{10,11... | collective-permute-start | bytes 3145736 | tf_op jit(solution)/shard_map/ppermute | solution.py:24
  15.8 22.8 %collective-permute-start.6 = (s32[5]{0:T(128)S(1)}, s32[5]{0:T(128)S(1)}, u32[]{:S(2)}, u32[]{:S(2)}) collective-permute-start(s32[5]{0:T(128)S(1)} %pad_add_fusion), channel_id=1, source_target_pairs={{0,2},{1,3},{2,4},{3,5},{4,6},{5,7},{6,8},{7,9},{8,10},{9,11},{10,... | collective-permute-start | bytes 68 | tf_op jit(solution)/shard_map/ppermute | solution.py:101
  19.2 21.3 %collective-permute-start.4 = (s32[5]{0:T(128)S(1)}, s32[5]{0:T(128)S(1)}, u32[]{:S(2)}, u32[]{:S(2)}) collective-permute-start(s32[5]{0:T(128)S(1)} %pad_add_fusion), channel_id=1, source_target_pairs={{2,0},{3,1},{4,2},{5,3},{6,4},{7,5},{8,6},{9,7},{10,8},{11,9},{12,... | collective-permute-start | bytes 68 | tf_op jit(solution)/shard_map/ppermute | solution.py:101
  23.1 18.0 %collective-permute-start.2 = (s32[5]{0:T(128)S(1)}, s32[5]{0:T(128)S(1)}, u32[]{:S(2)}, u32[]{:S(2)}) collective-permute-start(s32[5]{0:T(128)S(1)} %pad_add_fusion), channel_id=1, source_target_pairs={{0,1},{1,2},{2,3},{3,4},{4,5},{5,6},{6,7},{7,8},{8,9},{9,10},{10,1... | collective-permute-start | bytes 68 | tf_op jit(solution)/shard_map/ppermute | solution.py:101
  38.6 5.7 %collective-permute-start.3 = (s32[5]{0:T(128)S(1)}, s32[5]{0:T(128)S(1)}, u32[]{:S(2)}, u32[]{:S(2)}) collective-permute-start(s32[5]{0:T(128)S(1)} %pad_add_fusion), channel_id=1, source_target_pairs={{1,0},{2,1},{3,2},{4,3},{5,4},{6,5},{7,6},{8,7},{9,8},{10,9},{11,1... | collective-permute-start | bytes 68 | tf_op jit(solution)/shard_map/ppermute | solution.py:101
  57.7 51.1 %collective-permute-start.5 = (f32[2,512,512]{2,1,0:T(8,128)}, f32[2,512,512]{2,1,0:T(8,128)}, u32[]{:S(2)}, u32[]{:S(2)}) collective-permute-start(f32[2,512,512]{2,1,0:T(8,128)} %get-tuple-element.34), channel_id=1, source_target_pairs={{0,1},{2,3},{4,5},{6,7},{8,9},{10,11},{12,13},{14,15},{16,17},{18,... | collective-permute-start | bytes 6291464 | tf_op jit(solution)/shard_map/ppermute | solution.py:101
  63.9 47.6 %collective-permute-start.7 = (f32[2,512,512]{2,1,0:T(8,128)}, f32[2,512,512]{2,1,0:T(8,128)}, u32[]{:S(2)}, u32[]{:S(2)}) collective-permute-start(f32[2,512,512]{2,1,0:T(8,128)} %get-tuple-element.33), channel_id=1, source_target_pairs={{1,0},{2,1},{3,2},{4,3},{5,4},{6,5},{7,6},{8,7},{9,8},{10,9},{11,1... | collective-permute-start | bytes 6291464 | tf_op jit(solution)/shard_map/ppermute | solution.py:101
  65.8 90.6 %collective-permute-start.8 = (f32[2,512,512]{2,1,0:T(8,128)}, f32[2,512,512]{2,1,0:T(8,128)}, u32[]{:S(2)}, u32[]{:S(2)}) collective-permute-start(f32[2,512,512]{2,1,0:T(8,128)} %get-tuple-element.32), channel_id=1, source_target_pairs={{2,0},{4,2},{6,4},{8,6},{10,8},{12,10},{14,12},{18,16},{20,18},{22... | collective-permute-start | bytes 6291464 | tf_op jit(solution)/shard_map/ppermute | solution.py:101
  197.8 6.0 %collective-permute-start.13 = (f32[1536,512]{1,0:T(8,128)}, f32[1536,512]{1,0:T(8,128)}, u32[]{:S(2)}, u32[]{:S(2)}) collective-permute-start(f32[1536,512]{1,0:T(8,128)} %fusion.10), channel_id=1, source_target_pairs={{0,16},{16,0},{1,17},{17,1},{2,18},{18,2},{3,19},{19,3},{4,20},{20... | collective-permute-start | bytes 9437192 | tf_op jit(solution)/shard_map/ppermute | solution.py:35
  210.0 20.5 %collective-permute-start.14 = (f32[384,512]{1,0:T(8,128)}, f32[384,512]{1,0:T(8,128)S(1)}, u32[]{:S(2)}, u32[]{:S(2)}) collective-permute-start(f32[384,512]{1,0:T(8,128)} %get-tuple-element.39), channel_id=1, source_target_pairs={{0,32},{32,64},{64,96},{96,0},{1,33},{33,65},{65,97},{97,1},{2,34}... | collective-permute-start | bytes 2359304 | tf_op jit(solution)/shard_map/ppermute | solution.py:35
  211.9 22.3 %collective-permute-start.15 = (f32[384,512]{1,0:T(8,128)}, f32[384,512]{1,0:T(8,128)}, u32[]{:S(2)}, u32[]{:S(2)}) collective-permute-start(f32[384,512]{1,0:T(8,128)} %get-tuple-element.41), channel_id=1, source_target_pairs={{0,64},{32,96},{64,0},{96,32},{1,65},{33,97},{65,1},{97,33},{2,66}... | collective-permute-start | bytes 2359304 | tf_op jit(solution)/shard_map/ppermute | solution.py:35
  214.0 36.9 %collective-permute-start.16 = (f32[384,512]{1,0:T(8,128)}, f32[384,512]{1,0:T(8,128)}, u32[]{:S(2)}, u32[]{:S(2)}) collective-permute-start(f32[384,512]{1,0:T(8,128)} %get-tuple-element.40), channel_id=1, source_target_pairs={{0,96},{32,0},{64,32},{96,64},{1,97},{33,1},{65,33},{97,65},{2,98}... | collective-permute-start | bytes 2359304 | tf_op jit(solution)/shard_map/ppermute | solution.py:35
  253.8 8.8 %collective-permute-start.17 = (f32[96,512]{1,0:T(8,128)}, f32[96,512]{1,0:T(8,128)S(1)}, u32[]{:S(2)}, u32[]{:S(2)}) collective-permute-start(f32[96,512]{1,0:T(8,128)} %get-tuple-element.46), channel_id=1, source_target_pairs={{0,4},{4,8},{8,12},{12,0},{1,5},{5,9},{9,13},{13,1},{2,6},{6,10},{... | collective-permute-start | bytes 589832 | tf_op jit(solution)/shard_map/ppermute | solution.py:35
  255.3 11.2 %collective-permute-start.18 = (f32[96,512]{1,0:T(8,128)S(1)}, f32[96,512]{1,0:T(8,128)}, u32[]{:S(2)}, u32[]{:S(2)}) collective-permute-start(f32[96,512]{1,0:T(8,128)S(1)} %get-tuple-element.48), channel_id=1, source_target_pairs={{0,8},{4,12},{8,0},{12,4},{1,9},{5,13},{9,1},{13,5},{2,10},{6,14},... | collective-permute-start | bytes 589832 | tf_op jit(solution)/shard_map/ppermute | solution.py:35
  256.8 10.0 %collective-permute-start.19 = (f32[96,512]{1,0:T(8,128)S(1)}, f32[96,512]{1,0:T(8,128)}, u32[]{:S(2)}, u32[]{:S(2)}) collective-permute-start(f32[96,512]{1,0:T(8,128)S(1)} %get-tuple-element.47), channel_id=1, source_target_pairs={{0,12},{4,0},{8,4},{12,8},{1,13},{5,1},{9,5},{13,9},{2,14},{6,2},{... | collective-permute-start | bytes 589832 | tf_op jit(solution)/shard_map/ppermute | solution.py:35
  267.9 4.5 %collective-permute-start.20 = (f32[24,512]{1,0:T(8,128)S(1)}, f32[24,512]{1,0:T(8,128)S(1)}, u32[]{:S(2)}, u32[]{:S(2)}) collective-permute-start(f32[24,512]{1,0:T(8,128)S(1)} %get-tuple-element.49), channel_id=1, source_target_pairs={{0,1},{1,2},{2,3},{3,0},{4,5},{5,6},{6,7},{7,4},{8,9},{9,10},{10,1... | collective-permute-start | bytes 147464 | tf_op jit(solution)/shard_map/ppermute | solution.py:35
  268.0 5.7 %collective-permute-start.21 = (f32[24,512]{1,0:T(8,128)S(1)}, f32[24,512]{1,0:T(8,128)S(1)}, u32[]{:S(2)}, u32[]{:S(2)}) collective-permute-start(f32[24,512]{1,0:T(8,128)S(1)} %get-tuple-element.51), channel_id=1, source_target_pairs={{0,2},{1,3},{2,0},{3,1},{4,6},{5,7},{6,4},{7,5},{8,10},{9,11},{10,... | collective-permute-start | bytes 147464 | tf_op jit(solution)/shard_map/ppermute | solution.py:35
  268.1 6.6 %collective-permute-start.22 = (f32[24,512]{1,0:T(8,128)S(1)}, f32[24,512]{1,0:T(8,128)S(1)}, u32[]{:S(2)}, u32[]{:S(2)}) collective-permute-start(f32[24,512]{1,0:T(8,128)S(1)} %get-tuple-element.50), channel_id=1, source_target_pairs={{0,3},{1,0},{2,1},{3,2},{4,7},{5,4},{6,5},{7,6},{8,11},{9,8},{10,9... | collective-permute-start | bytes 147464 | tf_op jit(solution)/shard_map/ppermute | solution.py:35
  279.9 78.5 %collective-permute-start.10 = (f32[2,512,512]{2,1,0:T(8,128)}, f32[2,512,512]{2,1,0:T(8,128)}, u32[]{:S(2)}, u32[]{:S(2)}) collective-permute-start(f32[2,512,512]{2,1,0:T(8,128)} %get-tuple-element.37), channel_id=1, source_target_pairs={{0,2},{2,4},{4,6},{6,8},{8,10},{10,12},{12,14},{16,18},{18,20},{20... | collective-permute-start | bytes 6291464 | tf_op jit(solution)/shard_map/ppermute | solution.py:101
  284.2 74.1 %collective-permute-start.11 = (f32[2,512,512]{2,1,0:T(8,128)}, f32[2,512,512]{2,1,0:T(8,128)}, u32[]{:S(2)}, u32[]{:S(2)}) collective-permute-start(f32[2,512,512]{2,1,0:T(8,128)} %get-tuple-element.35), channel_id=1, source_target_pairs={{1,0},{3,2},{5,4},{7,6},{9,8},{11,10},{13,12},{15,14},{17,16},{19,... | collective-permute-start | bytes 6291464 | tf_op jit(solution)/shard_map/ppermute | solution.py:101
  285.5 89.0 %collective-permute-start.9 = (f32[2,512,512]{2,1,0:T(8,128)}, f32[2,512,512]{2,1,0:T(8,128)}, u32[]{:S(2)}, u32[]{:S(2)}) collective-permute-start(f32[2,512,512]{2,1,0:T(8,128)} %get-tuple-element.36), channel_id=1, source_target_pairs={{0,1},{1,2},{2,3},{3,4},{4,5},{5,6},{6,7},{7,8},{8,9},{9,10},{10,1... | collective-permute-start | bytes 6291464 | tf_op jit(solution)/shard_map/ppermute | solution.py:101
  383.4 32.2 %collective-permute-start.12 = (f32[2,512,512]{2,1,0:T(8,128)S(1)}, f32[2,512,512]{2,1,0:T(8,128)S(1)}, u32[]{:S(2)}, u32[]{:S(2)}) collective-permute-start(f32[2,512,512]{2,1,0:T(8,128)S(1)} %slice.248), channel_id=1, source_target_pairs={{0,16},{16,32},{32,48},{48,64},{64,80},{80,96},{96,112},{1,17},{17... | collective-permute-start | bytes 6291464 | tf_op jit(solution)/shard_map/ppermute | solution.py:18
  (24 other events, 377.4 us)
Sparse Core Ops, SparseCore 0:
  275.5 150.8 all-gather.1
